TPU v7x, 256 devices: a whole 4x4x8 slice. The times are simulated.
256 devices in a mesh: dp: 128 (over x, y, z_hi, core), rep: 2 (over z_lo).
Axes of the slice: x: 4, y: 4, z: 8 (z_hi: 4, z_lo: 2; z = z_hi * 2 + z_lo), core: 2. Of those that a mesh axis runs over, the one named last changes fastest.
Arguments:
- queries: bfloat16 [262144, 1024], P(('dp', 'rep')), may hold values from -12 to 12
- keys: bfloat16 [16384, 1024], P('dp'), may hold values from -5 to 5
- neg_mask: int32 [2048, 128], P(('dp', 'rep')), may hold values from 0 to 1, as said below
- positive: int32 [2048], P(('dp', 'rep')), may hold values from 0 to 127, as said below
- row_weight: float32 [262144], P(('dp', 'rep')), may hold values from 2 to 20
Outputs:
- row_loss: float32 [262144], P(('dp', 'rep'))
- grad_queries: float32 [262144, 1024], P(('dp', 'rep'))
- grad_keys: float32 [16384, 1024], P(('dp', 'rep'))
Inputs may be any that keep to these rules, and one draw needn't show every extreme that they name: neg_mask[b, c] is 0 unless key block c lies at cyclic distance at most 4 from the dp index that holds query block b (query blocks numbered along dp+rep, 8 to a device); for every b the two key blocks at distance exactly 4 are 1. positive[b] lies at cyclic distance at most 4 from the dp index that holds query block b.
All inputs are finite; a program needn't handle non-finite values.
Results may differ from a plain program's by a relative error of at most 0.003.
Values may be sent and summed in bfloat16 or wider, within the bound.
No kernel may reach another device: no remote copies, remote signals or barrier semaphores. Data moves between devices by JAX's collectives and lax.ppermute only.
A program may use at most 128 MiB of HBM per device.

v0:
```python
import math

import jax
import jax.numpy as jnp
from jax import lax
from jax.sharding import PartitionSpec as P

D = 1024
REACH = 4


def passed_along(x, axis, by):
    count = lax.axis_size(axis)
    return lax.ppermute(x, axis, [(i, (i + by) % count) for i in range(count)])


def body(queries, keys, neg_mask, positive, row_weight):
    logit_scale = 2.0 / math.sqrt(D)
    cycle_size = lax.axis_size("dp")
    cycle_index = lax.axis_index("dp")
    query_rows = queries.shape[0]
    tile_rows = keys.shape[0]
    query_blocks = query_rows // tile_rows
    inner_idx = jnp.arange(tile_rows, dtype=jnp.int32)
    same_row = inner_idx[:, None] == inner_idx[None, :]
    key_tiles = [(0, keys)]
    upward = keys
    downward = keys
    for hop_count in range(1, REACH + 1):
        upward = passed_along(upward, "dp", 1)
        downward = passed_along(downward, "dp", -1)
        key_tiles.append((hop_count, upward))
        key_tiles.append((-hop_count, downward))
    run_max = jnp.full((query_rows,), -1e30, jnp.float32)
    run_sum = jnp.zeros((query_rows,), jnp.float32)
    pos_logit = jnp.zeros((query_rows,), jnp.float32)
    stored = []
    for distance, key_tile in key_tiles:
        owner_idx = (cycle_index - distance) % cycle_size
        column = lax.dynamic_slice_in_dim(neg_mask, owner_idx, 1, 1)[:, 0]
        hit_block = positive == owner_idx
        allow_block = (column == 1) | hit_block
        allowed = jnp.broadcast_to(
            allow_block[:, None, None], (query_blocks, tile_rows, tile_rows)
        ).reshape(query_rows, tile_rows)
        at_positive = (hit_block[:, None, None] & same_row[None, :, :]).reshape(
            query_rows, tile_rows
        )
        allowed, at_positive = (allowed, at_positive)
        logit_tile = logit_scale * lax.dot_general(
            queries, key_tile, (((1,), (1,)), ((), ())), preferred_element_type=jnp.float32
        )
        masked = jnp.where(allowed, logit_tile, jnp.float32(-1e30))
        next_max = jnp.maximum(run_max, jnp.max(masked, axis=1))
        run_sum = run_sum * jnp.exp(run_max - next_max) + jnp.sum(
            jnp.where(allowed, jnp.exp(masked - next_max[:, None]), 0.0), axis=1
        )
        run_max = next_max
        pos_logit = pos_logit + jnp.sum(jnp.where(at_positive, logit_tile, 0.0), axis=1)
        stored.append((distance, key_tile, masked, at_positive))
    log_total = run_max + jnp.log(run_sum)
    row_loss = log_total - pos_logit
    grad_query = jnp.zeros(queries.shape, jnp.float32)
    key_parts = {}
    for distance, key_tile, masked, at_positive in stored:
        softmax_p = jnp.exp(masked - log_total[:, None])
        coefficient = (row_weight[:, None] * (softmax_p - at_positive.astype(jnp.float32))).astype(
            jnp.bfloat16
        )
        grad_query = grad_query + logit_scale * jnp.dot(
            coefficient, key_tile, preferred_element_type=jnp.float32
        )
        key_parts[distance] = logit_scale * lax.dot_general(
            coefficient, queries, (((0,), (0,)), ((), ())), preferred_element_type=jnp.float32
        )
    upward = jnp.zeros_like(key_parts[0])
    for distance in range(REACH, 0, -1):
        upward = passed_along(upward + key_parts[distance], "dp", -1)
    downward = jnp.zeros_like(key_parts[0])
    for distance in range(-REACH, 0):
        downward = passed_along(downward + key_parts[distance], "dp", 1)
    grad_keys = lax.psum_scatter(
        key_parts[0] + upward + downward, "rep", scatter_dimension=0, tiled=True
    )
    return (row_loss, grad_query, grad_keys)


def solution(mesh):
    placed = (
        P(("dp", "rep"), None),
        P("dp", None),
        P(("dp", "rep"), None),
        P(("dp", "rep")),
        P(("dp", "rep")),
    )
    return jax.shard_map(
        body,
        mesh=mesh,
        in_specs=placed,
        out_specs=(P(("dp", "rep")), P(("dp", "rep"), None), P(("dp", "rep"), None)),
        check_vma=False,
    )
```

profile of v0, /device:TPU:1, one launch (start us, length us, event | category | flops | bytes accessed | tf_op | source)
XLA Modules:
  0.0 184.3 jit_solution(12621977750519283713)
XLA Ops:
  7.2 4.4 %collective-permute-start = (bf16[128,1024]{1,0:T(8,128)(2,1)}, bf16[128,1024]{1,0:T(8,128)(2,1)S(1)}, u32[]{:S(2)}, u32[]{:S(2)}) collective-permute-start(bf16[128,1024]{1,0:T(8,128)(2,1)} %param.6), channel_id=1, source_target_pairs={{0,2},{2,4},{4,6},{6,8},{8,10},{10,12},{12,14},{14,16},{16,18},{18... | collective-permute-start | bytes 786440 | tf_op jit(solution)/shard_map/ppermute | solution.py:14
  11.7 0.6 iota_compare_fusion
  12.3 1.3 fusion.10
  13.6 0.7 fusion.48
  14.4 0.1 broadcast_bitcast_fusion.16
  14.4 0.1 broadcast_bitcast_fusion.8
  14.5 0.1 broadcast_bitcast_fusion.10
  14.6 0.1 broadcast_bitcast_fusion.2
  14.7 0.1 broadcast_bitcast_fusion.12
  14.7 0.1 broadcast_bitcast_fusion.4
  14.8 0.1 broadcast_bitcast_fusion.14
  14.9 0.1 broadcast_bitcast_fusion.6
  15.0 0.1 broadcast_bitcast_fusion
  15.0 1.8 select_reduce_fusion.26
  16.9 2.7 %collective-permute-start.2 = (bf16[128,1024]{1,0:T(8,128)(2,1)S(1)}, bf16[128,1024]{1,0:T(8,128)(2,1)S(1)}, u32[]{:S(2)}, u32[]{:S(2)}) collective-permute-start(bf16[128,1024]{1,0:T(8,128)(2,1)S(1)} %collective-permute-done), channel_id=1, source_target_pairs={{0,2},{2,4},{4,6},{6,8},{8,10},{10,12},{12,14},{14,16},{16,18},{18... | collective-permute-start | bytes 786440 | tf_op jit(solution)/shard_map/ppermute | solution.py:14
  19.6 2.1 %collective-permute-done.1 = bf16[128,1024]{1,0:T(8,128)(2,1)S(1)} collective-permute-done((bf16[128,1024]{1,0:T(8,128)(2,1)}, bf16[128,1024]{1,0:T(8,128)(2,1)S(1)}, u32[]{:S(2)}, u32[]{:S(2)}) %collective-permute-start.1) | collective-permute-done | bytes 262176 | tf_op jit(solution)/shard_map/ppermute | solution.py:14
  21.7 4.6 %collective-permute-start.3 = (bf16[128,1024]{1,0:T(8,128)(2,1)S(1)}, bf16[128,1024]{1,0:T(8,128)(2,1)S(1)}, u32[]{:S(2)}, u32[]{:S(2)}) collective-permute-start(bf16[128,1024]{1,0:T(8,128)(2,1)S(1)} %collective-permute-done.1), channel_id=1, source_target_pairs={{0,254},{2,0},{4,2},{6,4},{8,6},{10,8},{12,10},{14,12},{16,14},{18... | collective-permute-start | bytes 786440 | tf_op jit(solution)/shard_map/ppermute | solution.py:14
  26.3 0.8 select_reduce_fusion.24
  27.1 0.8 select_reduce_fusion.25
  28.0 0.1 collective-permute-start.4
  28.1 3.1 %collective-permute-done.3 = bf16[128,1024]{1,0:T(8,128)(2,1)S(1)} collective-permute-done((bf16[128,1024]{1,0:T(8,128)(2,1)S(1)}, bf16[128,1024]{1,0:T(8,128)(2,1)S(1)}, u32[]{:S(2)}, u32[]{:S(2)}) %collective-permute-start.3) | collective-permute-done | bytes 262176 | tf_op jit(solution)/shard_map/ppermute | solution.py:14
  31.2 10.1 %collective-permute-start.5 = (bf16[128,1024]{1,0:T(8,128)(2,1)S(1)}, bf16[128,1024]{1,0:T(8,128)(2,1)S(1)}, u32[]{:S(2)}, u32[]{:S(2)}) collective-permute-start(bf16[128,1024]{1,0:T(8,128)(2,1)S(1)} %collective-permute-done.3), channel_id=1, source_target_pairs={{0,254},{2,0},{4,2},{6,4},{8,6},{10,8},{12,10},{14,12},{16,14},{18... | collective-permute-start | bytes 786440 | tf_op jit(solution)/shard_map/ppermute | solution.py:14
  41.2 0.8 select_reduce_fusion.22
  42.1 0.8 select_reduce_fusion.23
  42.9 0.1 collective-permute-start.6
  43.1 13.1 %collective-permute-start.7 = (bf16[128,1024]{1,0:T(8,128)(2,1)S(1)}, bf16[128,1024]{1,0:T(8,128)(2,1)S(1)}, u32[]{:S(2)}, u32[]{:S(2)}) collective-permute-start(bf16[128,1024]{1,0:T(8,128)(2,1)S(1)} %collective-permute-done.5), channel_id=1, source_target_pairs={{0,254},{2,0},{4,2},{6,4},{8,6},{10,8},{12,10},{14,12},{16,14},{18... | collective-permute-start | bytes 786440 | tf_op jit(solution)/shard_map/ppermute | solution.py:14
  56.2 0.8 select_reduce_fusion.20
  57.0 0.8 select_reduce_fusion.21
  57.9 0.8 select_reduce_fusion.18
  58.8 0.8 select_reduce_fusion.19
  59.6 0.1 and.230
  59.7 0.2 select_reduce_fusion.6
  59.9 0.8 select_reduce_fusion.8
  60.7 0.8 select_reduce_fusion.7
  61.5 0.6 add_subtract_fusion
  62.2 0.5 convolution_multiply_fusion.7
  62.7 0.5 convolution_multiply_fusion.3
  63.2 0.4 copy-done.2
  63.7 2.7 %fusion.12 = f32[1024,1024]{1,0:T(8,128)} fusion(bf16[128,1024]{1,0:T(8,128)(2,1)S(1)} %copy-done.2, f32[1024,128]{0,1:T(8,128)S(1)} %get-tuple-element.104, f32[1024]{0:T(1024)S(1)} %get-tuple-element.43, f32[1024]{0:T(1024)S(1)} %copy-done.1, pred[1024]{0:T(1024)(128)(4,1)S(1)} %get-tuple-element.113, pred[1024]{0:T(1024)(128)(4,1)S(1)} %get-tuple-element.122, ...), kind=kOutput, calls=%fused_computation.117 | convolution fusion | flops 269352960 | bytes 5122048 | tf_op jit(solution)/shard_map/dot_general | solution.py:70
  66.4 12.5 %collective-permute-start.8 = (f32[128,1024]{1,0:T(8,128)S(1)}, f32[128,1024]{1,0:T(8,128)S(1)}, u32[]{:S(2)}, u32[]{:S(2)}) collective-permute-start(f32[128,1024]{1,0:T(8,128)S(1)} %convolution_multiply_fusion.7), channel_id=1, source_target_pairs={{0,254},{2,0},{4,2},{6,4},{8,6},{10,8},{12,10},{14,12},{16,14},{18... | collective-permute-start | bytes 1572872 | tf_op jit(solution)/shard_map/ppermute | solution.py:14
  78.9 2.7 %fusion.17 = f32[1024,1024]{1,0:T(8,128)} fusion(bf16[128,1024]{1,0:T(8,128)(2,1)S(1)} %collective-permute-done.4, f32[1024,128]{0,1:T(8,128)S(1)} %get-tuple-element.94, f32[1024]{0:T(1024)S(1)} %get-tuple-element.43, f32[1024]{0:T(1024)S(1)} %copy-done.1, pred[1024]{0:T(1024)(128)(4,1)S(1)} %get-tuple-element.108, ...), kind=kOutput, calls=%fused_computation.122 | convolution fusion | flops 269352960 | bytes 5122048 | tf_op jit(solution)/shard_map/dot_general | solution.py:70
  81.6 2.7 %fusion.18 = f32[1024,1024]{1,0:T(8,128)} fusion(bf16[128,1024]{1,0:T(8,128)(2,1)S(1)} %collective-permute-done.5, f32[1024,128]{0,1:T(8,128)S(1)} %get-tuple-element.92, f32[1024]{0:T(1024)S(1)} %get-tuple-element.43, f32[1024]{0:T(1024)S(1)} %copy-done.1, pred[1024]{0:T(1024)(128)(4,1)S(1)} %get-tuple-element.107, ...), kind=kOutput, calls=%fused_computation.123 | convolution fusion | flops 269352960 | bytes 5122048 | tf_op jit(solution)/shard_map/dot_general | solution.py:70
  84.3 2.7 %fusion.13 = f32[1024,1024]{1,0:T(8,128)} fusion(bf16[128,1024]{1,0:T(8,128)(2,1)S(1)} %collective-permute-done, f32[1024,128]{0,1:T(8,128)S(1)} %get-tuple-element.102, f32[1024]{0:T(1024)S(1)} %get-tuple-element.43, f32[1024]{0:T(1024)S(1)} %copy-done.1, pred[1024]{0:T(1024)(128)(4,1)S(1)} %get-tuple-element.112, ...), kind=kOutput, calls=%fused_computation.118 | convolution fusion | flops 269352960 | bytes 5122048 | tf_op jit(solution)/shard_map/dot_general | solution.py:70
  87.0 2.7 %fusion.14 = f32[1024,1024]{1,0:T(8,128)} fusion(bf16[128,1024]{1,0:T(8,128)(2,1)S(1)} %collective-permute-done.1, f32[1024,128]{0,1:T(8,128)S(1)} %get-tuple-element.100, f32[1024]{0:T(1024)S(1)} %get-tuple-element.43, f32[1024]{0:T(1024)S(1)} %copy-done.1, pred[1024]{0:T(1024)(128)(4,1)S(1)} %get-tuple-element.111, ...), kind=kOutput, calls=%fused_computation.119 | convolution fusion | flops 269352960 | bytes 5122048 | tf_op jit(solution)/shard_map/dot_general | solution.py:70
  89.7 0.5 convolution_multiply_fusion.1
  90.2 0.5 convolution_multiply_fusion.5
  90.8 0.5 fusion
  91.3 0.3 collective-permute-start.13
  91.6 0.5 fusion.1
  92.1 8.4 %collective-permute-start.9 = (f32[128,1024]{1,0:T(8,128)S(1)}, f32[128,1024]{1,0:T(8,128)S(1)}, u32[]{:S(2)}, u32[]{:S(2)}) collective-permute-start(f32[128,1024]{1,0:T(8,128)S(1)} %fusion.1), channel_id=1, source_target_pairs={{0,254},{2,0},{4,2},{6,4},{8,6},{10,8},{12,10},{14,12},{16,14},{18... | collective-permute-start | bytes 1572872 | tf_op jit(solution)/shard_map/ppermute | solution.py:14
  100.5 0.5 convolution_multiply_fusion
  101.0 2.7 %fusion.15 = f32[1024,1024]{1,0:T(8,128)} fusion(bf16[128,1024]{1,0:T(8,128)(2,1)S(1)} %collective-permute-done.2, f32[1024,128]{0,1:T(8,128)S(1)} %get-tuple-element.98, f32[1024]{0:T(1024)S(1)} %get-tuple-element.43, f32[1024]{0:T(1024)S(1)} %copy-done.1, pred[1024]{0:T(1024)(128)(4,1)S(1)} %get-tuple-element.110, ...), kind=kOutput, calls=%fused_computation.120 | convolution fusion | flops 269352960 | bytes 5122048 | tf_op jit(solution)/shard_map/dot_general | solution.py:70
  103.8 0.1 collective-permute-start.14
  103.9 3.3 %collective-permute-done.9 = f32[128,1024]{1,0:T(8,128)S(1)} collective-permute-done((f32[128,1024]{1,0:T(8,128)S(1)}, f32[128,1024]{1,0:T(8,128)S(1)}, u32[]{:S(2)}, u32[]{:S(2)}) %collective-permute-start.9) | collective-permute-done | bytes 524320 | tf_op jit(solution)/shard_map/ppermute | solution.py:14
  107.3 15.1 %collective-permute-start.10 = (f32[128,1024]{1,0:T(8,128)S(1)}, f32[128,1024]{1,0:T(8,128)S(1)}, u32[]{:S(2)}, u32[]{:S(2)}) collective-permute-start(f32[128,1024]{1,0:T(8,128)S(1)} %add.260), channel_id=1, source_target_pairs={{0,254},{2,0},{4,2},{6,4},{8,6},{10,8},{12,10},{14,12},{16,14},{18... | collective-permute-start | bytes 1572872 | tf_op jit(solution)/shard_map/ppermute | solution.py:14
  122.4 0.5 convolution_multiply_fusion.4
  122.9 2.7 %fusion.16 = f32[1024,1024]{1,0:T(8,128)} fusion(bf16[128,1024]{1,0:T(8,128)(2,1)S(1)} %collective-permute-done.3, f32[1024,128]{0,1:T(8,128)S(1)} %get-tuple-element.96, f32[1024]{0:T(1024)S(1)} %get-tuple-element.43, f32[1024]{0:T(1024)S(1)} %copy-done.1, pred[1024]{0:T(1024)(128)(4,1)S(1)} %get-tuple-element.109, ...), kind=kOutput, calls=%fused_computation.121 | convolution fusion | flops 269352960 | bytes 5122048 | tf_op jit(solution)/shard_map/dot_general | solution.py:70
  125.7 0.1 collective-permute-start.15
  125.9 14.3 %collective-permute-start.11 = (f32[128,1024]{1,0:T(8,128)S(1)}, f32[128,1024]{1,0:T(8,128)S(1)}, u32[]{:S(2)}, u32[]{:S(2)}) collective-permute-start(f32[128,1024]{1,0:T(8,128)S(1)} %add.261), channel_id=1, source_target_pairs={{0,254},{2,0},{4,2},{6,4},{8,6},{10,8},{12,10},{14,12},{16,14},{18... | collective-permute-start | bytes 1572872 | tf_op jit(solution)/shard_map/ppermute | solution.py:14
  140.3 0.5 convolution_multiply_fusion.8
  140.8 2.8 %fusion.19 = f32[1024,1024]{1,0:T(8,128)} fusion(bf16[128,1024]{1,0:T(8,128)(2,1)S(1)} %collective-permute-done.6, f32[1024,128]{0,1:T(8,128)S(1)} %get-tuple-element.90, f32[1024]{0:T(1024)S(1)} %get-tuple-element.43, f32[1024]{0:T(1024)S(1)} %copy-done.1, pred[1024]{0:T(1024)(128)(4,1)S(1)} %get-tuple-element.106, ...), kind=kOutput, calls=%fused_computation.124 | convolution fusion | flops 269352960 | bytes 5122048 | tf_op jit(solution)/shard_map/dot_general | solution.py:70
  143.6 0.9 add_add_fusion
  144.5 13.7 %add_multiply_fusion = f32[1024,1024]{1,0:T(8,128)} fusion(f32[1024,1024]{1,0:T(8,128)} %fusion.19, f32[1024,1024]{1,0:T(8,128)} %fusion.18, f32[1024,1024]{1,0:T(8,128)} %fusion.17, f32[1024,1024]{1,0:T(8,128)} %fusion.16, f32[1024,1024]{1,0:T(8,128)} %fusion.15, f32[1024,1024]{1,0:T(8,128)} %fusion.14, f32[1024,1024]{1,0:T(8,128)} %fusion.12, ...), kind=kOutput, calls=%fused_computation | convolution fusion | flops 278790144 | bytes 38676480 | tf_op jit(solution)/shard_map/dot_general | solution.py:70
  158.2 19.2 %reduce-scatter.2.cloned.1.call-done = f32[64,1024]{1,0:T(8,128)} async-done(((f32[128,1024]{1,0:T(8,128)}), f32[64,1024]{1,0:T(8,128)}) %reduce-scatter.2.cloned.1.call-update) | async-done | bytes 262160 | tf_op jit(solution)/shard_map/reduce_scatter | solution.py:82
  (29 shorter events, 0.4 us)
Async XLA Ops:
  7.2 7.9 %copy-start = (bf16[1024,1024]{1,0:T(8,128)(2,1)S(1)}, bf16[1024,1024]{1,0:T(8,128)(2,1)}, u32[]{:S(2)}) copy-start(bf16[1024,1024]{1,0:T(8,128)(2,1)} %param.5) | copy-start | bytes 6291460
  7.2 170.2 %reduce-scatter.2.cloned.1.call-start = ((), (), s32[]{:S(2)}) async-start(), calls=%async_computation.1 | async-start | bytes 786432 | tf_op jit(solution)/shard_map/reduce_scatter | solution.py:82
  7.2 9.6 %collective-permute-start = (bf16[128,1024]{1,0:T(8,128)(2,1)}, bf16[128,1024]{1,0:T(8,128)(2,1)S(1)}, u32[]{:S(2)}, u32[]{:S(2)}) collective-permute-start(bf16[128,1024]{1,0:T(8,128)(2,1)} %param.6), channel_id=1, source_target_pairs={{0,2},{2,4},{4,6},{6,8},{8,10},{10,12},{12,14},{14,16},{16,18},{18... | collective-permute-start | bytes 786440 | tf_op jit(solution)/shard_map/ppermute | solution.py:14
  11.7 10.0 %collective-permute-start.1 = (bf16[128,1024]{1,0:T(8,128)(2,1)}, bf16[128,1024]{1,0:T(8,128)(2,1)S(1)}, u32[]{:S(2)}, u32[]{:S(2)}) collective-permute-start(bf16[128,1024]{1,0:T(8,128)(2,1)} %param.6), channel_id=1, source_target_pairs={{0,254},{2,0},{4,2},{6,4},{8,6},{10,8},{12,10},{14,12},{16,14},{18... | collective-permute-start | bytes 786440 | tf_op jit(solution)/shard_map/ppermute | solution.py:14
  16.9 11.1 %collective-permute-start.2 = (bf16[128,1024]{1,0:T(8,128)(2,1)S(1)}, bf16[128,1024]{1,0:T(8,128)(2,1)S(1)}, u32[]{:S(2)}, u32[]{:S(2)}) collective-permute-start(bf16[128,1024]{1,0:T(8,128)(2,1)S(1)} %collective-permute-done), channel_id=1, source_target_pairs={{0,2},{2,4},{4,6},{6,8},{8,10},{10,12},{12,14},{14,16},{16,18},{18... | collective-permute-start | bytes 786440 | tf_op jit(solution)/shard_map/ppermute | solution.py:14
  21.7 9.5 %collective-permute-start.3 = (bf16[128,1024]{1,0:T(8,128)(2,1)S(1)}, bf16[128,1024]{1,0:T(8,128)(2,1)S(1)}, u32[]{:S(2)}, u32[]{:S(2)}) collective-permute-start(bf16[128,1024]{1,0:T(8,128)(2,1)S(1)} %collective-permute-done.1), channel_id=1, source_target_pairs={{0,254},{2,0},{4,2},{6,4},{8,6},{10,8},{12,10},{14,12},{16,14},{18... | collective-permute-start | bytes 786440 | tf_op jit(solution)/shard_map/ppermute | solution.py:14
  28.0 14.9 %collective-permute-start.4 = (bf16[128,1024]{1,0:T(8,128)(2,1)S(1)}, bf16[128,1024]{1,0:T(8,128)(2,1)S(1)}, u32[]{:S(2)}, u32[]{:S(2)}) collective-permute-start(bf16[128,1024]{1,0:T(8,128)(2,1)S(1)} %collective-permute-done.2), channel_id=1, source_target_pairs={{0,2},{2,4},{4,6},{6,8},{8,10},{10,12},{12,14},{14,16},{16,18},{18... | collective-permute-start | bytes 786440 | tf_op jit(solution)/shard_map/ppermute | solution.py:14
  31.2 11.9 %collective-permute-start.5 = (bf16[128,1024]{1,0:T(8,128)(2,1)S(1)}, bf16[128,1024]{1,0:T(8,128)(2,1)S(1)}, u32[]{:S(2)}, u32[]{:S(2)}) collective-permute-start(bf16[128,1024]{1,0:T(8,128)(2,1)S(1)} %collective-permute-done.3), channel_id=1, source_target_pairs={{0,254},{2,0},{4,2},{6,4},{8,6},{10,8},{12,10},{14,12},{16,14},{18... | collective-permute-start | bytes 786440 | tf_op jit(solution)/shard_map/ppermute | solution.py:14
  42.9 15.8 %collective-permute-start.6 = (bf16[128,1024]{1,0:T(8,128)(2,1)S(1)}, bf16[128,1024]{1,0:T(8,128)(2,1)S(1)}, u32[]{:S(2)}, u32[]{:S(2)}) collective-permute-start(bf16[128,1024]{1,0:T(8,128)(2,1)S(1)} %collective-permute-done.4), channel_id=1, source_target_pairs={{0,2},{2,4},{4,6},{6,8},{8,10},{10,12},{12,14},{14,16},{16,18},{18... | collective-permute-start | bytes 786440 | tf_op jit(solution)/shard_map/ppermute | solution.py:14
  43.1 14.8 %collective-permute-start.7 = (bf16[128,1024]{1,0:T(8,128)(2,1)S(1)}, bf16[128,1024]{1,0:T(8,128)(2,1)S(1)}, u32[]{:S(2)}, u32[]{:S(2)}) collective-permute-start(bf16[128,1024]{1,0:T(8,128)(2,1)S(1)} %collective-permute-done.5), channel_id=1, source_target_pairs={{0,254},{2,0},{4,2},{6,4},{8,6},{10,8},{12,10},{14,12},{16,14},{18... | collective-permute-start | bytes 786440 | tf_op jit(solution)/shard_map/ppermute | solution.py:14
  58.7 0.9 copy-start.3
  59.9 2.2 %copy-start.1 = (f32[1024]{0:T(1024)S(1)}, f32[1024]{0:T(1024)}, u32[]{:S(2)}) copy-start(f32[1024]{0:T(1024)} %param.9) | copy-start | bytes 12292
  62.7 1.0 copy-start.2
  66.4 24.4 %collective-permute-start.12 = (f32[128,1024]{1,0:T(8,128)S(1)}, f32[128,1024]{1,0:T(8,128)S(1)}, u32[]{:S(2)}, u32[]{:S(2)}) collective-permute-start(f32[128,1024]{1,0:T(8,128)S(1)} %convolution_multiply_fusion.3), channel_id=1, source_target_pairs={{0,2},{2,4},{4,6},{6,8},{8,10},{10,12},{12,14},{14,16},{16,18},{18... | collective-permute-start | bytes 1572872 | tf_op jit(solution)/shard_map/ppermute | solution.py:14
  66.4 25.2 %collective-permute-start.8 = (f32[128,1024]{1,0:T(8,128)S(1)}, f32[128,1024]{1,0:T(8,128)S(1)}, u32[]{:S(2)}, u32[]{:S(2)}) collective-permute-start(f32[128,1024]{1,0:T(8,128)S(1)} %convolution_multiply_fusion.7), channel_id=1, source_target_pairs={{0,254},{2,0},{4,2},{6,4},{8,6},{10,8},{12,10},{14,12},{16,14},{18... | collective-permute-start | bytes 1572872 | tf_op jit(solution)/shard_map/ppermute | solution.py:14
  91.3 12.5 %collective-permute-start.13 = (f32[128,1024]{1,0:T(8,128)S(1)}, f32[128,1024]{1,0:T(8,128)S(1)}, u32[]{:S(2)}, u32[]{:S(2)}) collective-permute-start(f32[128,1024]{1,0:T(8,128)S(1)} %fusion), channel_id=1, source_target_pairs={{0,2},{2,4},{4,6},{6,8},{8,10},{10,12},{12,14},{14,16},{16,18},{18... | collective-permute-start | bytes 1572872 | tf_op jit(solution)/shard_map/ppermute | solution.py:14
  92.1 15.1 %collective-permute-start.9 = (f32[128,1024]{1,0:T(8,128)S(1)}, f32[128,1024]{1,0:T(8,128)S(1)}, u32[]{:S(2)}, u32[]{:S(2)}) collective-permute-start(f32[128,1024]{1,0:T(8,128)S(1)} %fusion.1), channel_id=1, source_target_pairs={{0,254},{2,0},{4,2},{6,4},{8,6},{10,8},{12,10},{14,12},{16,14},{18... | collective-permute-start | bytes 1572872 | tf_op jit(solution)/shard_map/ppermute | solution.py:14
  103.8 21.8 %collective-permute-start.14 = (f32[128,1024]{1,0:T(8,128)S(1)}, f32[128,1024]{1,0:T(8,128)S(1)}, u32[]{:S(2)}, u32[]{:S(2)}) collective-permute-start(f32[128,1024]{1,0:T(8,128)S(1)} %add.264), channel_id=1, source_target_pairs={{0,2},{2,4},{4,6},{6,8},{8,10},{10,12},{12,14},{14,16},{16,18},{18... | collective-permute-start | bytes 1572872 | tf_op jit(solution)/shard_map/ppermute | solution.py:14
  107.3 18.5 %collective-permute-start.10 = (f32[128,1024]{1,0:T(8,128)S(1)}, f32[128,1024]{1,0:T(8,128)S(1)}, u32[]{:S(2)}, u32[]{:S(2)}) collective-permute-start(f32[128,1024]{1,0:T(8,128)S(1)} %add.260), channel_id=1, source_target_pairs={{0,254},{2,0},{4,2},{6,4},{8,6},{10,8},{12,10},{14,12},{16,14},{18... | collective-permute-start | bytes 1572872 | tf_op jit(solution)/shard_map/ppermute | solution.py:14
  125.7 17.8 %collective-permute-start.15 = (f32[128,1024]{1,0:T(8,128)S(1)}, f32[128,1024]{1,0:T(8,128)S(1)}, u32[]{:S(2)}, u32[]{:S(2)}) collective-permute-start(f32[128,1024]{1,0:T(8,128)S(1)} %add.265), channel_id=1, source_target_pairs={{0,2},{2,4},{4,6},{6,8},{8,10},{10,12},{12,14},{14,16},{16,18},{18... | collective-permute-start | bytes 1572872 | tf_op jit(solution)/shard_map/ppermute | solution.py:14
  125.9 17.7 %collective-permute-start.11 = (f32[128,1024]{1,0:T(8,128)S(1)}, f32[128,1024]{1,0:T(8,128)S(1)}, u32[]{:S(2)}, u32[]{:S(2)}) collective-permute-start(f32[128,1024]{1,0:T(8,128)S(1)} %add.261), channel_id=1, source_target_pairs={{0,254},{2,0},{4,2},{6,4},{8,6},{10,8},{12,10},{14,12},{16,14},{18... | collective-permute-start | bytes 1572872 | tf_op jit(solution)/shard_map/ppermute | solution.py:14
Sparse Core Ops, SparseCore 0:
  144.6 32.7 reduce-scatter.1
where the time goes:
time: 184 us
  starting transfers between devices  85.9 us (47%)
  matrix products  48.7 us (26%)
  waiting for transfers between devices  27.8 us (15%)
  between operations  14.4 us (8%)
  other arithmetic  6.3 us (3%)
    ppermute x16, starting transfers between devices, passed_along(): return lax.ppermute(x, axis, [(i, (i + by) % count) for i in range(count)])  85.9 us
    dot_general x9, matrix products, body(): jnp.dot(coefficient, key_tile, preferred_element_type=jnp.float32)  35.4 us
    reduce_scatter x1, waiting for transfers between devices, body(): lax.psum_scatter(key_parts[0] + upward + downward, 'rep', scatter_dimensi...  19.2 us
    ppermute x16, waiting for transfers between devices, passed_along(): return lax.ppermute(x, axis, [(i, (i + by) % count) for i in range(count)])  8.57 us
    dot_general x9, matrix products, body(): lax.dot_general(queries, key_tile, (((1,), (1,)), ((), ())), preferred_el...  8.53 us
    dot_general x9, matrix products, body(): lax.dot_general(coefficient, queries, (((0,), (0,)), ((), ())), preferred...  4.68 us
  transfers between devices with their start and end apart: 17, of which 4 were waited for; matrix products, arithmetic and copies ran while one was open for 26% of the time, Pallas kernels for 0%

commit v1 on v0

v1 whole, which is shorter than its diff:
```python
import math

import jax
import jax.numpy as jnp
from jax import lax
from jax.sharding import PartitionSpec as P

D = 1024
REACH = 4


def passed_along(x, axis, by):
    count = lax.axis_size(axis)
    return lax.ppermute(x, axis, [(i, (i + by) % count) for i in range(count)])


def swapped(x, axis):
    count = lax.axis_size(axis)
    return lax.ppermute(x, axis, [(i, i ^ 1) for i in range(count)])


def body(queries, keys, neg_mask, positive, row_weight):
    logit_scale = 2.0 / math.sqrt(D)
    cycle_size = lax.axis_size("dp")
    cycle_index = lax.axis_index("dp")
    rep_index = lax.axis_index("rep")
    core = cycle_index % 2
    delta = 1 - 2 * core
    query_rows = queries.shape[0]
    tile_rows = keys.shape[0]
    query_blocks = query_rows // tile_rows
    inner_idx = jnp.arange(tile_rows, dtype=jnp.int32)
    same_row = inner_idx[:, None] == inner_idx[None, :]

    down2 = passed_along(keys, "dp", 2)
    up2 = passed_along(keys, "dp", -2)
    down4 = passed_along(down2, "dp", 2)
    up4 = passed_along(up2, "dp", -2)
    sw_own = swapped(keys, "dp")
    sw_down2 = swapped(down2, "dp")
    sw_up2 = swapped(up2, "dp")
    sw_far = swapped(jnp.where(core == 0, up4, down4), "dp")
    key_tiles = [
        ("own", keys, 0),
        ("sw_own", sw_own, delta),
        ("down2", down2, -2),
        ("up2", up2, 2),
        ("sw_down2", sw_down2, delta - 2),
        ("sw_up2", sw_up2, delta + 2),
        ("down4", down4, -4),
        ("up4", up4, 4),
        ("sw_far", sw_far, -3 * delta),
    ]
    run_max = jnp.full((query_rows,), -1e30, jnp.float32)
    run_sum = jnp.zeros((query_rows,), jnp.float32)
    pos_logit = jnp.zeros((query_rows,), jnp.float32)
    stored = []
    for name, key_tile, offset in key_tiles:
        owner_idx = (cycle_index + offset) % cycle_size
        column = lax.dynamic_slice_in_dim(neg_mask, owner_idx, 1, 1)[:, 0]
        hit_block = positive == owner_idx
        allow_block = (column == 1) | hit_block
        allowed = jnp.broadcast_to(
            allow_block[:, None, None], (query_blocks, tile_rows, tile_rows)
        ).reshape(query_rows, tile_rows)
        at_positive = (hit_block[:, None, None] & same_row[None, :, :]).reshape(
            query_rows, tile_rows
        )
        logit_tile = logit_scale * lax.dot_general(
            queries, key_tile, (((1,), (1,)), ((), ())), preferred_element_type=jnp.float32
        )
        masked = jnp.where(allowed, logit_tile, jnp.float32(-1e30))
        next_max = jnp.maximum(run_max, jnp.max(masked, axis=1))
        run_sum = run_sum * jnp.exp(run_max - next_max) + jnp.sum(
            jnp.where(allowed, jnp.exp(masked - next_max[:, None]), 0.0), axis=1
        )
        run_max = next_max
        pos_logit = pos_logit + jnp.sum(jnp.where(at_positive, logit_tile, 0.0), axis=1)
        stored.append((name, key_tile, masked, at_positive))
    log_total = run_max + jnp.log(run_sum)
    row_loss = log_total - pos_logit
    grad_query = jnp.zeros(queries.shape, jnp.float32)
    key_parts = {}
    for name, key_tile, masked, at_positive in stored:
        softmax_p = jnp.exp(masked - log_total[:, None])
        coefficient = (row_weight[:, None] * (softmax_p - at_positive.astype(jnp.float32))).astype(
            jnp.bfloat16
        )
        grad_query = grad_query + logit_scale * jnp.dot(
            coefficient, key_tile, preferred_element_type=jnp.float32
        )
        key_parts[name] = lax.dot_general(
            coefficient, queries, (((0,), (0,)), ((), ())), preferred_element_type=jnp.float32
        )
    back_own = swapped(key_parts["sw_own"], "dp")
    back_down2 = swapped(key_parts["sw_down2"], "dp")
    back_up2 = swapped(key_parts["sw_up2"], "dp")
    back_far = swapped(key_parts["sw_far"], "dp")
    zero = jnp.zeros_like(back_far)
    far_up = key_parts["up4"] + jnp.where(core == 0, back_far, zero)
    far_down = key_parts["down4"] + jnp.where(core == 0, zero, back_far)
    near_up = key_parts["up2"] + back_up2 + passed_along(far_up, "dp", 2)
    near_down = key_parts["down2"] + back_down2 + passed_along(far_down, "dp", -2)
    total = (
        key_parts["own"]
        + back_own
        + passed_along(near_up, "dp", 2)
        + passed_along(near_down, "dp", -2)
    )
    half = tile_rows // 2
    halves = total.reshape(2, half, total.shape[1])
    mine = jnp.where(rep_index == 0, halves[0], halves[1])
    other = jnp.where(rep_index == 0, halves[1], halves[0])
    grad_keys = logit_scale * (mine + lax.ppermute(other, "rep", [(0, 1), (1, 0)]))
    return (row_loss, grad_query, grad_keys)


def solution(mesh):
    placed = (
        P(("dp", "rep"), None),
        P("dp", None),
        P(("dp", "rep"), None),
        P(("dp", "rep")),
        P(("dp", "rep")),
    )
    return jax.shard_map(
        body,
        mesh=mesh,
        in_specs=placed,
        out_specs=(P(("dp", "rep")), P(("dp", "rep"), None), P(("dp", "rep"), None)),
        check_vma=False,
    )
```

time: 184 us -> 144 us (0.78)
  starting transfers between devices: 85.9 us -> 51.9 us
  waiting for transfers between devices: 27.8 us -> 44.2 us
  between operations: 14.4 us -> 0.97 us
  matrix products: 48.7 us -> 40 us
    ppermute x16 -> x8, starting transfers between devices: 85.9 us -> 36.9 us  [passed_along(): return lax.ppermute(x, axis, [(i, (i + by) % count) for i in range(count)])]
    ppermute x16 -> x8, waiting for transfers between devices: 8.57 us -> 44.2 us  [passed_along(): return lax.ppermute(x, axis, [(i, (i + by) % count) for i in range(count)])]
    reduce_scatter x1 -> x0, waiting for transfers between devices: 19.2 us -> none  [body(): lax.psum_scatter(key_parts[0] + upward + downward, 'rep', scatter_dimensi...]
    ppermute x0 -> x9, starting transfers between devices: none -> 15 us  [the longest x8 14.9 us: swapped(): return lax.ppermute(x, axis, [(i, i ^ 1) for i in range(count)])]
    dot_general x9, matrix products: 35.4 us -> 26.4 us  [body(): jnp.dot(coefficient, key_tile, preferred_element_type=jnp.float32)]
  transfers between devices with their start and end apart: 17 -> 17, of which waited for: 4 -> 5; matrix products, arithmetic and copies ran while one was open for 26% -> 27% of each run, Pallas kernels for 0% -> 0%
where the time goes in v1:
time: 144 us
  starting transfers between devices  51.9 us (36%)
  waiting for transfers between devices  44.2 us (31%)
  matrix products  40 us (28%)
  other arithmetic  5.41 us (4%)
    ppermute x8, waiting for transfers between devices, passed_along(): return lax.ppermute(x, axis, [(i, (i + by) % count) for i in range(count)])  44.2 us
    ppermute x8, starting transfers between devices, passed_along(): return lax.ppermute(x, axis, [(i, (i + by) % count) for i in range(count)])  36.9 us
    dot_general x9, matrix products, body(): jnp.dot(coefficient, key_tile, preferred_element_type=jnp.float32)  26.4 us
    ppermute x8, starting transfers between devices, swapped(): return lax.ppermute(x, axis, [(i, i ^ 1) for i in range(count)])  14.9 us
    dot_general x9, matrix products, body(): lax.dot_general(queries, key_tile, (((1,), (1,)), ((), ())), preferred_el...  8.56 us
    dot_general x9, matrix products, body(): lax.dot_general(coefficient, queries, (((0,), (0,)), ((), ())), preferred...  4.97 us
  transfers between devices with their start and end apart: 17, of which 5 were waited for; matrix products, arithmetic and copies ran while one was open for 27% of the time, Pallas kernels for 0%

profile of v1, /device:TPU:1, one launch (start us, length us, event | category | flops | bytes accessed | tf_op | source)
XLA Modules:
  0.0 143.7 jit_solution(16728901150173894470)
XLA Ops:
  0.6 3.9 %collective-permute-start.1 = (bf16[128,1024]{1,0:T(8,128)(2,1)}, bf16[128,1024]{1,0:T(8,128)(2,1)S(1)}, u32[]{:S(2)}, u32[]{:S(2)}) collective-permute-start(bf16[128,1024]{1,0:T(8,128)(2,1)} %param.6), channel_id=1, source_target_pairs={{0,4},{2,6},{4,8},{6,10},{8,12},{10,14},{12,16},{14,18},{16,20},{1... | collective-permute-start | bytes 786440 | tf_op jit(solution)/shard_map/ppermute | solution.py:14
  4.5 1.0 collective-permute-start
  5.5 7.5 %collective-permute-start.2 = (bf16[128,1024]{1,0:T(8,128)(2,1)}, bf16[128,1024]{1,0:T(8,128)(2,1)S(1)}, u32[]{:S(2)}, u32[]{:S(2)}) collective-permute-start(bf16[128,1024]{1,0:T(8,128)(2,1)} %param.6), channel_id=1, source_target_pairs={{0,252},{2,254},{4,0},{6,2},{8,4},{10,6},{12,8},{14,10},{16,12},{1... | collective-permute-start | bytes 786440 | tf_op jit(solution)/shard_map/ppermute | solution.py:14
  13.1 1.4 fusion.13
  14.4 0.7 fusion.57
  15.2 0.1 broadcast_bitcast_fusion.16
  15.3 0.1 broadcast_bitcast_fusion.10
  15.4 0.1 broadcast_bitcast_fusion.2
  15.4 0.1 broadcast_bitcast_fusion.12
  15.5 0.1 broadcast_bitcast_fusion.4
  15.7 0.1 broadcast_bitcast_fusion.6
  15.7 0.1 broadcast_bitcast_fusion
  15.8 1.8 %select_reduce_fusion.26 = (f32[1024]{0:T(1024)S(1)}, f32[1024,128]{0,1:T(8,128)S(1)}) fusion(pred[1024]{0:T(1024)(128)(4,1)S(1)} %get-tuple-element.122, bf16[1024,1024]{1,0:T(8,128)(2,1)S(1)} %copy-done, bf16[128,1024]{1,0:T(8,128)(2,1)} %param.6), kind=kOutput, calls=%fused_computation.64 | convolution fusion | flops 268827648 | bytes 2888704 | tf_op jit(solution)/shard_map/dot_general | solution.py:69
  17.6 2.4 %collective-permute-done.1 = bf16[128,1024]{1,0:T(8,128)(2,1)S(1)} collective-permute-done((bf16[128,1024]{1,0:T(8,128)(2,1)}, bf16[128,1024]{1,0:T(8,128)(2,1)S(1)}, u32[]{:S(2)}, u32[]{:S(2)}) %collective-permute-start.1) | collective-permute-done | bytes 262176 | tf_op jit(solution)/shard_map/ppermute | solution.py:14
  20.0 0.2 collective-permute-start.5
  20.1 1.5 %collective-permute-start.3 = (bf16[128,1024]{1,0:T(8,128)(2,1)S(1)}, bf16[128,1024]{1,0:T(8,128)(2,1)S(1)}, u32[]{:S(2)}, u32[]{:S(2)}) collective-permute-start(bf16[128,1024]{1,0:T(8,128)(2,1)S(1)} %collective-permute-done.1), channel_id=1, source_target_pairs={{0,2},{2,0},{4,6},{6,4},{8,10},{10,8},{12,14},{14,12},{16,18},{18,... | collective-permute-start | bytes 786440 | tf_op jit(solution)/shard_map/ppermute | solution.py:19
  21.7 0.5 collective-permute-done.2
  22.2 7.9 %collective-permute-start.6 = (bf16[128,1024]{1,0:T(8,128)(2,1)S(1)}, bf16[128,1024]{1,0:T(8,128)(2,1)S(1)}, u32[]{:S(2)}, u32[]{:S(2)}) collective-permute-start(bf16[128,1024]{1,0:T(8,128)(2,1)S(1)} %collective-permute-done.2), channel_id=1, source_target_pairs={{0,252},{2,254},{4,0},{6,2},{8,4},{10,6},{12,8},{14,10},{16,12},{1... | collective-permute-start | bytes 786440 | tf_op jit(solution)/shard_map/ppermute | solution.py:14
  30.1 4.2 %collective-permute-start.4 = (bf16[128,1024]{1,0:T(8,128)(2,1)S(1)}, bf16[128,1024]{1,0:T(8,128)(2,1)S(1)}, u32[]{:S(2)}, u32[]{:S(2)}) collective-permute-start(bf16[128,1024]{1,0:T(8,128)(2,1)S(1)} %collective-permute-done.2), channel_id=1, source_target_pairs={{0,2},{2,0},{4,6},{6,4},{8,10},{10,8},{12,14},{14,12},{16,18},{18,... | collective-permute-start | bytes 786440 | tf_op jit(solution)/shard_map/ppermute | solution.py:19
  34.2 0.8 select_reduce_fusion.23
  35.1 0.8 select_reduce_fusion.24
  36.0 0.8 select_reduce_fusion.25
  36.9 7.2 %collective-permute-start.7 = (bf16[128,1024]{1,0:T(8,128)(2,1)S(1)}, bf16[128,1024]{1,0:T(8,128)(2,1)S(1)}, u32[]{:S(2)}, u32[]{:S(2)}) collective-permute-start(bf16[128,1024]{1,0:T(8,128)(2,1)S(1)} %broadcast_select_fusion), channel_id=1, source_target_pairs={{0,2},{2,0},{4,6},{6,4},{8,10},{10,8},{12,14},{14,12},{16,18},{18,... | collective-permute-start | bytes 786440 | tf_op jit(solution)/shard_map/ppermute | solution.py:19
  44.0 0.8 select_reduce_fusion.19
  44.9 0.9 select_reduce_fusion.20
  45.8 0.8 select_reduce_fusion.21
  46.6 0.8 select_reduce_fusion.22
  47.5 0.9 select_reduce_fusion.18
  48.4 0.2 select_reduce_fusion.6
  48.7 0.8 select_reduce_fusion.8
  49.5 0.8 select_reduce_fusion.7
  50.3 0.6 add_subtract_fusion
  50.9 0.5 fusion.22
  51.5 0.5 fusion.20
  52.0 0.5 fusion.16
  52.6 0.5 fusion.28
  53.1 0.4 copy-done.2
  53.5 0.8 fusion.15
  54.3 0.1 collective-permute-start.10
  54.4 0.5 collective-permute-start.8
  54.9 0.1 collective-permute-start.13
  55.0 0.4 collective-permute-start.9
  55.4 0.8 fusion.19
  56.2 0.8 fusion.18
  57.0 2.7 %fusion.25 = f32[1024,1024]{1,0:T(8,128)} fusion(bf16[128,1024]{1,0:T(8,128)(2,1)S(1)} %collective-permute-done.5, f32[1024,128]{0,1:T(8,128)S(1)} %get-tuple-element.92, f32[1024]{0:T(1024)S(1)} %get-tuple-element.43, f32[1024]{0:T(1024)S(1)} %copy-done.1, pred[1024]{0:T(1024)(128)(4,1)S(1)} %get-tuple-element.107, ...), kind=kOutput, calls=%fused_computation.128 | convolution fusion | flops 269352960 | bytes 5122048 | tf_op jit(solution)/shard_map/dot_general | solution.py:89
  59.7 2.8 %fusion.29 = f32[1024,1024]{1,0:T(8,128)} fusion(bf16[128,1024]{1,0:T(8,128)(2,1)S(1)} %collective-permute-done.7, f32[1024,128]{0,1:T(8,128)S(1)} %get-tuple-element.88, f32[1024]{0:T(1024)S(1)} %get-tuple-element.43, f32[1024]{0:T(1024)S(1)} %copy-done.1, pred[1024]{0:T(1024)(128)(4,1)S(1)} %get-tuple-element.105, ...), kind=kOutput, calls=%fused_computation.132 | convolution fusion | flops 269352960 | bytes 5122048 | tf_op jit(solution)/shard_map/dot_general | solution.py:89
  62.5 0.5 select_add_fusion
  63.0 8.6 %collective-permute-start.14 = (f32[128,1024]{1,0:T(8,128)S(1)}, f32[128,1024]{1,0:T(8,128)S(1)}, u32[]{:S(2)}, u32[]{:S(2)}) collective-permute-start(f32[128,1024]{1,0:T(8,128)S(1)} %select_add_fusion), channel_id=1, source_target_pairs={{0,252},{2,254},{4,0},{6,2},{8,4},{10,6},{12,8},{14,10},{16,12},{1... | collective-permute-start | bytes 1572872 | tf_op jit(solution)/shard_map/ppermute | solution.py:14
  71.6 0.5 select_add_fusion.1
  72.1 0.1 collective-permute-start.11
  72.2 2.7 %fusion.17 = f32[1024,1024]{1,0:T(8,128)} fusion(bf16[128,1024]{1,0:T(8,128)(2,1)S(1)} %collective-permute-done, f32[1024,128]{0,1:T(8,128)S(1)} %get-tuple-element.102, f32[1024]{0:T(1024)S(1)} %get-tuple-element.43, f32[1024]{0:T(1024)S(1)} %copy-done.1, pred[1024]{0:T(1024)(128)(4,1)S(1)} %get-tuple-element.112, ...), kind=kOutput, calls=%fused_computation.120 | convolution fusion | flops 269352960 | bytes 5122048 | tf_op jit(solution)/shard_map/dot_general | solution.py:89
  74.9 18.4 %collective-permute-done.14 = f32[128,1024]{1,0:T(8,128)S(1)} collective-permute-done((f32[128,1024]{1,0:T(8,128)S(1)}, f32[128,1024]{1,0:T(8,128)S(1)}, u32[]{:S(2)}, u32[]{:S(2)}) %collective-permute-start.14) | collective-permute-done | bytes 524320 | tf_op jit(solution)/shard_map/ppermute | solution.py:14
  93.4 0.6 fusion
  93.9 8.7 %collective-permute-start.15 = (f32[128,1024]{1,0:T(8,128)S(1)}, f32[128,1024]{1,0:T(8,128)S(1)}, u32[]{:S(2)}, u32[]{:S(2)}) collective-permute-start(f32[128,1024]{1,0:T(8,128)S(1)} %fusion), channel_id=1, source_target_pairs={{0,252},{2,254},{4,0},{6,2},{8,4},{10,6},{12,8},{14,10},{16,12},{1... | collective-permute-start | bytes 1572872 | tf_op jit(solution)/shard_map/ppermute | solution.py:14
  102.7 0.6 fusion.1
  103.3 0.1 collective-permute-start.12
  103.4 2.7 %fusion.21 = f32[1024,1024]{1,0:T(8,128)} fusion(bf16[128,1024]{1,0:T(8,128)(2,1)S(1)} %collective-permute-done.3, f32[1024,128]{0,1:T(8,128)S(1)} %get-tuple-element.96, f32[1024]{0:T(1024)S(1)} %get-tuple-element.43, f32[1024]{0:T(1024)S(1)} %copy-done.1, pred[1024]{0:T(1024)(128)(4,1)S(1)} %get-tuple-element.109, ...), kind=kOutput, calls=%fused_computation.124 | convolution fusion | flops 269352960 | bytes 5122048 | tf_op jit(solution)/shard_map/dot_general | solution.py:89
  106.1 2.7 %fusion.23 = f32[1024,1024]{1,0:T(8,128)} fusion(bf16[128,1024]{1,0:T(8,128)(2,1)S(1)} %collective-permute-done.4, f32[1024,128]{0,1:T(8,128)S(1)} %get-tuple-element.94, f32[1024]{0:T(1024)S(1)} %get-tuple-element.43, f32[1024]{0:T(1024)S(1)} %copy-done.1, pred[1024]{0:T(1024)(128)(4,1)S(1)} %get-tuple-element.108, ...), kind=kOutput, calls=%fused_computation.126 | convolution fusion | flops 269352960 | bytes 5122048 | tf_op jit(solution)/shard_map/dot_general | solution.py:89
  108.8 15.5 %collective-permute-done.15 = f32[128,1024]{1,0:T(8,128)S(1)} collective-permute-done((f32[128,1024]{1,0:T(8,128)S(1)}, f32[128,1024]{1,0:T(8,128)S(1)}, u32[]{:S(2)}, u32[]{:S(2)}) %collective-permute-start.15) | collective-permute-done | bytes 524320 | tf_op jit(solution)/shard_map/ppermute | solution.py:14
  124.3 7.4 %collective-permute-done.12 = f32[128,1024]{1,0:T(8,128)S(1)} collective-permute-done((f32[128,1024]{1,0:T(8,128)S(1)}, f32[128,1024]{1,0:T(8,128)S(1)}, u32[]{:S(2)}, u32[]{:S(2)}) %collective-permute-start.12) | collective-permute-done | bytes 524320 | tf_op jit(solution)/shard_map/ppermute | solution.py:14
  131.7 0.6 fusion.3
  132.4 0.1 collective-permute-start.16
  132.5 10.4 %add_multiply_fusion = f32[1024,1024]{1,0:T(8,128)} fusion(f32[1024,1024]{1,0:T(8,128)} %fusion.29, f32[1024,1024]{1,0:T(8,128)} %fusion.25, f32[1024,1024]{1,0:T(8,128)} %fusion.23, f32[1024,1024]{1,0:T(8,128)} %fusion.21, f32[1024,1024]{1,0:T(8,128)S(1)} %fusion.19, f32[1024,1024]{1,0:T(8,128)S(1)} %fusion.18, f32[1024,1024]{1,0:T(8,128)S(1)} %fusion.15, ...), kind=kOutput, calls=%fused_computation | convolution fusion | flops 278790144 | bytes 38676480 | tf_op jit(solution)/shard_map/dot_general | solution.py:89
  142.9 0.8 add_multiply_fusion.1
  (24 shorter events, 0.4 us)
Async XLA Ops:
  0.6 15.2 %copy-start = (bf16[1024,1024]{1,0:T(8,128)(2,1)S(1)}, bf16[1024,1024]{1,0:T(8,128)(2,1)}, u32[]{:S(2)}) copy-start(bf16[1024,1024]{1,0:T(8,128)(2,1)} %param.5) | copy-start | bytes 6291460
  0.6 19.3 %collective-permute-start.1 = (bf16[128,1024]{1,0:T(8,128)(2,1)}, bf16[128,1024]{1,0:T(8,128)(2,1)S(1)}, u32[]{:S(2)}, u32[]{:S(2)}) collective-permute-start(bf16[128,1024]{1,0:T(8,128)(2,1)} %param.6), channel_id=1, source_target_pairs={{0,4},{2,6},{4,8},{6,10},{8,12},{10,14},{12,16},{14,18},{16,20},{1... | collective-permute-start | bytes 786440 | tf_op jit(solution)/shard_map/ppermute | solution.py:14
  4.5 31.4 %collective-permute-start = (bf16[128,1024]{1,0:T(8,128)(2,1)}, bf16[128,1024]{1,0:T(8,128)(2,1)S(1)}, u32[]{:S(2)}, u32[]{:S(2)}) collective-permute-start(bf16[128,1024]{1,0:T(8,128)(2,1)} %param.6), channel_id=1, source_target_pairs={{0,2},{2,0},{4,6},{6,4},{8,10},{10,8},{12,14},{14,12},{16,18},{18,... | collective-permute-start | bytes 786440 | tf_op jit(solution)/shard_map/ppermute | solution.py:19
  5.5 16.7 %collective-permute-start.2 = (bf16[128,1024]{1,0:T(8,128)(2,1)}, bf16[128,1024]{1,0:T(8,128)(2,1)S(1)}, u32[]{:S(2)}, u32[]{:S(2)}) collective-permute-start(bf16[128,1024]{1,0:T(8,128)(2,1)} %param.6), channel_id=1, source_target_pairs={{0,252},{2,254},{4,0},{6,2},{8,4},{10,6},{12,8},{14,10},{16,12},{1... | collective-permute-start | bytes 786440 | tf_op jit(solution)/shard_map/ppermute | solution.py:14
  20.0 16.8 %collective-permute-start.5 = (bf16[128,1024]{1,0:T(8,128)(2,1)S(1)}, bf16[128,1024]{1,0:T(8,128)(2,1)S(1)}, u32[]{:S(2)}, u32[]{:S(2)}) collective-permute-start(bf16[128,1024]{1,0:T(8,128)(2,1)S(1)} %collective-permute-done.1), channel_id=1, source_target_pairs={{0,4},{2,6},{4,8},{6,10},{8,12},{10,14},{12,16},{14,18},{16,20},{1... | collective-permute-start | bytes 786440 | tf_op jit(solution)/shard_map/ppermute | solution.py:14
  20.1 26.5 %collective-permute-start.3 = (bf16[128,1024]{1,0:T(8,128)(2,1)S(1)}, bf16[128,1024]{1,0:T(8,128)(2,1)S(1)}, u32[]{:S(2)}, u32[]{:S(2)}) collective-permute-start(bf16[128,1024]{1,0:T(8,128)(2,1)S(1)} %collective-permute-done.1), channel_id=1, source_target_pairs={{0,2},{2,0},{4,6},{6,4},{8,10},{10,8},{12,14},{14,12},{16,18},{18,... | collective-permute-start | bytes 786440 | tf_op jit(solution)/shard_map/ppermute | solution.py:19
  22.2 14.6 %collective-permute-start.6 = (bf16[128,1024]{1,0:T(8,128)(2,1)S(1)}, bf16[128,1024]{1,0:T(8,128)(2,1)S(1)}, u32[]{:S(2)}, u32[]{:S(2)}) collective-permute-start(bf16[128,1024]{1,0:T(8,128)(2,1)S(1)} %collective-permute-done.2), channel_id=1, source_target_pairs={{0,252},{2,254},{4,0},{6,2},{8,4},{10,6},{12,8},{14,10},{16,12},{1... | collective-permute-start | bytes 786440 | tf_op jit(solution)/shard_map/ppermute | solution.py:14
  30.1 15.7 %collective-permute-start.4 = (bf16[128,1024]{1,0:T(8,128)(2,1)S(1)}, bf16[128,1024]{1,0:T(8,128)(2,1)S(1)}, u32[]{:S(2)}, u32[]{:S(2)}) collective-permute-start(bf16[128,1024]{1,0:T(8,128)(2,1)S(1)} %collective-permute-done.2), channel_id=1, source_target_pairs={{0,2},{2,0},{4,6},{6,4},{8,10},{10,8},{12,14},{14,12},{16,18},{18,... | collective-permute-start | bytes 786440 | tf_op jit(solution)/shard_map/ppermute | solution.py:19
  36.9 10.6 %collective-permute-start.7 = (bf16[128,1024]{1,0:T(8,128)(2,1)S(1)}, bf16[128,1024]{1,0:T(8,128)(2,1)S(1)}, u32[]{:S(2)}, u32[]{:S(2)}) collective-permute-start(bf16[128,1024]{1,0:T(8,128)(2,1)S(1)} %broadcast_select_fusion), channel_id=1, source_target_pairs={{0,2},{2,0},{4,6},{6,4},{8,10},{10,8},{12,14},{14,12},{16,18},{18,... | collective-permute-start | bytes 786440 | tf_op jit(solution)/shard_map/ppermute | solution.py:19
  48.7 2.3 %copy-start.1 = (f32[1024]{0:T(1024)S(1)}, f32[1024]{0:T(1024)}, u32[]{:S(2)}) copy-start(f32[1024]{0:T(1024)} %param.9) | copy-start | bytes 12292
  52.6 1.0 copy-start.2
  54.3 8.1 %collective-permute-start.10 = (f32[128,1024]{1,0:T(8,128)S(1)}, f32[128,1024]{1,0:T(8,128)S(1)}, u32[]{:S(2)}, u32[]{:S(2)}) collective-permute-start(f32[128,1024]{1,0:T(8,128)S(1)} %fusion.28), channel_id=1, source_target_pairs={{0,2},{2,0},{4,6},{6,4},{8,10},{10,8},{12,14},{14,12},{16,18},{18,... | collective-permute-start | bytes 1572872 | tf_op jit(solution)/shard_map/ppermute | solution.py:19
  54.4 54.4 %collective-permute-start.8 = (f32[128,1024]{1,0:T(8,128)S(1)}, f32[128,1024]{1,0:T(8,128)S(1)}, u32[]{:S(2)}, u32[]{:S(2)}) collective-permute-start(f32[128,1024]{1,0:T(8,128)S(1)} %fusion.16), channel_id=1, source_target_pairs={{0,2},{2,0},{4,6},{6,4},{8,10},{10,8},{12,14},{14,12},{16,18},{18,... | collective-permute-start | bytes 1572872 | tf_op jit(solution)/shard_map/ppermute | solution.py:19
  54.9 20.0 %collective-permute-start.13 = (f32[128,1024]{1,0:T(8,128)S(1)}, f32[128,1024]{1,0:T(8,128)S(1)}, u32[]{:S(2)}, u32[]{:S(2)}) collective-permute-start(f32[128,1024]{1,0:T(8,128)S(1)} %fusion.20), channel_id=1, source_target_pairs={{0,2},{2,0},{4,6},{6,4},{8,10},{10,8},{12,14},{14,12},{16,18},{18,... | collective-permute-start | bytes 1572872 | tf_op jit(solution)/shard_map/ppermute | solution.py:19
  55.0 47.7 %collective-permute-start.9 = (f32[128,1024]{1,0:T(8,128)S(1)}, f32[128,1024]{1,0:T(8,128)S(1)}, u32[]{:S(2)}, u32[]{:S(2)}) collective-permute-start(f32[128,1024]{1,0:T(8,128)S(1)} %fusion.22), channel_id=1, source_target_pairs={{0,2},{2,0},{4,6},{6,4},{8,10},{10,8},{12,14},{14,12},{16,18},{18,... | collective-permute-start | bytes 1572872 | tf_op jit(solution)/shard_map/ppermute | solution.py:19
  63.0 30.4 %collective-permute-start.14 = (f32[128,1024]{1,0:T(8,128)S(1)}, f32[128,1024]{1,0:T(8,128)S(1)}, u32[]{:S(2)}, u32[]{:S(2)}) collective-permute-start(f32[128,1024]{1,0:T(8,128)S(1)} %select_add_fusion), channel_id=1, source_target_pairs={{0,252},{2,254},{4,0},{6,2},{8,4},{10,6},{12,8},{14,10},{16,12},{1... | collective-permute-start | bytes 1572872 | tf_op jit(solution)/shard_map/ppermute | solution.py:14
  72.1 30.6 %collective-permute-start.11 = (f32[128,1024]{1,0:T(8,128)S(1)}, f32[128,1024]{1,0:T(8,128)S(1)}, u32[]{:S(2)}, u32[]{:S(2)}) collective-permute-start(f32[128,1024]{1,0:T(8,128)S(1)} %select_add_fusion.1), channel_id=1, source_target_pairs={{0,4},{2,6},{4,8},{6,10},{8,12},{10,14},{12,16},{14,18},{16,20},{1... | collective-permute-start | bytes 1572872 | tf_op jit(solution)/shard_map/ppermute | solution.py:14
  93.9 30.4 %collective-permute-start.15 = (f32[128,1024]{1,0:T(8,128)S(1)}, f32[128,1024]{1,0:T(8,128)S(1)}, u32[]{:S(2)}, u32[]{:S(2)}) collective-permute-start(f32[128,1024]{1,0:T(8,128)S(1)} %fusion), channel_id=1, source_target_pairs={{0,252},{2,254},{4,0},{6,2},{8,4},{10,6},{12,8},{14,10},{16,12},{1... | collective-permute-start | bytes 1572872 | tf_op jit(solution)/shard_map/ppermute | solution.py:14
  103.3 28.4 %collective-permute-start.12 = (f32[128,1024]{1,0:T(8,128)S(1)}, f32[128,1024]{1,0:T(8,128)S(1)}, u32[]{:S(2)}, u32[]{:S(2)}) collective-permute-start(f32[128,1024]{1,0:T(8,128)S(1)} %fusion.1), channel_id=1, source_target_pairs={{0,4},{2,6},{4,8},{6,10},{8,12},{10,14},{12,16},{14,18},{16,20},{1... | collective-permute-start | bytes 1572872 | tf_op jit(solution)/shard_map/ppermute | solution.py:14
  132.4 10.6 %collective-permute-start.16 = (f32[64,1024]{1,0:T(8,128)S(1)}, f32[64,1024]{1,0:T(8,128)S(1)}, u32[]{:S(2)}, u32[]{:S(2)}) collective-permute-start(f32[64,1024]{1,0:T(8,128)S(1)} %slice_select_fusion), channel_id=1, source_target_pairs={{0,1},{1,0},{2,3},{3,2},{4,5},{5,4},{6,7},{7,6},{8,9},{9,8},{10,11... | collective-permute-start | bytes 786440 | tf_op jit(solution)/shard_map/ppermute | solution.py:114

commit v2 on v1

--- a/solution.py
+++ b/solution.py
@@ -79,19 +79,21 @@
         stored.append((name, key_tile, masked, at_positive))
     log_total = run_max + jnp.log(run_sum)
     row_loss = log_total - pos_logit
-    grad_query = jnp.zeros(queries.shape, jnp.float32)
-    key_parts = {}
+    coefficients = []
     for name, key_tile, masked, at_positive in stored:
         softmax_p = jnp.exp(masked - log_total[:, None])
-        coefficient = (row_weight[:, None] * (softmax_p - at_positive.astype(jnp.float32))).astype(
-            jnp.bfloat16
+        coefficients.append(
+            (row_weight[:, None] * (softmax_p - at_positive.astype(jnp.float32))).astype(jnp.bfloat16)
         )
-        grad_query = grad_query + logit_scale * jnp.dot(
-            coefficient, key_tile, preferred_element_type=jnp.float32
-        )
-        key_parts[name] = lax.dot_general(
-            coefficient, queries, (((0,), (0,)), ((), ())), preferred_element_type=jnp.float32
-        )
+    coefficient = jnp.concatenate(coefficients, axis=1)
+    window = jnp.concatenate([key_tile for _, key_tile, _, _ in stored], axis=0)
+    grad_query = logit_scale * jnp.dot(coefficient, window, preferred_element_type=jnp.float32)
+    all_parts = lax.dot_general(
+        coefficient, queries, (((0,), (0,)), ((), ())), preferred_element_type=jnp.float32
+    )
+    key_parts = {
+        name: all_parts[i * tile_rows : (i + 1) * tile_rows] for i, (name, _, _, _) in enumerate(stored)
+    }
     back_own = swapped(key_parts["sw_own"], "dp")
     back_down2 = swapped(key_parts["sw_down2"], "dp")
     back_up2 = swapped(key_parts["sw_up2"], "dp")

time: 144 us -> 134 us (0.931)
  matrix products: 40 us -> 17.3 us
  local copies, waits for them, and re-layouts: 1.14 us -> 10.5 us
  starting transfers between devices: 51.9 us -> 46.1 us
  other arithmetic: 5.41 us -> 10.6 us
  waiting for transfers between devices: 44.2 us -> 48.1 us
    dot_general x9 -> x1, matrix products: 26.4 us -> 6.13 us  [body(): jnp.dot(coefficient, window, preferred_element_type=jnp.float32)]
    unnamed x6 -> x17, local copies, waits for them, and re-layouts: 0.41 us -> 7.5 us
    ppermute x8, starting transfers between devices: 14.9 us -> 10.1 us  [swapped(): return lax.ppermute(x, axis, [(i, i ^ 1) for i in range(count)])]
    add x0 -> x3, other arithmetic: none -> 2.8 us  [the longest x1 1.35 us: body(): key_parts['own'] + back_own + passed_along(near_up, 'dp', 2)]
    dot_general x9 -> x1, matrix products: 4.97 us -> 2.62 us  [body(): lax.dot_general(coefficient, queries, (((0,), (0,)), ((), ())), preferred...]
    unnamed x0 -> x9, other arithmetic: none -> 2.27 us
  transfers between devices with their start and end apart: 17 -> 17, of which waited for: 5 -> 6; matrix products, arithmetic and copies ran while one was open for 27% -> 19% of each run, Pallas kernels for 0% -> 0%
where the time goes in v2:
time: 134 us; the launch traced here: 133 us
  waiting for transfers between devices  48.1 us (36%)
  starting transfers between devices  46.1 us (34%)
  matrix products  17.3 us (13%)
  other arithmetic  10.6 us (8%)
  local copies, waits for them, and re-layouts  10.5 us (8%)
    ppermute x8, waiting for transfers between devices, passed_along(): return lax.ppermute(x, axis, [(i, (i + by) % count) for i in range(count)])  45.5 us
    ppermute x8, starting transfers between devices, passed_along(): return lax.ppermute(x, axis, [(i, (i + by) % count) for i in range(count)])  35.9 us
    ppermute x8, starting transfers between devices, swapped(): return lax.ppermute(x, axis, [(i, i ^ 1) for i in range(count)])  10.1 us
    dot_general x9, matrix products, body(): lax.dot_general(queries, key_tile, (((1,), (1,)), ((), ())), preferred_el...  8.52 us
    unnamed x17, local copies, waits for them, and re-layouts  7.5 us
    dot_general x1, matrix products, body(): jnp.dot(coefficient, window, preferred_element_type=jnp.float32)  6.13 us
  transfers between devices with their start and end apart: 17, of which 6 were waited for; matrix products, arithmetic and copies ran while one was open for 19% of the time, Pallas kernels for 0%

profile of v2, /device:TPU:1, one launch (start us, length us, event | category | flops | bytes accessed | tf_op | source)
XLA Modules:
  0.0 133.4 jit_solution(10816405391290460699)
XLA Ops:
  0.6 3.9 %collective-permute-start.1 = (bf16[128,1024]{1,0:T(8,128)(2,1)}, bf16[128,1024]{1,0:T(8,128)(2,1)S(1)}, u32[]{:S(2)}, u32[]{:S(2)}) collective-permute-start(bf16[128,1024]{1,0:T(8,128)(2,1)} %param.6), channel_id=1, source_target_pairs={{0,4},{2,6},{4,8},{6,10},{8,12},{10,14},{12,16},{14,18},{16,20},{1... | collective-permute-start | bytes 786440 | tf_op jit(solution)/shard_map/ppermute | solution.py:14
  4.5 1.0 collective-permute-start
  5.5 7.5 %collective-permute-start.2 = (bf16[128,1024]{1,0:T(8,128)(2,1)}, bf16[128,1024]{1,0:T(8,128)(2,1)S(1)}, u32[]{:S(2)}, u32[]{:S(2)}) collective-permute-start(bf16[128,1024]{1,0:T(8,128)(2,1)} %param.6), channel_id=1, source_target_pairs={{0,252},{2,254},{4,0},{6,2},{8,4},{10,6},{12,8},{14,10},{16,12},{1... | collective-permute-start | bytes 786440 | tf_op jit(solution)/shard_map/ppermute | solution.py:14
  13.0 1.7 %constant_dynamic-update-slice_fusion.8 = bf16[1152,1024]{1,0:T(8,128)(2,1)} fusion(bf16[128,1024]{1,0:T(8,128)(2,1)} %param.6), kind=kLoop, calls=%fused_computation.86 | loop fusion | bytes 524288
  14.7 1.3 %fusion.22 = (pred[8]{0:T(512)(128)(4,1)S(1)}, pred[8]{0:T(512)(128)(4,1)S(1)}, pred[8]{0:T(512)(128)(4,1)S(1)}, pred[8]{0:T(512)(128)(4,1)S(1)}, pred[8]{0:T(51...) fusion(s32[8,128]{1,0:T(8,128)} %param.7, ...), kind=kLoop, calls=%fused_computation.106 | loop fusion | flops 72 | bytes 396 | tf_op jit(solution)/shard_map/eq | solution.py:62
  16.0 0.7 fusion.33
  16.8 0.1 broadcast_bitcast_fusion.17
  17.6 0.1 broadcast_bitcast_fusion.4
  17.7 0.1 broadcast_bitcast_fusion.6
  17.9 1.8 %select_reduce_fusion.26 = (f32[1024]{0:T(1024)S(1)}, f32[1024,128]{0,1:T(8,128)S(1)}) fusion(pred[1024]{0:T(1024)(128)(4,1)S(1)} %broadcast_bitcast_fusion.17, bf16[1024,1024]{1,0:T(8,128)(2,1)S(1)} %copy-done, bf16[128,1024]{1,0:T(8,128)(2,1)} %param.6), kind=kOutput, calls=%fused_computation.64 | convolution fusion | flops 268827648 | bytes 2888704 | tf_op jit(solution)/shard_map/dot_general | solution.py:69
  19.7 0.3 collective-permute-done.1
  20.0 0.2 collective-permute-start.5
  20.1 1.5 %collective-permute-start.3 = (bf16[128,1024]{1,0:T(8,128)(2,1)S(1)}, bf16[128,1024]{1,0:T(8,128)(2,1)S(1)}, u32[]{:S(2)}, u32[]{:S(2)}) collective-permute-start(bf16[128,1024]{1,0:T(8,128)(2,1)S(1)} %collective-permute-done.1), channel_id=1, source_target_pairs={{0,2},{2,0},{4,6},{6,4},{8,10},{10,8},{12,14},{14,12},{16,18},{18,... | collective-permute-start | bytes 786440 | tf_op jit(solution)/shard_map/ppermute | solution.py:19
  21.7 0.5 collective-permute-done.2
  22.2 7.9 %collective-permute-start.6 = (bf16[128,1024]{1,0:T(8,128)(2,1)S(1)}, bf16[128,1024]{1,0:T(8,128)(2,1)S(1)}, u32[]{:S(2)}, u32[]{:S(2)}) collective-permute-start(bf16[128,1024]{1,0:T(8,128)(2,1)S(1)} %collective-permute-done.2), channel_id=1, source_target_pairs={{0,252},{2,254},{4,0},{6,2},{8,4},{10,6},{12,8},{14,10},{16,12},{1... | collective-permute-start | bytes 786440 | tf_op jit(solution)/shard_map/ppermute | solution.py:14
  30.1 4.2 %collective-permute-start.4 = (bf16[128,1024]{1,0:T(8,128)(2,1)S(1)}, bf16[128,1024]{1,0:T(8,128)(2,1)S(1)}, u32[]{:S(2)}, u32[]{:S(2)}) collective-permute-start(bf16[128,1024]{1,0:T(8,128)(2,1)S(1)} %collective-permute-done.2), channel_id=1, source_target_pairs={{0,2},{2,0},{4,6},{6,4},{8,10},{10,8},{12,14},{14,12},{16,18},{18,... | collective-permute-start | bytes 786440 | tf_op jit(solution)/shard_map/ppermute | solution.py:19
  34.2 0.8 select_reduce_fusion.23
  35.1 0.8 select_reduce_fusion.24
  36.0 0.8 select_reduce_fusion.25
  36.8 0.7 constant_dynamic-update-slice_fusion.7
  37.5 0.7 constant_dynamic-update-slice_fusion.6
  38.3 0.7 constant_dynamic-update-slice_fusion.5
  39.0 0.7 constant_dynamic-update-slice_fusion.4
  39.7 0.7 constant_dynamic-update-slice_fusion.3
  40.5 0.7 constant_dynamic-update-slice_fusion.2
  41.2 0.8 constant_dynamic-update-slice_fusion.1
  42.0 2.5 %collective-permute-start.7 = (bf16[128,1024]{1,0:T(8,128)(2,1)S(1)}, bf16[128,1024]{1,0:T(8,128)(2,1)S(1)}, u32[]{:S(2)}, u32[]{:S(2)}) collective-permute-start(bf16[128,1024]{1,0:T(8,128)(2,1)S(1)} %get-tuple-element.79), channel_id=1, source_target_pairs={{0,2},{2,0},{4,6},{6,4},{8,10},{10,8},{12,14},{14,12},{16,18},{18,... | collective-permute-start | bytes 786440 | tf_op jit(solution)/shard_map/ppermute | solution.py:19
  44.5 0.8 select_reduce_fusion.21
  45.3 0.8 select_reduce_fusion.19
  46.2 0.8 select_reduce_fusion.22
  47.0 0.8 select_reduce_fusion.20
  47.9 0.8 select_reduce_fusion.18
  48.9 0.2 select_reduce_fusion.6
  49.1 0.8 select_reduce_fusion.8
  49.9 0.8 select_reduce_fusion.7
  50.7 0.6 add_subtract_fusion
  51.3 0.2 fusion.5
  51.5 0.2 fusion.6
  51.7 0.2 fusion.7
  51.9 0.2 fusion.8
  52.1 0.2 fusion.9
  52.3 0.2 fusion.10
  52.5 0.2 fusion.11
  52.7 0.2 fusion.12
  52.8 0.2 fusion.13
  53.0 1.4 %copy-done.3 = bf16[1024,1152]{0,1:T(8,128)(2,1)} copy-done((bf16[1024,1152]{0,1:T(8,128)(2,1)}, bf16[1024,1152]{0,1:T(8,128)(2,1)S(1)}, u32[]{:S(2)}) %copy-start.3) | copy-done | bytes 2359320
  54.4 2.6 %fusion.36 = f32[1152,1024]{1,0:T(8,128)S(1)} fusion(bf16[1024,1152]{0,1:T(8,128)(2,1)S(1)} %fusion.13, bf16[1024,1024]{1,0:T(8,128)(2,1)S(1)} %copy-done), kind=kOutput, calls=%fused_computation.147 | convolution fusion | flops 2415919104 | bytes 9175040 | tf_op jit(solution)/shard_map/dot_general | solution.py:91
  57.1 1.1 fusion.35
  58.2 0.5 collective-permute-start.13
  58.7 1.4 %collective-permute-done.10 = f32[128,1024]{1,0:T(8,128)S(1)} collective-permute-done((f32[128,1024]{1,0:T(8,128)S(1)}, f32[128,1024]{1,0:T(8,128)S(1)}, u32[]{:S(2)}, u32[]{:S(2)}) %collective-permute-start.10) | collective-permute-done | bytes 524320 | tf_op jit(solution)/shard_map/ppermute | solution.py:19
  60.1 0.1 slice_add_fusion.2
  60.2 0.1 collective-permute-start.11
  60.3 8.6 %collective-permute-start.14 = (f32[128,1024]{1,0:T(8,128)S(1)}, f32[128,1024]{1,0:T(8,128)S(1)}, u32[]{:S(2)}, u32[]{:S(2)}) collective-permute-start(f32[128,1024]{1,0:T(8,128)S(1)} %get-tuple-element.71), channel_id=1, source_target_pairs={{0,252},{2,254},{4,0},{6,2},{8,4},{10,6},{12,8},{14,10},{16,12},{1... | collective-permute-start | bytes 1572872 | tf_op jit(solution)/shard_map/ppermute | solution.py:14
  68.9 0.4 collective-permute-start.8
  69.3 23.0 %collective-permute-done.11 = f32[128,1024]{1,0:T(8,128)S(1)} collective-permute-done((f32[128,1024]{1,0:T(8,128)S(1)}, f32[128,1024]{1,0:T(8,128)S(1)}, u32[]{:S(2)}, u32[]{:S(2)}) %collective-permute-start.11) | collective-permute-done | bytes 524320 | tf_op jit(solution)/shard_map/ppermute | solution.py:14
  92.3 1.3 %fusion.2 = (f32[128,1024]{1,0:T(8,128)}, f32[128,1024]{1,0:T(8,128)}) fusion(f32[128,1024]{1,0:T(8,128)S(1)} %collective-permute-done.11, f32[128,1024]{1,0:T(8,128)S(1)} %collective-permute-done.9, f32[1152,1024]{1,0:T(8,128)S(1)} %fusion.36, f32[128,1024]{1,0:T(8,128)S(1)} %collective-permute-done.14, f32[128,1024]{1,0:T(8,128)S(1)} %collective-permute-done.13), kind=kLoop, calls=%fused_computation.16 | loop fusion | flops 524288 | bytes 4194304 | tf_op jit(solution)/shard_map/add | solution.py:104
  93.6 7.8 %collective-permute-start.15 = (f32[128,1024]{1,0:T(8,128)}, f32[128,1024]{1,0:T(8,128)}, u32[]{:S(2)}, u32[]{:S(2)}) collective-permute-start(f32[128,1024]{1,0:T(8,128)} %get-tuple-element.77), channel_id=1, source_target_pairs={{0,252},{2,254},{4,0},{6,2},{8,4},{10,6},{12,8},{14,10},{16,12},{1... | collective-permute-start | bytes 1572872 | tf_op jit(solution)/shard_map/ppermute | solution.py:14
  101.4 0.7 constant_dynamic-update-slice_fusion
  102.2 21.6 %collective-permute-done.12 = f32[128,1024]{1,0:T(8,128)S(1)} collective-permute-done((f32[128,1024]{1,0:T(8,128)}, f32[128,1024]{1,0:T(8,128)S(1)}, u32[]{:S(2)}, u32[]{:S(2)}) %collective-permute-start.12) | collective-permute-done | bytes 524320 | tf_op jit(solution)/shard_map/ppermute | solution.py:14
  123.8 1.3 %fusion.4 = f32[128,1024]{1,0:T(8,128)S(1)} fusion(f32[128,1024]{1,0:T(8,128)} %collective-permute-done.15, f32[128,1024]{1,0:T(8,128)S(1)} %collective-permute-done.12, f32[128,1024]{1,0:T(8,128)S(1)} %collective-permute-done.8, f32[1152,1024]{1,0:T(8,128)} %copy-done.1), kind=kLoop, calls=%fused_computation.19 | loop fusion | flops 393216 | bytes 2621440 | tf_op jit(solution)/shard_map/add | solution.py:107
  125.2 0.1 collective-permute-start.16
  125.3 6.1 %convolution_multiply_fusion = f32[1024,1024]{1,0:T(8,128)} fusion(bf16[1024,1152]{0,1:T(8,128)(2,1)S(1)} %copy-done.4, bf16[1152,1024]{1,0:T(8,128)(2,1)} %constant_dynamic-update-slice_fusion), kind=kOutput, calls=%fused_computation | convolution fusion | flops 2416967680 | bytes 8912896 | tf_op jit(solution)/shard_map/dot_general | solution.py:90
  131.5 1.2 collective-permute-done.16
  132.7 0.7 add_multiply_fusion
  (39 shorter events, 1.1 us)
Async XLA Ops:
  0.6 17.2 %copy-start = (bf16[1024,1024]{1,0:T(8,128)(2,1)S(1)}, bf16[1024,1024]{1,0:T(8,128)(2,1)}, u32[]{:S(2)}) copy-start(bf16[1024,1024]{1,0:T(8,128)(2,1)} %param.5) | copy-start | bytes 6291460
  0.6 19.3 %collective-permute-start.1 = (bf16[128,1024]{1,0:T(8,128)(2,1)}, bf16[128,1024]{1,0:T(8,128)(2,1)S(1)}, u32[]{:S(2)}, u32[]{:S(2)}) collective-permute-start(bf16[128,1024]{1,0:T(8,128)(2,1)} %param.6), channel_id=1, source_target_pairs={{0,4},{2,6},{4,8},{6,10},{8,12},{10,14},{12,16},{14,18},{16,20},{1... | collective-permute-start | bytes 786440 | tf_op jit(solution)/shard_map/ppermute | solution.py:14
  4.5 31.4 %collective-permute-start = (bf16[128,1024]{1,0:T(8,128)(2,1)}, bf16[128,1024]{1,0:T(8,128)(2,1)S(1)}, u32[]{:S(2)}, u32[]{:S(2)}) collective-permute-start(bf16[128,1024]{1,0:T(8,128)(2,1)} %param.6), channel_id=1, source_target_pairs={{0,2},{2,0},{4,6},{6,4},{8,10},{10,8},{12,14},{14,12},{16,18},{18,... | collective-permute-start | bytes 786440 | tf_op jit(solution)/shard_map/ppermute | solution.py:19
  5.5 16.7 %collective-permute-start.2 = (bf16[128,1024]{1,0:T(8,128)(2,1)}, bf16[128,1024]{1,0:T(8,128)(2,1)S(1)}, u32[]{:S(2)}, u32[]{:S(2)}) collective-permute-start(bf16[128,1024]{1,0:T(8,128)(2,1)} %param.6), channel_id=1, source_target_pairs={{0,252},{2,254},{4,0},{6,2},{8,4},{10,6},{12,8},{14,10},{16,12},{1... | collective-permute-start | bytes 786440 | tf_op jit(solution)/shard_map/ppermute | solution.py:14
  20.0 20.5 %collective-permute-start.5 = (bf16[128,1024]{1,0:T(8,128)(2,1)S(1)}, bf16[128,1024]{1,0:T(8,128)(2,1)S(1)}, u32[]{:S(2)}, u32[]{:S(2)}) collective-permute-start(bf16[128,1024]{1,0:T(8,128)(2,1)S(1)} %collective-permute-done.1), channel_id=1, source_target_pairs={{0,4},{2,6},{4,8},{6,10},{8,12},{10,14},{12,16},{14,18},{16,20},{1... | collective-permute-start | bytes 786440 | tf_op jit(solution)/shard_map/ppermute | solution.py:14
  20.1 18.9 %collective-permute-start.3 = (bf16[128,1024]{1,0:T(8,128)(2,1)S(1)}, bf16[128,1024]{1,0:T(8,128)(2,1)S(1)}, u32[]{:S(2)}, u32[]{:S(2)}) collective-permute-start(bf16[128,1024]{1,0:T(8,128)(2,1)S(1)} %collective-permute-done.1), channel_id=1, source_target_pairs={{0,2},{2,0},{4,6},{6,4},{8,10},{10,8},{12,14},{14,12},{16,18},{18,... | collective-permute-start | bytes 786440 | tf_op jit(solution)/shard_map/ppermute | solution.py:19
  22.2 19.0 %collective-permute-start.6 = (bf16[128,1024]{1,0:T(8,128)(2,1)S(1)}, bf16[128,1024]{1,0:T(8,128)(2,1)S(1)}, u32[]{:S(2)}, u32[]{:S(2)}) collective-permute-start(bf16[128,1024]{1,0:T(8,128)(2,1)S(1)} %collective-permute-done.2), channel_id=1, source_target_pairs={{0,252},{2,254},{4,0},{6,2},{8,4},{10,6},{12,8},{14,10},{16,12},{1... | collective-permute-start | bytes 786440 | tf_op jit(solution)/shard_map/ppermute | solution.py:14
  30.1 9.7 %collective-permute-start.4 = (bf16[128,1024]{1,0:T(8,128)(2,1)S(1)}, bf16[128,1024]{1,0:T(8,128)(2,1)S(1)}, u32[]{:S(2)}, u32[]{:S(2)}) collective-permute-start(bf16[128,1024]{1,0:T(8,128)(2,1)S(1)} %collective-permute-done.2), channel_id=1, source_target_pairs={{0,2},{2,0},{4,6},{6,4},{8,10},{10,8},{12,14},{14,12},{16,18},{18,... | collective-permute-start | bytes 786440 | tf_op jit(solution)/shard_map/ppermute | solution.py:19
  42.0 5.9 %collective-permute-start.7 = (bf16[128,1024]{1,0:T(8,128)(2,1)S(1)}, bf16[128,1024]{1,0:T(8,128)(2,1)S(1)}, u32[]{:S(2)}, u32[]{:S(2)}) collective-permute-start(bf16[128,1024]{1,0:T(8,128)(2,1)S(1)} %get-tuple-element.79), channel_id=1, source_target_pairs={{0,2},{2,0},{4,6},{6,4},{8,10},{10,8},{12,14},{14,12},{16,18},{18,... | collective-permute-start | bytes 786440 | tf_op jit(solution)/shard_map/ppermute | solution.py:19
  49.1 2.2 %copy-start.2 = (f32[1024]{0:T(1024)S(1)}, f32[1024]{0:T(1024)}, u32[]{:S(2)}) copy-start(f32[1024]{0:T(1024)} %param.9) | copy-start | bytes 12292
  53.0 1.4 %copy-start.3 = (bf16[1024,1152]{0,1:T(8,128)(2,1)}, bf16[1024,1152]{0,1:T(8,128)(2,1)S(1)}, u32[]{:S(2)}) copy-start(bf16[1024,1152]{0,1:T(8,128)(2,1)S(1)} %fusion.13) | copy-start | bytes 7077892
  57.1 35.2 %copy-start.1 = (f32[1152,1024]{1,0:T(8,128)}, f32[1152,1024]{1,0:T(8,128)S(1)}, u32[]{:S(2)}) copy-start(f32[1152,1024]{1,0:T(8,128)S(1)} %fusion.36) | copy-start | bytes 14155780
  58.2 1.9 %collective-permute-start.10 = (f32[128,1024]{1,0:T(8,128)S(1)}, f32[128,1024]{1,0:T(8,128)S(1)}, u32[]{:S(2)}, u32[]{:S(2)}) collective-permute-start(f32[128,1024]{1,0:T(8,128)S(1)} %get-tuple-element.74), channel_id=1, source_target_pairs={{0,2},{2,0},{4,6},{6,4},{8,10},{10,8},{12,14},{14,12},{16,18},{18,... | collective-permute-start | bytes 1572872 | tf_op jit(solution)/shard_map/ppermute | solution.py:19
  58.2 11.1 %collective-permute-start.13 = (f32[128,1024]{1,0:T(8,128)S(1)}, f32[128,1024]{1,0:T(8,128)S(1)}, u32[]{:S(2)}, u32[]{:S(2)}) collective-permute-start(f32[128,1024]{1,0:T(8,128)S(1)} %get-tuple-element.73), channel_id=1, source_target_pairs={{0,2},{2,0},{4,6},{6,4},{8,10},{10,8},{12,14},{14,12},{16,18},{18,... | collective-permute-start | bytes 1572872 | tf_op jit(solution)/shard_map/ppermute | solution.py:19
  58.7 10.6 %collective-permute-start.9 = (f32[128,1024]{1,0:T(8,128)S(1)}, f32[128,1024]{1,0:T(8,128)S(1)}, u32[]{:S(2)}, u32[]{:S(2)}) collective-permute-start(f32[128,1024]{1,0:T(8,128)S(1)} %get-tuple-element.75), channel_id=1, source_target_pairs={{0,2},{2,0},{4,6},{6,4},{8,10},{10,8},{12,14},{14,12},{16,18},{18,... | collective-permute-start | bytes 1572872 | tf_op jit(solution)/shard_map/ppermute | solution.py:19
  60.2 32.1 %collective-permute-start.11 = (f32[128,1024]{1,0:T(8,128)S(1)}, f32[128,1024]{1,0:T(8,128)S(1)}, u32[]{:S(2)}, u32[]{:S(2)}) collective-permute-start(f32[128,1024]{1,0:T(8,128)S(1)} %get-tuple-element.70), channel_id=1, source_target_pairs={{0,4},{2,6},{4,8},{6,10},{8,12},{10,14},{12,16},{14,18},{16,20},{1... | collective-permute-start | bytes 1572872 | tf_op jit(solution)/shard_map/ppermute | solution.py:14
  60.3 32.0 %collective-permute-start.14 = (f32[128,1024]{1,0:T(8,128)S(1)}, f32[128,1024]{1,0:T(8,128)S(1)}, u32[]{:S(2)}, u32[]{:S(2)}) collective-permute-start(f32[128,1024]{1,0:T(8,128)S(1)} %get-tuple-element.71), channel_id=1, source_target_pairs={{0,252},{2,254},{4,0},{6,2},{8,4},{10,6},{12,8},{14,10},{16,12},{1... | collective-permute-start | bytes 1572872 | tf_op jit(solution)/shard_map/ppermute | solution.py:14
  68.9 33.3 %collective-permute-start.8 = (f32[128,1024]{1,0:T(8,128)}, f32[128,1024]{1,0:T(8,128)S(1)}, u32[]{:S(2)}, u32[]{:S(2)}) collective-permute-start(f32[128,1024]{1,0:T(8,128)} %get-tuple-element.72), channel_id=1, source_target_pairs={{0,2},{2,0},{4,6},{6,4},{8,10},{10,8},{12,14},{14,12},{16,18},{18,... | collective-permute-start | bytes 1572872 | tf_op jit(solution)/shard_map/ppermute | solution.py:19
  93.6 30.2 %collective-permute-start.12 = (f32[128,1024]{1,0:T(8,128)}, f32[128,1024]{1,0:T(8,128)S(1)}, u32[]{:S(2)}, u32[]{:S(2)}) collective-permute-start(f32[128,1024]{1,0:T(8,128)} %get-tuple-element.76), channel_id=1, source_target_pairs={{0,4},{2,6},{4,8},{6,10},{8,12},{10,14},{12,16},{14,18},{16,20},{1... | collective-permute-start | bytes 1572872 | tf_op jit(solution)/shard_map/ppermute | solution.py:14
  93.6 30.2 %collective-permute-start.15 = (f32[128,1024]{1,0:T(8,128)}, f32[128,1024]{1,0:T(8,128)}, u32[]{:S(2)}, u32[]{:S(2)}) collective-permute-start(f32[128,1024]{1,0:T(8,128)} %get-tuple-element.77), channel_id=1, source_target_pairs={{0,252},{2,254},{4,0},{6,2},{8,4},{10,6},{12,8},{14,10},{16,12},{1... | collective-permute-start | bytes 1572872 | tf_op jit(solution)/shard_map/ppermute | solution.py:14
  101.4 23.9 %copy-start.4 = (bf16[1024,1152]{0,1:T(8,128)(2,1)S(1)}, bf16[1024,1152]{0,1:T(8,128)(2,1)}, u32[]{:S(2)}) copy-start(bf16[1024,1152]{0,1:T(8,128)(2,1)} %copy-done.3) | copy-start | bytes 7077892
  125.2 7.5 %collective-permute-start.16 = (f32[64,1024]{1,0:T(8,128)S(1)}, f32[64,1024]{1,0:T(8,128)S(1)}, u32[]{:S(2)}, u32[]{:S(2)}) collective-permute-start(f32[64,1024]{1,0:T(8,128)S(1)} %slice_select_fusion), channel_id=1, source_target_pairs={{0,1},{1,0},{2,3},{3,2},{4,5},{5,4},{6,7},{7,6},{8,9},{9,8},{10,11... | collective-permute-start | bytes 786440 | tf_op jit(solution)/shard_map/ppermute | solution.py:116

commit v3 on v2

--- a/solution.py
+++ b/solution.py
@@ -103,17 +103,32 @@
     far_down = key_parts["down4"] + jnp.where(core == 0, zero, back_far)
     near_up = key_parts["up2"] + back_up2 + passed_along(far_up, "dp", 2)
     near_down = key_parts["down2"] + back_down2 + passed_along(far_down, "dp", -2)
+    half = tile_rows // 2
+    mine_at = rep_index * half
+    other_at = (1 - rep_index) * half
+
+    def rows_at(x, start):
+        return lax.dynamic_slice_in_dim(x, start, half, 0)
+
+    own_part = key_parts["own"] + back_own
+    rep_count = lax.axis_size("rep")
+
+    def crossed(x, by):
+        pairs = []
+        for i in range(cycle_size):
+            for j in range(rep_count):
+                pairs.append((i * rep_count + j, ((i + by) % cycle_size) * rep_count + (1 - j)))
+        return lax.ppermute(x, ("dp", "rep"), pairs)
+
     total = (
-        key_parts["own"]
-        + back_own
-        + passed_along(near_up, "dp", 2)
-        + passed_along(near_down, "dp", -2)
+        rows_at(own_part, mine_at)
+        + lax.ppermute(rows_at(own_part, other_at), "rep", [(0, 1), (1, 0)])
+        + passed_along(rows_at(near_up, mine_at), "dp", 2)
+        + passed_along(rows_at(near_down, mine_at), "dp", -2)
+        + crossed(rows_at(near_up, other_at), 2)
+        + crossed(rows_at(near_down, other_at), -2)
     )
-    half = tile_rows // 2
-    halves = total.reshape(2, half, total.shape[1])
-    mine = jnp.where(rep_index == 0, halves[0], halves[1])
-    other = jnp.where(rep_index == 0, halves[1], halves[0])
-    grad_keys = logit_scale * (mine + lax.ppermute(other, "rep", [(0, 1), (1, 0)]))
+    grad_keys = logit_scale * total
     return (row_loss, grad_query, grad_keys)
 
 

time: 134 us -> 135 us (level)
  starting transfers between devices: 46.1 us -> 53.8 us
  waiting for transfers between devices: 48.1 us -> 44.8 us
  local copies, waits for them, and re-layouts: 10.5 us -> 8.05 us
  matrix products: 17.3 us -> 15.6 us
  other arithmetic: 10.6 us -> 12 us
    ppermute x1 -> x3, starting transfers between devices: 0.09 us -> 6.14 us  [the longest x2 5.69 us: crossed(): return lax.ppermute(x, ('dp', 'rep'), pairs)]
    ppermute x8, waiting for transfers between devices: 45.5 us -> 41.6 us  [passed_along(): return lax.ppermute(x, axis, [(i, (i + by) % count) for i in range(count)])]
    ppermute x8, waiting for transfers between devices: 1.41 us -> 3.18 us  [swapped(): return lax.ppermute(x, axis, [(i, i ^ 1) for i in range(count)])]
    dot_general x1, matrix products: 6.13 us -> 4.47 us  [body(): jnp.dot(coefficient, window, preferred_element_type=jnp.float32)]
    unnamed x17 -> x19, local copies, waits for them, and re-layouts: 7.5 us -> 6.04 us
  transfers between devices with their start and end apart: 17 -> 19, of which waited for: 6 -> 7; matrix products, arithmetic and copies ran while one was open for 19% -> 19% of each run, Pallas kernels for 0% -> 0%
where the time goes in v3:
time: 135 us
  starting transfers between devices  53.8 us (40%)
  waiting for transfers between devices  44.8 us (33%)
  matrix products  15.6 us (12%)
  other arithmetic  12 us (9%)
  local copies, waits for them, and re-layouts  8.05 us (6%)
    ppermute x8, waiting for transfers between devices, passed_along(): return lax.ppermute(x, axis, [(i, (i + by) % count) for i in range(count)])  41.6 us
    ppermute x8, starting transfers between devices, passed_along(): return lax.ppermute(x, axis, [(i, (i + by) % count) for i in range(count)])  36.7 us
    ppermute x8, starting transfers between devices, swapped(): return lax.ppermute(x, axis, [(i, i ^ 1) for i in range(count)])  11 us
    dot_general x9, matrix products, body(): lax.dot_general(queries, key_tile, (((1,), (1,)), ((), ())), preferred_el...  8.52 us
    unnamed x19, local copies, waits for them, and re-layouts  6.04 us
    ppermute x2, starting transfers between devices, crossed(): return lax.ppermute(x, ('dp', 'rep'), pairs)  5.69 us
    dot_general x1, matrix products, body(): jnp.dot(coefficient, window, preferred_element_type=jnp.float32)  4.47 us
    ppermute x8, waiting for transfers between devices, swapped(): return lax.ppermute(x, axis, [(i, i ^ 1) for i in range(count)])  3.18 us
  transfers between devices with their start and end apart: 19, of which 7 were waited for; matrix products, arithmetic and copies ran while one was open for 19% of the time, Pallas kernels for 0%

profile of v3, /device:TPU:1, one launch (start us, length us, event | category | flops | bytes accessed | tf_op | source)
XLA Modules:
  0.0 135.2 jit_solution(11746728559698541336)
XLA Ops:
  0.6 3.3 %collective-permute-start = (bf16[128,1024]{1,0:T(8,128)(2,1)}, bf16[128,1024]{1,0:T(8,128)(2,1)S(1)}, u32[]{:S(2)}, u32[]{:S(2)}) collective-permute-start(bf16[128,1024]{1,0:T(8,128)(2,1)} %param.6), channel_id=1, source_target_pairs={{0,2},{2,0},{4,6},{6,4},{8,10},{10,8},{12,14},{14,12},{16,18},{18,... | collective-permute-start | bytes 786440 | tf_op jit(solution)/shard_map/ppermute | solution.py:19
  3.9 1.3 collective-permute-start.1
  5.2 7.7 %collective-permute-start.2 = (bf16[128,1024]{1,0:T(8,128)(2,1)}, bf16[128,1024]{1,0:T(8,128)(2,1)S(1)}, u32[]{:S(2)}, u32[]{:S(2)}) collective-permute-start(bf16[128,1024]{1,0:T(8,128)(2,1)} %param.6), channel_id=1, source_target_pairs={{0,252},{2,254},{4,0},{6,2},{8,4},{10,6},{12,8},{14,10},{16,12},{1... | collective-permute-start | bytes 786440 | tf_op jit(solution)/shard_map/ppermute | solution.py:14
  12.9 1.7 %constant_dynamic-update-slice_fusion.8 = bf16[1152,1024]{1,0:T(8,128)(2,1)} fusion(bf16[128,1024]{1,0:T(8,128)(2,1)} %param.6), kind=kLoop, calls=%fused_computation.83 | loop fusion | bytes 524288
  14.6 1.3 fusion.20
  15.9 0.7 fusion.31
  16.7 0.1 broadcast_bitcast_fusion.16
  17.6 0.1 broadcast_bitcast_fusion.6
  17.8 1.8 %select_reduce_fusion.26 = (f32[1024]{0:T(1024)S(1)}, f32[1024,128]{0,1:T(8,128)S(1)}) fusion(pred[1024]{0:T(1024)(128)(4,1)S(1)} %broadcast_bitcast_fusion.17, bf16[1024,1024]{1,0:T(8,128)(2,1)S(1)} %copy-done, bf16[128,1024]{1,0:T(8,128)(2,1)} %param.6), kind=kOutput, calls=%fused_computation.62 | convolution fusion | flops 268827648 | bytes 2888704 | tf_op jit(solution)/shard_map/dot_general | solution.py:69
  19.6 2.1 %collective-permute-done.1 = bf16[128,1024]{1,0:T(8,128)(2,1)S(1)} collective-permute-done((bf16[128,1024]{1,0:T(8,128)(2,1)}, bf16[128,1024]{1,0:T(8,128)(2,1)S(1)}, u32[]{:S(2)}, u32[]{:S(2)}) %collective-permute-start.1) | collective-permute-done | bytes 262176 | tf_op jit(solution)/shard_map/ppermute | solution.py:14
  21.7 0.7 collective-permute-start.3
  22.4 3.0 %collective-permute-start.4 = (bf16[128,1024]{1,0:T(8,128)(2,1)S(1)}, bf16[128,1024]{1,0:T(8,128)(2,1)S(1)}, u32[]{:S(2)}, u32[]{:S(2)}) collective-permute-start(bf16[128,1024]{1,0:T(8,128)(2,1)S(1)} %collective-permute-done.2), channel_id=1, source_target_pairs={{0,2},{2,0},{4,6},{6,4},{8,10},{10,8},{12,14},{14,12},{16,18},{18,... | collective-permute-start | bytes 786440 | tf_op jit(solution)/shard_map/ppermute | solution.py:19
  25.4 8.5 %collective-permute-start.6 = (bf16[128,1024]{1,0:T(8,128)(2,1)S(1)}, bf16[128,1024]{1,0:T(8,128)(2,1)S(1)}, u32[]{:S(2)}, u32[]{:S(2)}) collective-permute-start(bf16[128,1024]{1,0:T(8,128)(2,1)S(1)} %collective-permute-done.2), channel_id=1, source_target_pairs={{0,252},{2,254},{4,0},{6,2},{8,4},{10,6},{12,8},{14,10},{16,12},{1... | collective-permute-start | bytes 786440 | tf_op jit(solution)/shard_map/ppermute | solution.py:14
  33.9 0.8 select_reduce_fusion.23
  34.7 0.8 select_reduce_fusion.24
  35.6 0.8 select_reduce_fusion.25
  36.4 0.7 constant_dynamic-update-slice_fusion.7
  37.2 0.7 constant_dynamic-update-slice_fusion.6
  37.9 0.7 constant_dynamic-update-slice_fusion.5
  38.6 0.7 constant_dynamic-update-slice_fusion.4
  39.3 0.7 constant_dynamic-update-slice_fusion.3
  40.0 2.0 %collective-permute-done.5 = bf16[128,1024]{1,0:T(8,128)(2,1)S(1)} collective-permute-done((bf16[128,1024]{1,0:T(8,128)(2,1)S(1)}, bf16[128,1024]{1,0:T(8,128)(2,1)S(1)}, u32[]{:S(2)}, u32[]{:S(2)}) %collective-permute-start.5) | collective-permute-done | bytes 262176 | tf_op jit(solution)/shard_map/ppermute | solution.py:14
  42.0 0.7 constant_dynamic-update-slice_fusion.2
  42.8 0.8 constant_dynamic-update-slice_fusion.1
  43.5 3.3 %collective-permute-start.7 = (bf16[128,1024]{1,0:T(8,128)(2,1)S(1)}, bf16[128,1024]{1,0:T(8,128)(2,1)S(1)}, u32[]{:S(2)}, u32[]{:S(2)}) collective-permute-start(bf16[128,1024]{1,0:T(8,128)(2,1)S(1)} %get-tuple-element.83), channel_id=1, source_target_pairs={{0,2},{2,0},{4,6},{6,4},{8,10},{10,8},{12,14},{14,12},{16,18},{18,... | collective-permute-start | bytes 786440 | tf_op jit(solution)/shard_map/ppermute | solution.py:19
  46.8 0.8 select_reduce_fusion.19
  47.7 0.8 select_reduce_fusion.20
  48.5 0.8 select_reduce_fusion.21
  49.4 0.8 select_reduce_fusion.22
  50.2 0.8 select_reduce_fusion.18
  51.2 0.2 select_reduce_fusion.6
  51.4 0.8 select_reduce_fusion.7
  52.2 0.8 select_reduce_fusion.8
  53.0 0.6 add_subtract_fusion
  53.6 0.2 fusion.3
  53.8 0.2 fusion.4
  54.0 0.2 fusion.5
  54.2 0.2 fusion.6
  54.4 0.2 fusion.7
  54.6 0.2 fusion.8
  54.8 0.2 fusion.9
  55.0 0.2 fusion.10
  55.2 0.2 fusion.11
  55.4 2.6 %fusion.33 = f32[1152,1024]{1,0:T(8,128)S(1)} fusion(bf16[1024,1152]{0,1:T(8,128)(2,1)S(1)} %fusion.11, bf16[1024,1024]{1,0:T(8,128)(2,1)S(1)} %copy-done), kind=kOutput, calls=%fused_computation.148 | convolution fusion | flops 2415919104 | bytes 9175040 | tf_op jit(solution)/shard_map/dot_general | solution.py:91
  58.1 0.1 collective-permute-start.8
  58.2 1.9 %collective-permute-done.8 = f32[128,1024]{1,0:T(8,128)S(1)} collective-permute-done((f32[128,1024]{1,0:T(8,128)S(1)}, f32[128,1024]{1,0:T(8,128)S(1)}, u32[]{:S(2)}, u32[]{:S(2)}) %collective-permute-start.8) | collective-permute-done | bytes 524320 | tf_op jit(solution)/shard_map/ppermute | solution.py:19
  60.0 1.0 slice_add_fusion.4
  61.1 0.1 collective-permute-start.11
  61.2 0.4 collective-permute-start.10
  61.6 0.1 collective-permute-start.14
  61.7 1.3 collective-permute-done.11
  63.0 1.1 slice_add_fusion.2
  64.1 8.5 %collective-permute-start.15 = (f32[128,1024]{1,0:T(8,128)}, f32[128,1024]{1,0:T(8,128)}, u32[]{:S(2)}, u32[]{:S(2)}) collective-permute-start(f32[128,1024]{1,0:T(8,128)} %get-tuple-element.71), channel_id=1, source_target_pairs={{0,252},{2,254},{4,0},{6,2},{8,4},{10,6},{12,8},{14,10},{16,12},{1... | collective-permute-start | bytes 1572872 | tf_op jit(solution)/shard_map/ppermute | solution.py:14
  72.6 0.7 constant_dynamic-update-slice_fusion
  73.3 0.4 collective-permute-start.9
  73.8 22.5 %collective-permute-done.12 = f32[128,1024]{1,0:T(8,128)} collective-permute-done((f32[128,1024]{1,0:T(8,128)}, f32[128,1024]{1,0:T(8,128)}, u32[]{:S(2)}, u32[]{:S(2)}) %collective-permute-start.12) | collective-permute-done | bytes 524320 | tf_op jit(solution)/shard_map/ppermute | solution.py:14
  96.3 2.1 %fusion.2 = (f32[128,1024]{1,0:T(8,128)S(1)}, f32[128,1024]{1,0:T(8,128)S(1)}) fusion(f32[128,1024]{1,0:T(8,128)} %collective-permute-done.12, f32[128,1024]{1,0:T(8,128)} %collective-permute-done.10, f32[1152,1024]{1,0:T(8,128)} %copy-done.1, f32[128,1024]{1,0:T(8,128)} %collective-permute-done.15, f32[128,1024]{1,0:T(8,128)} %collective-permute-done.14), kind=kLoop, calls=%fused_computation.16 | loop fusion | flops 524288 | bytes 4194304 | tf_op jit(solution)/shard_map/add | solution.py:104
  98.5 5.6 %collective-permute-start.18 = (f32[64,1024]{1,0:T(8,128)S(1)}, f32[64,1024]{1,0:T(8,128)S(1)}, u32[]{:S(2)}, u32[]{:S(2)}) collective-permute-start(f32[64,1024]{1,0:T(8,128)S(1)} %get-tuple-element.81), channel_id=1, source_target_pairs={{0,253},{1,252},{2,255},{3,254},{4,1},{5,0},{6,3},{7,2},{8,5},{9,4... | collective-permute-start | bytes 786440 | tf_op jit(solution)/shard_map/ppermute | solution.py:121
  104.1 0.1 collective-permute-start.17
  104.2 10.7 %collective-permute-start.16 = (f32[64,1024]{1,0:T(8,128)S(1)}, f32[64,1024]{1,0:T(8,128)S(1)}, u32[]{:S(2)}, u32[]{:S(2)}) collective-permute-start(f32[64,1024]{1,0:T(8,128)S(1)} %get-tuple-element.80), channel_id=1, source_target_pairs={{0,252},{2,254},{4,0},{6,2},{8,4},{10,6},{12,8},{14,10},{16,12},{1... | collective-permute-start | bytes 786440 | tf_op jit(solution)/shard_map/ppermute | solution.py:14
  115.0 4.5 %convolution_multiply_fusion = f32[1024,1024]{1,0:T(8,128)} fusion(bf16[1024,1152]{0,1:T(8,128)(2,1)S(1)} %copy-done.4, bf16[1152,1024]{1,0:T(8,128)(2,1)S(1)} %copy-done.5), kind=kOutput, calls=%fused_computation | convolution fusion | flops 2416967680 | bytes 8912896 | tf_op jit(solution)/shard_map/dot_general | solution.py:90
  119.4 9.8 %collective-permute-done.16 = f32[64,1024]{1,0:T(8,128)S(1)} collective-permute-done((f32[64,1024]{1,0:T(8,128)S(1)}, f32[64,1024]{1,0:T(8,128)S(1)}, u32[]{:S(2)}, u32[]{:S(2)}) %collective-permute-start.16) | collective-permute-done | bytes 262176 | tf_op jit(solution)/shard_map/ppermute | solution.py:14
  129.2 5.2 %collective-permute-done.13 = f32[64,1024]{1,0:T(8,128)S(1)} collective-permute-done((f32[64,1024]{1,0:T(8,128)S(1)}, f32[64,1024]{1,0:T(8,128)S(1)}, u32[]{:S(2)}, u32[]{:S(2)}) %collective-permute-start.13) | collective-permute-done | bytes 262176 | tf_op jit(solution)/shard_map/ppermute | solution.py:14
  134.4 0.8 add_multiply_fusion
  (47 shorter events, 1.2 us)
Async XLA Ops:
  0.6 17.1 %copy-start = (bf16[1024,1024]{1,0:T(8,128)(2,1)S(1)}, bf16[1024,1024]{1,0:T(8,128)(2,1)}, u32[]{:S(2)}) copy-start(bf16[1024,1024]{1,0:T(8,128)(2,1)} %param.5) | copy-start | bytes 6291460
  0.6 34.9 %collective-permute-start = (bf16[128,1024]{1,0:T(8,128)(2,1)}, bf16[128,1024]{1,0:T(8,128)(2,1)S(1)}, u32[]{:S(2)}, u32[]{:S(2)}) collective-permute-start(bf16[128,1024]{1,0:T(8,128)(2,1)} %param.6), channel_id=1, source_target_pairs={{0,2},{2,0},{4,6},{6,4},{8,10},{10,8},{12,14},{14,12},{16,18},{18,... | collective-permute-start | bytes 786440 | tf_op jit(solution)/shard_map/ppermute | solution.py:19
  3.9 17.8 %collective-permute-start.1 = (bf16[128,1024]{1,0:T(8,128)(2,1)}, bf16[128,1024]{1,0:T(8,128)(2,1)S(1)}, u32[]{:S(2)}, u32[]{:S(2)}) collective-permute-start(bf16[128,1024]{1,0:T(8,128)(2,1)} %param.6), channel_id=1, source_target_pairs={{0,4},{2,6},{4,8},{6,10},{8,12},{10,14},{12,16},{14,18},{16,20},{1... | collective-permute-start | bytes 786440 | tf_op jit(solution)/shard_map/ppermute | solution.py:14
  5.2 17.2 %collective-permute-start.2 = (bf16[128,1024]{1,0:T(8,128)(2,1)}, bf16[128,1024]{1,0:T(8,128)(2,1)S(1)}, u32[]{:S(2)}, u32[]{:S(2)}) collective-permute-start(bf16[128,1024]{1,0:T(8,128)(2,1)} %param.6), channel_id=1, source_target_pairs={{0,252},{2,254},{4,0},{6,2},{8,4},{10,6},{12,8},{14,10},{16,12},{1... | collective-permute-start | bytes 786440 | tf_op jit(solution)/shard_map/ppermute | solution.py:14
  21.7 16.9 %collective-permute-start.3 = (bf16[128,1024]{1,0:T(8,128)(2,1)S(1)}, bf16[128,1024]{1,0:T(8,128)(2,1)S(1)}, u32[]{:S(2)}, u32[]{:S(2)}) collective-permute-start(bf16[128,1024]{1,0:T(8,128)(2,1)S(1)} %collective-permute-done.1), channel_id=1, source_target_pairs={{0,2},{2,0},{4,6},{6,4},{8,10},{10,8},{12,14},{14,12},{16,18},{18,... | collective-permute-start | bytes 786440 | tf_op jit(solution)/shard_map/ppermute | solution.py:19
  22.4 19.6 %collective-permute-start.5 = (bf16[128,1024]{1,0:T(8,128)(2,1)S(1)}, bf16[128,1024]{1,0:T(8,128)(2,1)S(1)}, u32[]{:S(2)}, u32[]{:S(2)}) collective-permute-start(bf16[128,1024]{1,0:T(8,128)(2,1)S(1)} %collective-permute-done.1), channel_id=1, source_target_pairs={{0,4},{2,6},{4,8},{6,10},{8,12},{10,14},{12,16},{14,18},{16,20},{1... | collective-permute-start | bytes 786440 | tf_op jit(solution)/shard_map/ppermute | solution.py:14
  22.4 16.9 %collective-permute-start.4 = (bf16[128,1024]{1,0:T(8,128)(2,1)S(1)}, bf16[128,1024]{1,0:T(8,128)(2,1)S(1)}, u32[]{:S(2)}, u32[]{:S(2)}) collective-permute-start(bf16[128,1024]{1,0:T(8,128)(2,1)S(1)} %collective-permute-done.2), channel_id=1, source_target_pairs={{0,2},{2,0},{4,6},{6,4},{8,10},{10,8},{12,14},{14,12},{16,18},{18,... | collective-permute-start | bytes 786440 | tf_op jit(solution)/shard_map/ppermute | solution.py:19
  25.4 17.4 %collective-permute-start.6 = (bf16[128,1024]{1,0:T(8,128)(2,1)S(1)}, bf16[128,1024]{1,0:T(8,128)(2,1)S(1)}, u32[]{:S(2)}, u32[]{:S(2)}) collective-permute-start(bf16[128,1024]{1,0:T(8,128)(2,1)S(1)} %collective-permute-done.2), channel_id=1, source_target_pairs={{0,252},{2,254},{4,0},{6,2},{8,4},{10,6},{12,8},{14,10},{16,12},{1... | collective-permute-start | bytes 786440 | tf_op jit(solution)/shard_map/ppermute | solution.py:14
  43.5 6.7 %collective-permute-start.7 = (bf16[128,1024]{1,0:T(8,128)(2,1)S(1)}, bf16[128,1024]{1,0:T(8,128)(2,1)S(1)}, u32[]{:S(2)}, u32[]{:S(2)}) collective-permute-start(bf16[128,1024]{1,0:T(8,128)(2,1)S(1)} %get-tuple-element.83), channel_id=1, source_target_pairs={{0,2},{2,0},{4,6},{6,4},{8,10},{10,8},{12,14},{14,12},{16,18},{18,... | collective-permute-start | bytes 786440 | tf_op jit(solution)/shard_map/ppermute | solution.py:19
  51.4 2.3 %copy-start.2 = (f32[1024]{0:T(1024)S(1)}, f32[1024]{0:T(1024)}, u32[]{:S(2)}) copy-start(f32[1024]{0:T(1024)} %param.9) | copy-start | bytes 12292
  55.4 2.6 %copy-start.3 = (bf16[1024,1152]{0,1:T(8,128)(2,1)}, bf16[1024,1152]{0,1:T(8,128)(2,1)S(1)}, u32[]{:S(2)}) copy-start(bf16[1024,1152]{0,1:T(8,128)(2,1)S(1)} %fusion.11) | copy-start | bytes 7077892
  58.0 5.0 %copy-start.1 = (f32[1152,1024]{1,0:T(8,128)}, f32[1152,1024]{1,0:T(8,128)S(1)}, u32[]{:S(2)}) copy-start(f32[1152,1024]{1,0:T(8,128)S(1)} %fusion.33) | copy-start | bytes 14155780
  58.1 2.0 %collective-permute-start.8 = (f32[128,1024]{1,0:T(8,128)S(1)}, f32[128,1024]{1,0:T(8,128)S(1)}, u32[]{:S(2)}, u32[]{:S(2)}) collective-permute-start(f32[128,1024]{1,0:T(8,128)S(1)} %slice.37), channel_id=1, source_target_pairs={{0,2},{2,0},{4,6},{6,4},{8,10},{10,8},{12,14},{14,12},{16,18},{18,... | collective-permute-start | bytes 1572872 | tf_op jit(solution)/shard_map/ppermute | solution.py:19
  61.1 1.9 %collective-permute-start.11 = (f32[128,1024]{1,0:T(8,128)S(1)}, f32[128,1024]{1,0:T(8,128)S(1)}, u32[]{:S(2)}, u32[]{:S(2)}) collective-permute-start(f32[128,1024]{1,0:T(8,128)S(1)} %get-tuple-element.74), channel_id=1, source_target_pairs={{0,2},{2,0},{4,6},{6,4},{8,10},{10,8},{12,14},{14,12},{16,18},{18,... | collective-permute-start | bytes 1572872 | tf_op jit(solution)/shard_map/ppermute | solution.py:19
  61.2 12.6 %collective-permute-start.10 = (f32[128,1024]{1,0:T(8,128)}, f32[128,1024]{1,0:T(8,128)}, u32[]{:S(2)}, u32[]{:S(2)}) collective-permute-start(f32[128,1024]{1,0:T(8,128)} %get-tuple-element.75), channel_id=1, source_target_pairs={{0,2},{2,0},{4,6},{6,4},{8,10},{10,8},{12,14},{14,12},{16,18},{18,... | collective-permute-start | bytes 1572872 | tf_op jit(solution)/shard_map/ppermute | solution.py:19
  61.6 12.2 %collective-permute-start.14 = (f32[128,1024]{1,0:T(8,128)S(1)}, f32[128,1024]{1,0:T(8,128)}, u32[]{:S(2)}, u32[]{:S(2)}) collective-permute-start(f32[128,1024]{1,0:T(8,128)S(1)} %get-tuple-element.73), channel_id=1, source_target_pairs={{0,2},{2,0},{4,6},{6,4},{8,10},{10,8},{12,14},{14,12},{16,18},{18,... | collective-permute-start | bytes 1572872 | tf_op jit(solution)/shard_map/ppermute | solution.py:19
  64.1 32.3 %collective-permute-start.12 = (f32[128,1024]{1,0:T(8,128)}, f32[128,1024]{1,0:T(8,128)}, u32[]{:S(2)}, u32[]{:S(2)}) collective-permute-start(f32[128,1024]{1,0:T(8,128)} %get-tuple-element.70), channel_id=1, source_target_pairs={{0,4},{2,6},{4,8},{6,10},{8,12},{10,14},{12,16},{14,18},{16,20},{1... | collective-permute-start | bytes 1572872 | tf_op jit(solution)/shard_map/ppermute | solution.py:14
  64.1 32.3 %collective-permute-start.15 = (f32[128,1024]{1,0:T(8,128)}, f32[128,1024]{1,0:T(8,128)}, u32[]{:S(2)}, u32[]{:S(2)}) collective-permute-start(f32[128,1024]{1,0:T(8,128)} %get-tuple-element.71), channel_id=1, source_target_pairs={{0,252},{2,254},{4,0},{6,2},{8,4},{10,6},{12,8},{14,10},{16,12},{1... | collective-permute-start | bytes 1572872 | tf_op jit(solution)/shard_map/ppermute | solution.py:14
  73.3 41.6 %copy-start.4 = (bf16[1024,1152]{0,1:T(8,128)(2,1)S(1)}, bf16[1024,1152]{0,1:T(8,128)(2,1)}, u32[]{:S(2)}) copy-start(bf16[1024,1152]{0,1:T(8,128)(2,1)} %copy-done.3) | copy-start | bytes 7077892
  73.3 41.6 %copy-start.5 = (bf16[1152,1024]{1,0:T(8,128)(2,1)S(1)}, bf16[1152,1024]{1,0:T(8,128)(2,1)}, u32[]{:S(2)}) copy-start(bf16[1152,1024]{1,0:T(8,128)(2,1)} %constant_dynamic-update-slice_fusion) | copy-start | bytes 7077892
  73.3 46.1 %collective-permute-start.9 = (f32[64,1024]{1,0:T(8,128)S(1)}, f32[64,1024]{1,0:T(8,128)S(1)}, u32[]{:S(2)}, u32[]{:S(2)}) collective-permute-start(f32[64,1024]{1,0:T(8,128)S(1)} %constant_dynamic-slice_fusion.4), channel_id=1, source_target_pairs={{0,1},{1,0},{2,3},{3,2},{4,5},{5,4},{6,7},{7,6},{8,9},{9,8},{10,11... | collective-permute-start | bytes 786440 | tf_op jit(solution)/shard_map/ppermute | solution.py:125
  98.5 20.9 %collective-permute-start.18 = (f32[64,1024]{1,0:T(8,128)S(1)}, f32[64,1024]{1,0:T(8,128)S(1)}, u32[]{:S(2)}, u32[]{:S(2)}) collective-permute-start(f32[64,1024]{1,0:T(8,128)S(1)} %get-tuple-element.81), channel_id=1, source_target_pairs={{0,253},{1,252},{2,255},{3,254},{4,1},{5,0},{6,3},{7,2},{8,5},{9,4... | collective-permute-start | bytes 786440 | tf_op jit(solution)/shard_map/ppermute | solution.py:121
  104.1 15.3 %collective-permute-start.17 = (f32[64,1024]{1,0:T(8,128)S(1)}, f32[64,1024]{1,0:T(8,128)S(1)}, u32[]{:S(2)}, u32[]{:S(2)}) collective-permute-start(f32[64,1024]{1,0:T(8,128)S(1)} %get-tuple-element.79), channel_id=1, source_target_pairs={{0,5},{1,4},{2,7},{3,6},{4,9},{5,8},{6,11},{7,10},{8,13},{9,12},{1... | collective-permute-start | bytes 786440 | tf_op jit(solution)/shard_map/ppermute | solution.py:121
  104.2 25.0 %collective-permute-start.16 = (f32[64,1024]{1,0:T(8,128)S(1)}, f32[64,1024]{1,0:T(8,128)S(1)}, u32[]{:S(2)}, u32[]{:S(2)}) collective-permute-start(f32[64,1024]{1,0:T(8,128)S(1)} %get-tuple-element.80), channel_id=1, source_target_pairs={{0,252},{2,254},{4,0},{6,2},{8,4},{10,6},{12,8},{14,10},{16,12},{1... | collective-permute-start | bytes 786440 | tf_op jit(solution)/shard_map/ppermute | solution.py:14
  114.9 19.5 %collective-permute-start.13 = (f32[64,1024]{1,0:T(8,128)S(1)}, f32[64,1024]{1,0:T(8,128)S(1)}, u32[]{:S(2)}, u32[]{:S(2)}) collective-permute-start(f32[64,1024]{1,0:T(8,128)S(1)} %get-tuple-element.78), channel_id=1, source_target_pairs={{0,4},{2,6},{4,8},{6,10},{8,12},{10,14},{12,16},{14,18},{16,20},{1... | collective-permute-start | bytes 786440 | tf_op jit(solution)/shard_map/ppermute | solution.py:14

commit v4 on v2

--- a/solution.py
+++ b/solution.py
@@ -103,6 +103,7 @@
     far_down = key_parts["down4"] + jnp.where(core == 0, zero, back_far)
     near_up = key_parts["up2"] + back_up2 + passed_along(far_up, "dp", 2)
     near_down = key_parts["down2"] + back_down2 + passed_along(far_down, "dp", -2)
+    near_up, near_down, grad_query = lax.optimization_barrier((near_up, near_down, grad_query))
     total = (
         key_parts["own"]
         + back_own

time: 134 us -> 136 us (1.015)
  local copies, waits for them, and re-layouts: 10.5 us -> 3.04 us
  waiting for transfers between devices: 48.1 us -> 54.6 us
  starting transfers between devices: 46.1 us -> 50.7 us
  matrix products: 17.3 us -> 15.6 us
    ppermute x1, waiting for transfers between devices: 1.22 us -> 7.26 us  [body(): lax.ppermute(other, 'rep', [(0, 1), (1, 0)])]
    unnamed x17 -> x15, local copies, waits for them, and re-layouts: 7.5 us -> 1.83 us
    ppermute x8, starting transfers between devices: 10.1 us -> 14.8 us  [swapped(): return lax.ppermute(x, axis, [(i, i ^ 1) for i in range(count)])]
    dot_general x1, matrix products: 6.13 us -> 4.45 us  [body(): jnp.dot(coefficient, window, preferred_element_type=jnp.float32)]
  transfers between devices with their start and end apart: 17 -> 17, of which waited for: 6 -> 7; matrix products, arithmetic and copies ran while one was open for 19% -> 14% of each run, Pallas kernels for 0% -> 0%
where the time goes in v4:
time: 136 us
  waiting for transfers between devices  54.6 us (40%)
  starting transfers between devices  50.7 us (37%)
  matrix products  15.6 us (11%)
  other arithmetic  10.7 us (8%)
  local copies, waits for them, and re-layouts  3.04 us (2%)
    ppermute x8, waiting for transfers between devices, passed_along(): return lax.ppermute(x, axis, [(i, (i + by) % count) for i in range(count)])  45.4 us
    ppermute x8, starting transfers between devices, passed_along(): return lax.ppermute(x, axis, [(i, (i + by) % count) for i in range(count)])  35.9 us
    ppermute x8, starting transfers between devices, swapped(): return lax.ppermute(x, axis, [(i, i ^ 1) for i in range(count)])  14.8 us
    dot_general x9, matrix products, body(): lax.dot_general(queries, key_tile, (((1,), (1,)), ((), ())), preferred_el...  8.53 us
    ppermute x1, waiting for transfers between devices, body(): lax.ppermute(other, 'rep', [(0, 1), (1, 0)])  7.26 us
    dot_general x1, matrix products, body(): jnp.dot(coefficient, window, preferred_element_type=jnp.float32)  4.45 us
  transfers between devices with their start and end apart: 17, of which 7 were waited for; matrix products, arithmetic and copies ran while one was open for 14% of the time, Pallas kernels for 0%

profile of v4, /device:TPU:1, one launch (start us, length us, event | category | flops | bytes accessed | tf_op | source)
XLA Modules:
  0.0 135.6 jit_solution(15995402012241928699)
XLA Ops:
  0.6 3.9 %collective-permute-start.1 = (bf16[128,1024]{1,0:T(8,128)(2,1)}, bf16[128,1024]{1,0:T(8,128)(2,1)S(1)}, u32[]{:S(2)}, u32[]{:S(2)}) collective-permute-start(bf16[128,1024]{1,0:T(8,128)(2,1)} %param.6), channel_id=1, source_target_pairs={{0,4},{2,6},{4,8},{6,10},{8,12},{10,14},{12,16},{14,18},{16,20},{1... | collective-permute-start | bytes 786440 | tf_op jit(solution)/shard_map/ppermute | solution.py:14
  4.5 1.0 collective-permute-start
  5.5 7.5 %collective-permute-start.2 = (bf16[128,1024]{1,0:T(8,128)(2,1)}, bf16[128,1024]{1,0:T(8,128)(2,1)S(1)}, u32[]{:S(2)}, u32[]{:S(2)}) collective-permute-start(bf16[128,1024]{1,0:T(8,128)(2,1)} %param.6), channel_id=1, source_target_pairs={{0,252},{2,254},{4,0},{6,2},{8,4},{10,6},{12,8},{14,10},{16,12},{1... | collective-permute-start | bytes 786440 | tf_op jit(solution)/shard_map/ppermute | solution.py:14
  13.0 1.7 %constant_dynamic-update-slice_fusion.8 = bf16[1152,1024]{1,0:T(8,128)(2,1)} fusion(bf16[128,1024]{1,0:T(8,128)(2,1)} %param.6), kind=kLoop, calls=%fused_computation.86 | loop fusion | bytes 524288
  14.7 1.3 fusion.22
  16.0 0.7 fusion.33
  16.8 0.1 broadcast_bitcast_fusion.17
  16.8 0.1 broadcast_bitcast_fusion.11
  17.0 0.1 broadcast_bitcast_fusion.13
  17.1 0.1 broadcast_bitcast_fusion.14
  17.1 0.1 broadcast_bitcast_fusion.16
  17.2 0.1 broadcast_bitcast_fusion.9
  17.3 0.1 broadcast_bitcast_fusion.10
  17.6 0.1 broadcast_bitcast_fusion.4
  17.7 0.1 broadcast_bitcast_fusion.6
  17.8 0.1 broadcast_bitcast_fusion
  17.9 1.8 %select_reduce_fusion.26 = (f32[1024]{0:T(1024)S(1)}, f32[1024,128]{0,1:T(8,128)S(1)}) fusion(pred[1024]{0:T(1024)(128)(4,1)S(1)} %broadcast_bitcast_fusion.17, bf16[1024,1024]{1,0:T(8,128)(2,1)S(1)} %copy-done, bf16[128,1024]{1,0:T(8,128)(2,1)} %param.6), kind=kOutput, calls=%fused_computation.64 | convolution fusion | flops 268827648 | bytes 2888704 | tf_op jit(solution)/shard_map/dot_general | solution.py:69
  19.7 0.3 collective-permute-done.1
  20.0 0.2 collective-permute-start.5
  20.1 1.5 %collective-permute-start.3 = (bf16[128,1024]{1,0:T(8,128)(2,1)S(1)}, bf16[128,1024]{1,0:T(8,128)(2,1)S(1)}, u32[]{:S(2)}, u32[]{:S(2)}) collective-permute-start(bf16[128,1024]{1,0:T(8,128)(2,1)S(1)} %collective-permute-done.1), channel_id=1, source_target_pairs={{0,2},{2,0},{4,6},{6,4},{8,10},{10,8},{12,14},{14,12},{16,18},{18,... | collective-permute-start | bytes 786440 | tf_op jit(solution)/shard_map/ppermute | solution.py:19
  21.7 0.5 collective-permute-done.2
  22.2 7.9 %collective-permute-start.6 = (bf16[128,1024]{1,0:T(8,128)(2,1)S(1)}, bf16[128,1024]{1,0:T(8,128)(2,1)S(1)}, u32[]{:S(2)}, u32[]{:S(2)}) collective-permute-start(bf16[128,1024]{1,0:T(8,128)(2,1)S(1)} %collective-permute-done.2), channel_id=1, source_target_pairs={{0,252},{2,254},{4,0},{6,2},{8,4},{10,6},{12,8},{14,10},{16,12},{1... | collective-permute-start | bytes 786440 | tf_op jit(solution)/shard_map/ppermute | solution.py:14
  30.1 4.2 %collective-permute-start.4 = (bf16[128,1024]{1,0:T(8,128)(2,1)S(1)}, bf16[128,1024]{1,0:T(8,128)(2,1)S(1)}, u32[]{:S(2)}, u32[]{:S(2)}) collective-permute-start(bf16[128,1024]{1,0:T(8,128)(2,1)S(1)} %collective-permute-done.2), channel_id=1, source_target_pairs={{0,2},{2,0},{4,6},{6,4},{8,10},{10,8},{12,14},{14,12},{16,18},{18,... | collective-permute-start | bytes 786440 | tf_op jit(solution)/shard_map/ppermute | solution.py:19
  34.2 0.8 select_reduce_fusion.23
  35.1 0.8 select_reduce_fusion.24
  36.0 0.8 select_reduce_fusion.25
  37.1 7.0 %collective-permute-start.7 = (bf16[128,1024]{1,0:T(8,128)(2,1)S(1)}, bf16[128,1024]{1,0:T(8,128)(2,1)S(1)}, u32[]{:S(2)}, u32[]{:S(2)}) collective-permute-start(bf16[128,1024]{1,0:T(8,128)(2,1)S(1)} %get-tuple-element.83), channel_id=1, source_target_pairs={{0,2},{2,0},{4,6},{6,4},{8,10},{10,8},{12,14},{14,12},{16,18},{18,... | collective-permute-start | bytes 786440 | tf_op jit(solution)/shard_map/ppermute | solution.py:19
  44.1 0.8 select_reduce_fusion.21
  44.9 0.8 select_reduce_fusion.19
  45.8 0.8 select_reduce_fusion.22
  46.6 0.8 select_reduce_fusion.20
  47.5 0.8 select_reduce_fusion.18
  48.4 0.2 select_reduce_fusion.6
  48.7 0.8 select_reduce_fusion.8
  49.5 0.8 select_reduce_fusion.7
  50.3 0.6 add_subtract_fusion
  50.9 0.2 fusion.5
  51.1 0.2 fusion.6
  51.3 0.2 fusion.7
  51.5 0.2 fusion.8
  51.7 0.2 fusion.9
  51.8 0.2 fusion.10
  52.0 0.2 fusion.11
  52.2 0.2 fusion.12
  52.4 0.2 fusion.13
  52.6 2.6 %fusion.35 = f32[1152,1024]{1,0:T(8,128)S(1)} fusion(bf16[1024,1152]{0,1:T(8,128)(2,1)S(1)} %fusion.13, bf16[1024,1024]{1,0:T(8,128)(2,1)S(1)} %copy-done), kind=kOutput, calls=%fused_computation.146 | convolution fusion | flops 2415919104 | bytes 9175040 | tf_op jit(solution)/shard_map/dot_general | solution.py:91
  55.3 0.1 collective-permute-start.9
  55.4 1.9 %collective-permute-done.9 = f32[128,1024]{1,0:T(8,128)S(1)} collective-permute-done((f32[128,1024]{1,0:T(8,128)S(1)}, f32[128,1024]{1,0:T(8,128)S(1)}, u32[]{:S(2)}, u32[]{:S(2)}) %collective-permute-start.9) | collective-permute-done | bytes 524320 | tf_op jit(solution)/shard_map/ppermute | solution.py:19
  57.3 0.2 slice_add_fusion.1
  57.5 8.6 %collective-permute-start.12 = (f32[128,1024]{1,0:T(8,128)S(1)}, f32[128,1024]{1,0:T(8,128)S(1)}, u32[]{:S(2)}, u32[]{:S(2)}) collective-permute-start(f32[128,1024]{1,0:T(8,128)S(1)} %get-tuple-element.76), channel_id=1, source_target_pairs={{0,252},{2,254},{4,0},{6,2},{8,4},{10,6},{12,8},{14,10},{16,12},{1... | collective-permute-start | bytes 1572872 | tf_op jit(solution)/shard_map/ppermute | solution.py:14
  66.1 0.4 collective-permute-start.11
  66.5 0.1 collective-permute-start.10
  66.6 21.3 %collective-permute-done.12 = f32[128,1024]{1,0:T(8,128)S(1)} collective-permute-done((f32[128,1024]{1,0:T(8,128)S(1)}, f32[128,1024]{1,0:T(8,128)S(1)}, u32[]{:S(2)}, u32[]{:S(2)}) %collective-permute-start.12) | collective-permute-done | bytes 524320 | tf_op jit(solution)/shard_map/ppermute | solution.py:14
  87.9 1.0 fusion.3
  88.9 0.6 collective-permute-start.8
  89.5 4.4 %convolution_multiply_fusion = f32[1024,1024]{1,0:T(8,128)} fusion(bf16[1024,1152]{0,1:T(8,128)(2,1)S(1)} %fusion.13, bf16[1152,1024]{1,0:T(8,128)(2,1)S(1)} %constant_dynamic-update-slice_fusion), kind=kOutput, calls=%fused_computation | convolution fusion | flops 2416967680 | bytes 8912896 | tf_op jit(solution)/shard_map/dot_general | solution.py:90
  94.0 1.7 %collective-permute-done.10 = f32[128,1024]{1,0:T(8,128)S(1)} collective-permute-done((f32[128,1024]{1,0:T(8,128)S(1)}, f32[128,1024]{1,0:T(8,128)S(1)}, u32[]{:S(2)}, u32[]{:S(2)}) %collective-permute-start.10) | collective-permute-done | bytes 524320 | tf_op jit(solution)/shard_map/ppermute | solution.py:14
  95.7 0.9 fusion.4
  96.6 7.8 %collective-permute-start.15 = (f32[128,1024]{1,0:T(8,128)}, f32[128,1024]{1,0:T(8,128)}, u32[]{:S(2)}, u32[]{:S(2)}) collective-permute-start(f32[128,1024]{1,0:T(8,128)} %get-tuple-element.8), channel_id=1, source_target_pairs={{0,252},{2,254},{4,0},{6,2},{8,4},{10,6},{12,8},{14,10},{16,12},{1... | collective-permute-start | bytes 1572872 | tf_op jit(solution)/shard_map/ppermute | solution.py:14
  104.4 21.6 %collective-permute-done.14 = f32[128,1024]{1,0:T(8,128)} collective-permute-done((f32[128,1024]{1,0:T(8,128)}, f32[128,1024]{1,0:T(8,128)}, u32[]{:S(2)}, u32[]{:S(2)}) %collective-permute-start.14) | collective-permute-done | bytes 524320 | tf_op jit(solution)/shard_map/ppermute | solution.py:14
  125.9 1.5 %fusion.2 = f32[128,1024]{1,0:T(8,128)S(1)} fusion(f32[128,1024]{1,0:T(8,128)} %collective-permute-done.15, f32[128,1024]{1,0:T(8,128)} %collective-permute-done.14, f32[128,1024]{1,0:T(8,128)S(1)} %collective-permute-done.13, f32[1152,1024]{1,0:T(8,128)} %copy-done.1), kind=kLoop, calls=%fused_computation.13 | loop fusion | flops 393216 | bytes 2621440 | tf_op jit(solution)/shard_map/add | solution.py:108
  127.5 0.1 collective-permute-start.16
  127.6 7.3 %collective-permute-done.16 = f32[64,1024]{1,0:T(8,128)S(1)} collective-permute-done((f32[64,1024]{1,0:T(8,128)S(1)}, f32[64,1024]{1,0:T(8,128)S(1)}, u32[]{:S(2)}, u32[]{:S(2)}) %collective-permute-start.16) | collective-permute-done | bytes 262176 | tf_op jit(solution)/shard_map/ppermute | solution.py:117
  134.9 0.8 add_multiply_fusion
  (38 shorter events, 0.8 us)
Async XLA Ops:
  0.6 17.2 %copy-start = (bf16[1024,1024]{1,0:T(8,128)(2,1)S(1)}, bf16[1024,1024]{1,0:T(8,128)(2,1)}, u32[]{:S(2)}) copy-start(bf16[1024,1024]{1,0:T(8,128)(2,1)} %param.5) | copy-start | bytes 6291460
  0.6 19.3 %collective-permute-start.1 = (bf16[128,1024]{1,0:T(8,128)(2,1)}, bf16[128,1024]{1,0:T(8,128)(2,1)S(1)}, u32[]{:S(2)}, u32[]{:S(2)}) collective-permute-start(bf16[128,1024]{1,0:T(8,128)(2,1)} %param.6), channel_id=1, source_target_pairs={{0,4},{2,6},{4,8},{6,10},{8,12},{10,14},{12,16},{14,18},{16,20},{1... | collective-permute-start | bytes 786440 | tf_op jit(solution)/shard_map/ppermute | solution.py:14
  4.5 31.4 %collective-permute-start = (bf16[128,1024]{1,0:T(8,128)(2,1)}, bf16[128,1024]{1,0:T(8,128)(2,1)S(1)}, u32[]{:S(2)}, u32[]{:S(2)}) collective-permute-start(bf16[128,1024]{1,0:T(8,128)(2,1)} %param.6), channel_id=1, source_target_pairs={{0,2},{2,0},{4,6},{6,4},{8,10},{10,8},{12,14},{14,12},{16,18},{18,... | collective-permute-start | bytes 786440 | tf_op jit(solution)/shard_map/ppermute | solution.py:19
  5.5 16.7 %collective-permute-start.2 = (bf16[128,1024]{1,0:T(8,128)(2,1)}, bf16[128,1024]{1,0:T(8,128)(2,1)S(1)}, u32[]{:S(2)}, u32[]{:S(2)}) collective-permute-start(bf16[128,1024]{1,0:T(8,128)(2,1)} %param.6), channel_id=1, source_target_pairs={{0,252},{2,254},{4,0},{6,2},{8,4},{10,6},{12,8},{14,10},{16,12},{1... | collective-permute-start | bytes 786440 | tf_op jit(solution)/shard_map/ppermute | solution.py:14
  20.0 17.0 %collective-permute-start.5 = (bf16[128,1024]{1,0:T(8,128)(2,1)S(1)}, bf16[128,1024]{1,0:T(8,128)(2,1)S(1)}, u32[]{:S(2)}, u32[]{:S(2)}) collective-permute-start(bf16[128,1024]{1,0:T(8,128)(2,1)S(1)} %collective-permute-done.1), channel_id=1, source_target_pairs={{0,4},{2,6},{4,8},{6,10},{8,12},{10,14},{12,16},{14,18},{16,20},{1... | collective-permute-start | bytes 786440 | tf_op jit(solution)/shard_map/ppermute | solution.py:14
  20.1 16.8 %collective-permute-start.3 = (bf16[128,1024]{1,0:T(8,128)(2,1)S(1)}, bf16[128,1024]{1,0:T(8,128)(2,1)S(1)}, u32[]{:S(2)}, u32[]{:S(2)}) collective-permute-start(bf16[128,1024]{1,0:T(8,128)(2,1)S(1)} %collective-permute-done.1), channel_id=1, source_target_pairs={{0,2},{2,0},{4,6},{6,4},{8,10},{10,8},{12,14},{14,12},{16,18},{18,... | collective-permute-start | bytes 786440 | tf_op jit(solution)/shard_map/ppermute | solution.py:19
  22.2 14.8 %collective-permute-start.6 = (bf16[128,1024]{1,0:T(8,128)(2,1)S(1)}, bf16[128,1024]{1,0:T(8,128)(2,1)S(1)}, u32[]{:S(2)}, u32[]{:S(2)}) collective-permute-start(bf16[128,1024]{1,0:T(8,128)(2,1)S(1)} %collective-permute-done.2), channel_id=1, source_target_pairs={{0,252},{2,254},{4,0},{6,2},{8,4},{10,6},{12,8},{14,10},{16,12},{1... | collective-permute-start | bytes 786440 | tf_op jit(solution)/shard_map/ppermute | solution.py:14
  30.1 6.9 %collective-permute-start.4 = (bf16[128,1024]{1,0:T(8,128)(2,1)S(1)}, bf16[128,1024]{1,0:T(8,128)(2,1)S(1)}, u32[]{:S(2)}, u32[]{:S(2)}) collective-permute-start(bf16[128,1024]{1,0:T(8,128)(2,1)S(1)} %collective-permute-done.2), channel_id=1, source_target_pairs={{0,2},{2,0},{4,6},{6,4},{8,10},{10,8},{12,14},{14,12},{16,18},{18,... | collective-permute-start | bytes 786440 | tf_op jit(solution)/shard_map/ppermute | solution.py:19
  35.1 1.7 %copy-start.3 = (bf16[1152,1024]{1,0:T(8,128)(2,1)S(1)}, bf16[1152,1024]{1,0:T(8,128)(2,1)}, u32[]{:S(2)}) copy-start(bf16[1152,1024]{1,0:T(8,128)(2,1)} %constant_dynamic-update-slice_fusion.8) | copy-start | bytes 7077892
  37.1 10.4 %collective-permute-start.7 = (bf16[128,1024]{1,0:T(8,128)(2,1)S(1)}, bf16[128,1024]{1,0:T(8,128)(2,1)S(1)}, u32[]{:S(2)}, u32[]{:S(2)}) collective-permute-start(bf16[128,1024]{1,0:T(8,128)(2,1)S(1)} %get-tuple-element.83), channel_id=1, source_target_pairs={{0,2},{2,0},{4,6},{6,4},{8,10},{10,8},{12,14},{14,12},{16,18},{18,... | collective-permute-start | bytes 786440 | tf_op jit(solution)/shard_map/ppermute | solution.py:19
  48.6 2.2 %copy-start.2 = (f32[1024]{0:T(1024)S(1)}, f32[1024]{0:T(1024)}, u32[]{:S(2)}) copy-start(f32[1024]{0:T(1024)} %param.9) | copy-start | bytes 12292
  55.2 40.5 %copy-start.1 = (f32[1152,1024]{1,0:T(8,128)}, f32[1152,1024]{1,0:T(8,128)S(1)}, u32[]{:S(2)}) copy-start(f32[1152,1024]{1,0:T(8,128)S(1)} %fusion.35) | copy-start | bytes 14155780
  55.3 2.0 %collective-permute-start.9 = (f32[128,1024]{1,0:T(8,128)S(1)}, f32[128,1024]{1,0:T(8,128)S(1)}, u32[]{:S(2)}, u32[]{:S(2)}) collective-permute-start(f32[128,1024]{1,0:T(8,128)S(1)} %slice.51), channel_id=1, source_target_pairs={{0,2},{2,0},{4,6},{6,4},{8,10},{10,8},{12,14},{14,12},{16,18},{18,... | collective-permute-start | bytes 1572872 | tf_op jit(solution)/shard_map/ppermute | solution.py:19
  57.5 30.4 %collective-permute-start.12 = (f32[128,1024]{1,0:T(8,128)S(1)}, f32[128,1024]{1,0:T(8,128)S(1)}, u32[]{:S(2)}, u32[]{:S(2)}) collective-permute-start(f32[128,1024]{1,0:T(8,128)S(1)} %get-tuple-element.76), channel_id=1, source_target_pairs={{0,252},{2,254},{4,0},{6,2},{8,4},{10,6},{12,8},{14,10},{16,12},{1... | collective-permute-start | bytes 1572872 | tf_op jit(solution)/shard_map/ppermute | solution.py:14
  66.1 21.8 %collective-permute-start.11 = (f32[128,1024]{1,0:T(8,128)S(1)}, f32[128,1024]{1,0:T(8,128)S(1)}, u32[]{:S(2)}, u32[]{:S(2)}) collective-permute-start(f32[128,1024]{1,0:T(8,128)S(1)} %get-tuple-element.81), channel_id=1, source_target_pairs={{0,2},{2,0},{4,6},{6,4},{8,10},{10,8},{12,14},{14,12},{16,18},{18,... | collective-permute-start | bytes 1572872 | tf_op jit(solution)/shard_map/ppermute | solution.py:19
  66.5 29.2 %collective-permute-start.10 = (f32[128,1024]{1,0:T(8,128)S(1)}, f32[128,1024]{1,0:T(8,128)S(1)}, u32[]{:S(2)}, u32[]{:S(2)}) collective-permute-start(f32[128,1024]{1,0:T(8,128)S(1)} %get-tuple-element.77), channel_id=1, source_target_pairs={{0,4},{2,6},{4,8},{6,10},{8,12},{10,14},{12,16},{14,18},{16,20},{1... | collective-permute-start | bytes 1572872 | tf_op jit(solution)/shard_map/ppermute | solution.py:14
  88.9 6.8 %collective-permute-start.8 = (f32[128,1024]{1,0:T(8,128)S(1)}, f32[128,1024]{1,0:T(8,128)S(1)}, u32[]{:S(2)}, u32[]{:S(2)}) collective-permute-start(f32[128,1024]{1,0:T(8,128)S(1)} %get-tuple-element.80), channel_id=1, source_target_pairs={{0,2},{2,0},{4,6},{6,4},{8,10},{10,8},{12,14},{14,12},{16,18},{18,... | collective-permute-start | bytes 1572872 | tf_op jit(solution)/shard_map/ppermute | solution.py:19
  94.0 10.4 %collective-permute-start.13 = (f32[128,1024]{1,0:T(8,128)S(1)}, f32[128,1024]{1,0:T(8,128)S(1)}, u32[]{:S(2)}, u32[]{:S(2)}) collective-permute-start(f32[128,1024]{1,0:T(8,128)S(1)} %get-tuple-element.78), channel_id=1, source_target_pairs={{0,2},{2,0},{4,6},{6,4},{8,10},{10,8},{12,14},{14,12},{16,18},{18,... | collective-permute-start | bytes 1572872 | tf_op jit(solution)/shard_map/ppermute | solution.py:19
  96.6 29.3 %collective-permute-start.14 = (f32[128,1024]{1,0:T(8,128)}, f32[128,1024]{1,0:T(8,128)}, u32[]{:S(2)}, u32[]{:S(2)}) collective-permute-start(f32[128,1024]{1,0:T(8,128)} %fusion.4), channel_id=1, source_target_pairs={{0,4},{2,6},{4,8},{6,10},{8,12},{10,14},{12,16},{14,18},{16,20},{1... | collective-permute-start | bytes 1572872 | tf_op jit(solution)/shard_map/ppermute | solution.py:14
  96.6 29.3 %collective-permute-start.15 = (f32[128,1024]{1,0:T(8,128)}, f32[128,1024]{1,0:T(8,128)}, u32[]{:S(2)}, u32[]{:S(2)}) collective-permute-start(f32[128,1024]{1,0:T(8,128)} %get-tuple-element.8), channel_id=1, source_target_pairs={{0,252},{2,254},{4,0},{6,2},{8,4},{10,6},{12,8},{14,10},{16,12},{1... | collective-permute-start | bytes 1572872 | tf_op jit(solution)/shard_map/ppermute | solution.py:14
  127.5 7.4 %collective-permute-start.16 = (f32[64,1024]{1,0:T(8,128)S(1)}, f32[64,1024]{1,0:T(8,128)S(1)}, u32[]{:S(2)}, u32[]{:S(2)}) collective-permute-start(f32[64,1024]{1,0:T(8,128)S(1)} %slice_select_fusion), channel_id=1, source_target_pairs={{0,1},{1,0},{2,3},{3,2},{4,5},{5,4},{6,7},{7,6},{8,9},{9,8},{10,11... | collective-permute-start | bytes 786440 | tf_op jit(solution)/shard_map/ppermute | solution.py:117

commit v5 on v2

--- a/solution.py
+++ b/solution.py
@@ -32,24 +32,33 @@
     inner_idx = jnp.arange(tile_rows, dtype=jnp.int32)
     same_row = inner_idx[:, None] == inner_idx[None, :]
 
-    down2 = passed_along(keys, "dp", 2)
-    up2 = passed_along(keys, "dp", -2)
-    down4 = passed_along(down2, "dp", 2)
-    up4 = passed_along(up2, "dp", -2)
-    sw_own = swapped(keys, "dp")
-    sw_down2 = swapped(down2, "dp")
-    sw_up2 = swapped(up2, "dp")
-    sw_far = swapped(jnp.where(core == 0, up4, down4), "dp")
+    def ring(x, forward):
+        pairs = []
+        for i in range(cycle_size):
+            step = 2 if (i % 2 == 0) == forward else -2
+            pairs.append((i, (i + step) % cycle_size))
+        return lax.ppermute(x, "dp", pairs)
+
+    partner_keys = swapped(keys, "dp")
+    pair = jnp.where(
+        core == 0,
+        jnp.concatenate([keys, partner_keys], axis=0),
+        jnp.concatenate([partner_keys, keys], axis=0),
+    )
+    recv1 = ring(pair, True)
+    recv2 = ring(recv1, True)
+    side1 = swapped(recv1, "dp")
+    side2 = swapped(jnp.where(core == 0, recv2[tile_rows:], recv2[:tile_rows]), "dp")
     key_tiles = [
-        ("own", keys, 0),
-        ("sw_own", sw_own, delta),
-        ("down2", down2, -2),
-        ("up2", up2, 2),
-        ("sw_down2", sw_down2, delta - 2),
-        ("sw_up2", sw_up2, delta + 2),
-        ("down4", down4, -4),
-        ("up4", up4, 4),
-        ("sw_far", sw_far, -3 * delta),
+        ("pair0", pair[:tile_rows], -core),
+        ("pair1", pair[tile_rows:], 1 - core),
+        ("r1_0", recv1[:tile_rows], -2 * delta - core),
+        ("r1_1", recv1[tile_rows:], -2 * delta + 1 - core),
+        ("r2_0", recv2[:tile_rows], -4 * delta - core),
+        ("r2_1", recv2[tile_rows:], -4 * delta + 1 - core),
+        ("s1_0", side1[:tile_rows], 2 * delta - core),
+        ("s1_1", side1[tile_rows:], 2 * delta + 1 - core),
+        ("s2", side2, 4 * delta),
     ]
     run_max = jnp.full((query_rows,), -1e30, jnp.float32)
     run_sum = jnp.zeros((query_rows,), jnp.float32)
@@ -91,29 +100,29 @@
     all_parts = lax.dot_general(
         coefficient, queries, (((0,), (0,)), ((), ())), preferred_element_type=jnp.float32
     )
-    key_parts = {
-        name: all_parts[i * tile_rows : (i + 1) * tile_rows] for i, (name, _, _, _) in enumerate(stored)
-    }
-    back_own = swapped(key_parts["sw_own"], "dp")
-    back_down2 = swapped(key_parts["sw_down2"], "dp")
-    back_up2 = swapped(key_parts["sw_up2"], "dp")
-    back_far = swapped(key_parts["sw_far"], "dp")
-    zero = jnp.zeros_like(back_far)
-    far_up = key_parts["up4"] + jnp.where(core == 0, back_far, zero)
-    far_down = key_parts["down4"] + jnp.where(core == 0, zero, back_far)
-    near_up = key_parts["up2"] + back_up2 + passed_along(far_up, "dp", 2)
-    near_down = key_parts["down2"] + back_down2 + passed_along(far_down, "dp", -2)
-    total = (
-        key_parts["own"]
-        + back_own
-        + passed_along(near_up, "dp", 2)
-        + passed_along(near_down, "dp", -2)
+    t = tile_rows
+    part_pair = all_parts[0 : 2 * t]
+    part_r1 = all_parts[2 * t : 4 * t]
+    part_r2 = all_parts[4 * t : 6 * t]
+    part_s1 = all_parts[6 * t : 8 * t]
+    part_s2 = all_parts[8 * t : 9 * t]
+    back_s2 = swapped(part_s2, "dp")
+    zero = jnp.zeros_like(back_s2)
+    full_r2 = part_r2 + jnp.where(
+        core == 1,
+        jnp.concatenate([back_s2, zero], axis=0),
+        jnp.concatenate([zero, back_s2], axis=0),
     )
-    half = tile_rows // 2
+    full_r1 = part_r1 + swapped(part_s1, "dp") + ring(full_r2, False)
+    full_pair = part_pair + ring(full_r1, False)
+    mine = jnp.where(core == 0, full_pair[:t], full_pair[t:])
+    other = jnp.where(core == 0, full_pair[t:], full_pair[:t])
+    total = mine + swapped(other, "dp")
+    half = t // 2
     halves = total.reshape(2, half, total.shape[1])
-    mine = jnp.where(rep_index == 0, halves[0], halves[1])
-    other = jnp.where(rep_index == 0, halves[1], halves[0])
-    grad_keys = logit_scale * (mine + lax.ppermute(other, "rep", [(0, 1), (1, 0)]))
+    mine_half = jnp.where(rep_index == 0, halves[0], halves[1])
+    other_half = jnp.where(rep_index == 0, halves[1], halves[0])
+    grad_keys = logit_scale * (mine_half + lax.ppermute(other_half, "rep", [(0, 1), (1, 0)]))
     return (row_loss, grad_query, grad_keys)
 
 

time: 134 us -> 150 us (1.12)
  waiting for transfers between devices: 48.1 us -> 82.5 us
  starting transfers between devices: 46.1 us -> 26.4 us
  other arithmetic: 10.6 us -> 15.8 us
  matrix products: 17.3 us -> 14.6 us
  local copies, waits for them, and re-layouts: 10.5 us -> 9 us
    ppermute x9 -> x5, waiting for transfers between devices: 46.7 us -> 78.1 us  [the longest x4 75.1 us: ring(): return lax.ppermute(x, 'dp', pairs)]
    ppermute x9 -> x5, starting transfers between devices: 36 us -> 17.5 us  [the longest x4 17.4 us: ring(): return lax.ppermute(x, 'dp', pairs)]
    ppermute x8 -> x6, waiting for transfers between devices: 1.41 us -> 4.41 us  [swapped(): return lax.ppermute(x, axis, [(i, i ^ 1) for i in range(count)])]
    slice x0 -> x1, other arithmetic: none -> 1.77 us  [body(): part_s1 = all_parts[6 * t:8 * t]]
    dot_general x1, matrix products: 6.13 us -> 4.45 us  [body(): jnp.dot(coefficient, window, preferred_element_type=jnp.float32)]
    ppermute x8 -> x6, starting transfers between devices: 10.1 us -> 8.88 us  [swapped(): return lax.ppermute(x, axis, [(i, i ^ 1) for i in range(count)])]
    unnamed x17 -> x23, local copies, waits for them, and re-layouts: 7.5 us -> 7.31 us
  transfers between devices with their start and end apart: 17 -> 11, of which waited for: 6 -> 7; matrix products, arithmetic and copies ran while one was open for 19% -> 13% of each run, Pallas kernels for 0% -> 0%
where the time goes in v5:
time: 150 us; the launch traced here: 149 us
  waiting for transfers between devices  82.5 us (55%)
  starting transfers between devices  26.4 us (18%)
  other arithmetic  15.8 us (11%)
  matrix products  14.6 us (10%)
  local copies, waits for them, and re-layouts  9 us (6%)
    ppermute x4, waiting for transfers between devices, ring(): return lax.ppermute(x, 'dp', pairs)  75.1 us
    ppermute x4, starting transfers between devices, ring(): return lax.ppermute(x, 'dp', pairs)  17.4 us
    ppermute x6, starting transfers between devices, swapped(): return lax.ppermute(x, axis, [(i, i ^ 1) for i in range(count)])  8.88 us
    dot_general x9, matrix products, body(): lax.dot_general(queries, key_tile, (((1,), (1,)), ((), ())), preferred_el...  7.56 us
    unnamed x23, local copies, waits for them, and re-layouts  7.31 us
    dot_general x1, matrix products, body(): jnp.dot(coefficient, window, preferred_element_type=jnp.float32)  4.45 us
    ppermute x6, waiting for transfers between devices, swapped(): return lax.ppermute(x, axis, [(i, i ^ 1) for i in range(count)])  4.41 us
    unnamed x9, other arithmetic  3.48 us
  transfers between devices with their start and end apart: 11, of which 7 were waited for; matrix products, arithmetic and copies ran while one was open for 13% of the time, Pallas kernels for 0%

profile of v5, /device:TPU:1, one launch (start us, length us, event | category | flops | bytes accessed | tf_op | source)
XLA Modules:
  0.0 149.3 jit_solution(4491050616292521702)
XLA Ops:
  0.6 3.3 %collective-permute-start = (bf16[128,1024]{1,0:T(8,128)(2,1)}, bf16[128,1024]{1,0:T(8,128)(2,1)S(1)}, u32[]{:S(2)}, u32[]{:S(2)}) collective-permute-start(bf16[128,1024]{1,0:T(8,128)(2,1)} %param.6), channel_id=1, source_target_pairs={{0,2},{2,0},{4,6},{6,4},{8,10},{10,8},{12,14},{14,12},{16,18},{18,... | collective-permute-start | bytes 786440 | tf_op jit(solution)/shard_map/ppermute | solution.py:19
  3.9 1.3 fusion.35
  5.3 0.7 fusion.46
  6.0 0.1 broadcast_bitcast_fusion.17
  6.1 0.1 broadcast_bitcast_fusion.11
  6.2 0.1 broadcast_bitcast_fusion.14
  6.5 0.1 broadcast_bitcast_fusion.8
  6.5 0.1 broadcast_bitcast_fusion.1
  6.6 0.1 broadcast_bitcast_fusion.3
  6.7 0.1 broadcast_bitcast_fusion.4
  6.7 0.1 broadcast_bitcast_fusion.6
  6.9 0.1 broadcast_bitcast_fusion.7
  6.9 2.0 %constant_dynamic-update-slice_fusion.4 = (bf16[1152,1024]{1,0:T(8,128)(2,1)}, bf16[256,1024]{1,0:T(8,128)(2,1)S(1)}) fusion(bf16[128,1024]{1,0:T(8,128)(2,1)} %param.6, bf16[128,1024]{1,0:T(8,128)(2,1)S(1)} %collective-permute-done, pred[]{:T(512)S(6)} %eq.201), kind=kLoop, calls=%fused_computation.96 | loop fusion | flops 2359295 | bytes 1572865
  8.9 9.0 %collective-permute-start.1 = (bf16[256,1024]{1,0:T(8,128)(2,1)S(1)}, bf16[256,1024]{1,0:T(8,128)(2,1)S(1)}, u32[]{:S(2)}, u32[]{:S(2)}) collective-permute-start(bf16[256,1024]{1,0:T(8,128)(2,1)S(1)} %get-tuple-element.43), channel_id=1, source_target_pairs={{0,4},{2,254},{4,8},{6,2},{8,12},{10,6},{12,16},{14,10},{16,20},{1... | collective-permute-start | bytes 1572872 | tf_op jit(solution)/shard_map/ppermute | solution.py:40
  17.9 0.8 select_reduce_fusion.25
  18.7 0.8 select_reduce_fusion.26
  19.6 10.0 %collective-permute-done.1 = bf16[256,1024]{1,0:T(8,128)(2,1)S(1)} collective-permute-done((bf16[256,1024]{1,0:T(8,128)(2,1)S(1)}, bf16[256,1024]{1,0:T(8,128)(2,1)S(1)}, u32[]{:S(2)}, u32[]{:S(2)}) %collective-permute-start.1) | collective-permute-done | bytes 524320 | tf_op jit(solution)/shard_map/ppermute | solution.py:40
  29.6 8.3 %collective-permute-start.2 = (bf16[256,1024]{1,0:T(8,128)(2,1)S(1)}, bf16[256,1024]{1,0:T(8,128)(2,1)S(1)}, u32[]{:S(2)}, u32[]{:S(2)}) collective-permute-start(bf16[256,1024]{1,0:T(8,128)(2,1)S(1)} %collective-permute-done.1), channel_id=1, source_target_pairs={{0,4},{2,254},{4,8},{6,2},{8,12},{10,6},{12,16},{14,10},{16,20},{1... | collective-permute-start | bytes 1572872 | tf_op jit(solution)/shard_map/ppermute | solution.py:40
  38.0 0.8 select_reduce_fusion.23
  38.8 0.8 select_reduce_fusion.24
  39.7 9.6 %collective-permute-done.2 = bf16[256,1024]{1,0:T(8,128)(2,1)S(1)} collective-permute-done((bf16[256,1024]{1,0:T(8,128)(2,1)S(1)}, bf16[256,1024]{1,0:T(8,128)(2,1)S(1)}, u32[]{:S(2)}, u32[]{:S(2)}) %collective-permute-start.2) | collective-permute-done | bytes 524320 | tf_op jit(solution)/shard_map/ppermute | solution.py:40
  49.3 2.4 %collective-permute-start.4 = (bf16[128,1024]{1,0:T(8,128)(2,1)S(1)}, bf16[128,1024]{1,0:T(8,128)(2,1)S(1)}, u32[]{:S(2)}, u32[]{:S(2)}) collective-permute-start(bf16[128,1024]{1,0:T(8,128)(2,1)S(1)} %broadcast_select_fusion), channel_id=1, source_target_pairs={{0,2},{2,0},{4,6},{6,4},{8,10},{10,8},{12,14},{14,12},{16,18},{18,... | collective-permute-start | bytes 786440 | tf_op jit(solution)/shard_map/ppermute | solution.py:19
  51.8 0.8 select_reduce_fusion.19
  52.6 0.8 select_reduce_fusion.20
  53.5 0.8 select_reduce_fusion.21
  54.3 0.8 select_reduce_fusion.22
  55.2 0.8 select_reduce_fusion.18
  56.1 0.2 select_reduce_fusion.6
  56.4 0.8 select_reduce_fusion.8
  57.2 0.8 select_reduce_fusion.7
  58.0 0.6 add_subtract_fusion
  58.6 0.2 fusion.10
  58.8 0.2 fusion.11
  59.0 0.2 fusion.12
  59.2 0.2 fusion.13
  59.4 0.2 fusion.14
  59.6 0.2 fusion.15
  59.7 0.2 fusion.16
  59.9 0.2 fusion.17
  60.1 0.2 fusion.18
  60.3 2.6 %fusion.49 = f32[1152,1024]{1,0:T(8,128)S(1)} fusion(bf16[1024,1152]{0,1:T(8,128)(2,1)S(1)} %fusion.18, bf16[1024,1024]{1,0:T(8,128)(2,1)S(1)} %copy-done), kind=kOutput, calls=%fused_computation.157 | convolution fusion | flops 2415919104 | bytes 9175040 | tf_op jit(solution)/shard_map/dot_general | solution.py:100
  63.0 2.1 %copy-done.1 = f32[1152,1024]{1,0:T(8,128)} copy-done((f32[1152,1024]{1,0:T(8,128)}, f32[1152,1024]{1,0:T(8,128)S(1)}, u32[]{:S(2)}) %copy-start.1) | copy-done | bytes 4718616
  65.1 0.1 collective-permute-start.6
  65.2 1.9 %collective-permute-done.6 = f32[128,1024]{1,0:T(8,128)S(1)} collective-permute-done((f32[128,1024]{1,0:T(8,128)S(1)}, f32[128,1024]{1,0:T(8,128)S(1)}, u32[]{:S(2)}, u32[]{:S(2)}) %collective-permute-start.6) | collective-permute-done | bytes 524320 | tf_op jit(solution)/shard_map/ppermute | solution.py:19
  67.1 1.8 %fusion.48 = (f32[256,1024]{1,0:T(8,128)S(1)}, f32[256,1024]{1,0:T(8,128)S(1)}) fusion(f32[1152,1024]{1,0:T(8,128)} %copy-done.1, f32[128,1024]{1,0:T(8,128)S(1)} %collective-permute-done.6, pred[]{:T(512)S(6)} %eq.238), kind=kLoop, calls=%fused_computation.156 | loop fusion | flops 524288 | bytes 4718593 | tf_op jit(solution)/shard_map/slice | solution.py:107
  68.9 0.2 collective-permute-start.5
  69.1 2.5 %collective-permute-done.5 = f32[256,1024]{1,0:T(8,128)S(1)} collective-permute-done((f32[256,1024]{1,0:T(8,128)S(1)}, f32[256,1024]{1,0:T(8,128)S(1)}, u32[]{:S(2)}, u32[]{:S(2)}) %collective-permute-start.5) | collective-permute-done | bytes 1048608 | tf_op jit(solution)/shard_map/ppermute | solution.py:19
  71.6 25.4 %collective-permute-done.7 = f32[256,1024]{1,0:T(8,128)S(1)} collective-permute-done((f32[256,1024]{1,0:T(8,128)S(1)}, f32[256,1024]{1,0:T(8,128)S(1)}, u32[]{:S(2)}, u32[]{:S(2)}) %collective-permute-start.7) | collective-permute-done | bytes 1048608 | tf_op jit(solution)/shard_map/ppermute | solution.py:40
  97.0 1.5 %fusion.9 = f32[256,1024]{1,0:T(8,128)S(1)} fusion(f32[256,1024]{1,0:T(8,128)S(1)} %collective-permute-done.7, f32[256,1024]{1,0:T(8,128)S(1)} %collective-permute-done.5, f32[1152,1024]{1,0:T(8,128)} %copy-done.1), kind=kLoop, calls=%fused_computation.21 | loop fusion | flops 524288 | bytes 4194304 | tf_op jit(solution)/shard_map/add | solution.py:116
  98.5 0.1 collective-permute-start.8
  98.6 30.1 %collective-permute-done.8 = f32[256,1024]{1,0:T(8,128)S(1)} collective-permute-done((f32[256,1024]{1,0:T(8,128)S(1)}, f32[256,1024]{1,0:T(8,128)S(1)}, u32[]{:S(2)}, u32[]{:S(2)}) %collective-permute-start.8) | collective-permute-done | bytes 1048608 | tf_op jit(solution)/shard_map/ppermute | solution.py:40
  128.7 1.4 slice_add_fusion.2
  130.1 0.8 slice_select_fusion
  130.9 2.8 %collective-permute-start.9 = (f32[128,1024]{1,0:T(8,128)}, f32[128,1024]{1,0:T(8,128)}, u32[]{:S(2)}, u32[]{:S(2)}) collective-permute-start(f32[128,1024]{1,0:T(8,128)} %slice_select_fusion), channel_id=1, source_target_pairs={{0,2},{2,0},{4,6},{6,4},{8,10},{10,8},{12,14},{14,12},{16,18},{18,... | collective-permute-start | bytes 1572872 | tf_op jit(solution)/shard_map/ppermute | solution.py:19
  133.7 1.9 %constant_dynamic-update-slice_fusion.3 = bf16[1152,1024]{1,0:T(8,128)(2,1)} fusion(bf16[1152,1024]{1,0:T(8,128)(2,1)} %get-tuple-element.42, bf16[256,1024]{1,0:T(8,128)(2,1)} %copy-done.3), kind=kLoop, calls=%fused_computation.95 | loop fusion | bytes 1048576
  135.7 2.0 %constant_dynamic-update-slice_fusion.2 = bf16[1152,1024]{1,0:T(8,128)(2,1)} fusion(bf16[1152,1024]{1,0:T(8,128)(2,1)} %constant_dynamic-update-slice_fusion.3, bf16[256,1024]{1,0:T(8,128)(2,1)} %copy-done.2), kind=kLoop, calls=%fused_computation.94 | loop fusion | bytes 1048576
  137.7 0.8 constant_dynamic-update-slice_fusion.1
  138.5 0.7 constant_dynamic-update-slice_fusion
  139.2 1.3 select_add_fusion
  140.6 0.1 collective-permute-start.10
  140.7 0.4 copy-done.7
  141.1 4.4 %convolution_multiply_fusion = f32[1024,1024]{1,0:T(8,128)} fusion(bf16[1024,1152]{0,1:T(8,128)(2,1)S(1)} %copy-done.9, bf16[1152,1024]{1,0:T(8,128)(2,1)S(1)} %copy-done.7), kind=kOutput, calls=%fused_computation | convolution fusion | flops 2416967680 | bytes 8912896 | tf_op jit(solution)/shard_map/dot_general | solution.py:99
  145.5 3.0 %collective-permute-done.10 = f32[64,1024]{1,0:T(8,128)S(1)} collective-permute-done((f32[64,1024]{1,0:T(8,128)S(1)}, f32[64,1024]{1,0:T(8,128)S(1)}, u32[]{:S(2)}, u32[]{:S(2)}) %collective-permute-start.10) | collective-permute-done | bytes 262176 | tf_op jit(solution)/shard_map/ppermute | solution.py:125
  148.5 0.8 add_multiply_fusion
  (33 shorter events, 0.5 us)
Async XLA Ops:
  0.6 17.2 %copy-start = (bf16[1024,1024]{1,0:T(8,128)(2,1)S(1)}, bf16[1024,1024]{1,0:T(8,128)(2,1)}, u32[]{:S(2)}) copy-start(bf16[1024,1024]{1,0:T(8,128)(2,1)} %param.5) | copy-start | bytes 6291460
  0.6 6.3 %collective-permute-start = (bf16[128,1024]{1,0:T(8,128)(2,1)}, bf16[128,1024]{1,0:T(8,128)(2,1)S(1)}, u32[]{:S(2)}, u32[]{:S(2)}) collective-permute-start(bf16[128,1024]{1,0:T(8,128)(2,1)} %param.6), channel_id=1, source_target_pairs={{0,2},{2,0},{4,6},{6,4},{8,10},{10,8},{12,14},{14,12},{16,18},{18,... | collective-permute-start | bytes 786440 | tf_op jit(solution)/shard_map/ppermute | solution.py:19
  8.9 20.7 %collective-permute-start.1 = (bf16[256,1024]{1,0:T(8,128)(2,1)S(1)}, bf16[256,1024]{1,0:T(8,128)(2,1)S(1)}, u32[]{:S(2)}, u32[]{:S(2)}) collective-permute-start(bf16[256,1024]{1,0:T(8,128)(2,1)S(1)} %get-tuple-element.43), channel_id=1, source_target_pairs={{0,4},{2,254},{4,8},{6,2},{8,12},{10,6},{12,16},{14,10},{16,20},{1... | collective-permute-start | bytes 1572872 | tf_op jit(solution)/shard_map/ppermute | solution.py:40
  29.6 10.0 %copy-start.3 = (bf16[256,1024]{1,0:T(8,128)(2,1)}, bf16[256,1024]{1,0:T(8,128)(2,1)S(1)}, u32[]{:S(2)}) copy-start(bf16[256,1024]{1,0:T(8,128)(2,1)S(1)} %collective-permute-done.1) | copy-start | bytes 1572868
  29.6 22.1 %collective-permute-start.3 = (bf16[256,1024]{1,0:T(8,128)(2,1)S(1)}, bf16[256,1024]{1,0:T(8,128)(2,1)S(1)}, u32[]{:S(2)}, u32[]{:S(2)}) collective-permute-start(bf16[256,1024]{1,0:T(8,128)(2,1)S(1)} %collective-permute-done.1), channel_id=1, source_target_pairs={{0,2},{2,0},{4,6},{6,4},{8,10},{10,8},{12,14},{14,12},{16,18},{18,... | collective-permute-start | bytes 1572872 | tf_op jit(solution)/shard_map/ppermute | solution.py:19
  29.6 19.7 %collective-permute-start.2 = (bf16[256,1024]{1,0:T(8,128)(2,1)S(1)}, bf16[256,1024]{1,0:T(8,128)(2,1)S(1)}, u32[]{:S(2)}, u32[]{:S(2)}) collective-permute-start(bf16[256,1024]{1,0:T(8,128)(2,1)S(1)} %collective-permute-done.1), channel_id=1, source_target_pairs={{0,4},{2,254},{4,8},{6,2},{8,12},{10,6},{12,16},{14,10},{16,20},{1... | collective-permute-start | bytes 1572872 | tf_op jit(solution)/shard_map/ppermute | solution.py:40
  49.3 5.0 %copy-start.2 = (bf16[256,1024]{1,0:T(8,128)(2,1)}, bf16[256,1024]{1,0:T(8,128)(2,1)S(1)}, u32[]{:S(2)}) copy-start(bf16[256,1024]{1,0:T(8,128)(2,1)S(1)} %collective-permute-done.2) | copy-start | bytes 1572868
  49.3 5.9 %collective-permute-start.4 = (bf16[128,1024]{1,0:T(8,128)(2,1)S(1)}, bf16[128,1024]{1,0:T(8,128)(2,1)S(1)}, u32[]{:S(2)}, u32[]{:S(2)}) collective-permute-start(bf16[128,1024]{1,0:T(8,128)(2,1)S(1)} %broadcast_select_fusion), channel_id=1, source_target_pairs={{0,2},{2,0},{4,6},{6,4},{8,10},{10,8},{12,14},{14,12},{16,18},{18,... | collective-permute-start | bytes 786440 | tf_op jit(solution)/shard_map/ppermute | solution.py:19
  51.8 1.7 %copy-start.4 = (bf16[256,1024]{1,0:T(8,128)(2,1)}, bf16[256,1024]{1,0:T(8,128)(2,1)S(1)}, u32[]{:S(2)}) copy-start(bf16[256,1024]{1,0:T(8,128)(2,1)S(1)} %collective-permute-done.3) | copy-start | bytes 1572868
  56.4 2.2 %copy-start.6 = (f32[1024]{0:T(1024)S(1)}, f32[1024]{0:T(1024)}, u32[]{:S(2)}) copy-start(f32[1024]{0:T(1024)} %param.9) | copy-start | bytes 12292
  60.3 2.6 %copy-start.8 = (bf16[1024,1152]{0,1:T(8,128)(2,1)}, bf16[1024,1152]{0,1:T(8,128)(2,1)S(1)}, u32[]{:S(2)}) copy-start(bf16[1024,1152]{0,1:T(8,128)(2,1)S(1)} %fusion.18) | copy-start | bytes 7077892
  63.0 2.1 %copy-start.1 = (f32[1152,1024]{1,0:T(8,128)}, f32[1152,1024]{1,0:T(8,128)S(1)}, u32[]{:S(2)}) copy-start(f32[1152,1024]{1,0:T(8,128)S(1)} %fusion.49) | copy-start | bytes 14155780
  65.1 2.0 %collective-permute-start.6 = (f32[128,1024]{1,0:T(8,128)S(1)}, f32[128,1024]{1,0:T(8,128)S(1)}, u32[]{:S(2)}, u32[]{:S(2)}) collective-permute-start(f32[128,1024]{1,0:T(8,128)S(1)} %slice.92), channel_id=1, source_target_pairs={{0,2},{2,0},{4,6},{6,4},{8,10},{10,8},{12,14},{14,12},{16,18},{18,... | collective-permute-start | bytes 1572872 | tf_op jit(solution)/shard_map/ppermute | solution.py:19
  68.9 2.7 %collective-permute-start.5 = (f32[256,1024]{1,0:T(8,128)S(1)}, f32[256,1024]{1,0:T(8,128)S(1)}, u32[]{:S(2)}, u32[]{:S(2)}) collective-permute-start(f32[256,1024]{1,0:T(8,128)S(1)} %get-tuple-element.72), channel_id=1, source_target_pairs={{0,2},{2,0},{4,6},{6,4},{8,10},{10,8},{12,14},{14,12},{16,18},{18,... | collective-permute-start | bytes 3145736 | tf_op jit(solution)/shard_map/ppermute | solution.py:19
  69.1 27.9 %collective-permute-start.7 = (f32[256,1024]{1,0:T(8,128)S(1)}, f32[256,1024]{1,0:T(8,128)S(1)}, u32[]{:S(2)}, u32[]{:S(2)}) collective-permute-start(f32[256,1024]{1,0:T(8,128)S(1)} %get-tuple-element.73), channel_id=1, source_target_pairs={{0,252},{2,6},{4,0},{6,10},{8,4},{10,14},{12,8},{14,18},{16,12},{1... | collective-permute-start | bytes 3145736 | tf_op jit(solution)/shard_map/ppermute | solution.py:40
  98.5 30.2 %collective-permute-start.8 = (f32[256,1024]{1,0:T(8,128)S(1)}, f32[256,1024]{1,0:T(8,128)S(1)}, u32[]{:S(2)}, u32[]{:S(2)}) collective-permute-start(f32[256,1024]{1,0:T(8,128)S(1)} %fusion.9), channel_id=1, source_target_pairs={{0,252},{2,6},{4,0},{6,10},{8,4},{10,14},{12,8},{14,18},{16,12},{1... | collective-permute-start | bytes 3145736 | tf_op jit(solution)/shard_map/ppermute | solution.py:40
  130.9 8.3 %collective-permute-start.9 = (f32[128,1024]{1,0:T(8,128)}, f32[128,1024]{1,0:T(8,128)}, u32[]{:S(2)}, u32[]{:S(2)}) collective-permute-start(f32[128,1024]{1,0:T(8,128)} %slice_select_fusion), channel_id=1, source_target_pairs={{0,2},{2,0},{4,6},{6,4},{8,10},{10,8},{12,14},{14,12},{16,18},{18,... | collective-permute-start | bytes 1572872 | tf_op jit(solution)/shard_map/ppermute | solution.py:19
  133.7 4.0 %copy-start.5 = (bf16[256,1024]{1,0:T(8,128)(2,1)S(1)}, bf16[256,1024]{1,0:T(8,128)(2,1)}, u32[]{:S(2)}) copy-start(bf16[256,1024]{1,0:T(8,128)(2,1)} %copy-done.4) | copy-start | bytes 1572868
  135.7 5.0 %copy-start.9 = (bf16[1024,1152]{0,1:T(8,128)(2,1)S(1)}, bf16[1024,1152]{0,1:T(8,128)(2,1)}, u32[]{:S(2)}) copy-start(bf16[1024,1152]{0,1:T(8,128)(2,1)} %copy-done.8) | copy-start | bytes 7077892
  139.2 1.8 %copy-start.7 = (bf16[1152,1024]{1,0:T(8,128)(2,1)S(1)}, bf16[1152,1024]{1,0:T(8,128)(2,1)}, u32[]{:S(2)}) copy-start(bf16[1152,1024]{1,0:T(8,128)(2,1)} %constant_dynamic-update-slice_fusion) | copy-start | bytes 7077892
  140.6 7.9 %collective-permute-start.10 = (f32[64,1024]{1,0:T(8,128)S(1)}, f32[64,1024]{1,0:T(8,128)S(1)}, u32[]{:S(2)}, u32[]{:S(2)}) collective-permute-start(f32[64,1024]{1,0:T(8,128)S(1)} %slice_select_fusion.1), channel_id=1, source_target_pairs={{0,1},{1,0},{2,3},{3,2},{4,5},{5,4},{6,7},{7,6},{8,9},{9,8},{10,11... | collective-permute-start | bytes 786440 | tf_op jit(solution)/shard_map/ppermute | solution.py:125

commit v6 on v2

--- a/solution.py
+++ b/solution.py
@@ -37,8 +37,9 @@
     down4 = passed_along(down2, "dp", 2)
     up4 = passed_along(up2, "dp", -2)
     sw_own = swapped(keys, "dp")
-    sw_down2 = swapped(down2, "dp")
-    sw_up2 = swapped(up2, "dp")
+    sw_near = swapped(jnp.concatenate([down2, up2], axis=0), "dp")
+    sw_down2 = sw_near[:tile_rows]
+    sw_up2 = sw_near[tile_rows:]
     sw_far = swapped(jnp.where(core == 0, up4, down4), "dp")
     key_tiles = [
         ("own", keys, 0),
@@ -88,16 +89,26 @@
     coefficient = jnp.concatenate(coefficients, axis=1)
     window = jnp.concatenate([key_tile for _, key_tile, _, _ in stored], axis=0)
     grad_query = logit_scale * jnp.dot(coefficient, window, preferred_element_type=jnp.float32)
-    all_parts = lax.dot_general(
-        coefficient, queries, (((0,), (0,)), ((), ())), preferred_element_type=jnp.float32
+    first = ("sw_own", "sw_down2", "sw_up2", "down4", "up4", "sw_far")
+    order = {name: i for i, (name, _, _, _) in enumerate(stored)}
+
+    def parts_of(names):
+        cols = jnp.concatenate([coefficients[order[n]] for n in names], axis=1)
+        out = lax.dot_general(
+            cols, queries, (((0,), (0,)), ((), ())), preferred_element_type=jnp.float32
+        )
+        return {n: out[i * tile_rows : (i + 1) * tile_rows] for i, n in enumerate(names)}
+
+    key_parts = parts_of(first)
+    key_parts.update(parts_of(("own", "down2", "up2")))
+    backs = swapped(
+        jnp.concatenate([key_parts[n] for n in ("sw_own", "sw_down2", "sw_up2", "sw_far")], axis=0),
+        "dp",
     )
-    key_parts = {
-        name: all_parts[i * tile_rows : (i + 1) * tile_rows] for i, (name, _, _, _) in enumerate(stored)
-    }
-    back_own = swapped(key_parts["sw_own"], "dp")
-    back_down2 = swapped(key_parts["sw_down2"], "dp")
-    back_up2 = swapped(key_parts["sw_up2"], "dp")
-    back_far = swapped(key_parts["sw_far"], "dp")
+    back_own = backs[:tile_rows]
+    back_down2 = backs[tile_rows : 2 * tile_rows]
+    back_up2 = backs[2 * tile_rows : 3 * tile_rows]
+    back_far = backs[3 * tile_rows :]
     zero = jnp.zeros_like(back_far)
     far_up = key_parts["up4"] + jnp.where(core == 0, back_far, zero)
     far_down = key_parts["down4"] + jnp.where(core == 0, zero, back_far)

time: 134 us -> 141 us (1.052)
  waiting for transfers between devices: 48.1 us -> 62.3 us
  local copies, waits for them, and re-layouts: 10.5 us -> 4.32 us
  starting transfers between devices: 46.1 us -> 44.6 us
    ppermute x8, waiting for transfers between devices: 45.5 us -> 58.2 us  [passed_along(): return lax.ppermute(x, axis, [(i, (i + by) % count) for i in range(count)])]
    ppermute x1, starting transfers between devices: 0.09 us -> 7.62 us  [body(): lax.ppermute(other, 'rep', [(0, 1), (1, 0)])]
    ppermute x8, starting transfers between devices: 35.9 us -> 28.5 us  [passed_along(): return lax.ppermute(x, axis, [(i, (i + by) % count) for i in range(count)])]
    unnamed x17 -> x22, local copies, waits for them, and re-layouts: 7.5 us -> 2.53 us
    ppermute x8 -> x4, waiting for transfers between devices: 1.41 us -> 4.15 us  [swapped(): return lax.ppermute(x, axis, [(i, i ^ 1) for i in range(count)])]
    ppermute x8 -> x4, starting transfers between devices: 10.1 us -> 8.48 us  [swapped(): return lax.ppermute(x, axis, [(i, i ^ 1) for i in range(count)])]
  transfers between devices with their start and end apart: 17 -> 13, of which waited for: 6 -> 7; matrix products, arithmetic and copies ran while one was open for 19% -> 15% of each run, Pallas kernels for 0% -> 0%
where the time goes in v6:
time: 141 us
  waiting for transfers between devices  62.3 us (44%)
  starting transfers between devices  44.6 us (32%)
  matrix products  18.4 us (13%)
  other arithmetic  10.2 us (7%)
  local copies, waits for them, and re-layouts  4.32 us (3%)
    ppermute x8, waiting for transfers between devices, passed_along(): return lax.ppermute(x, axis, [(i, (i + by) % count) for i in range(count)])  58.2 us
    ppermute x8, starting transfers between devices, passed_along(): return lax.ppermute(x, axis, [(i, (i + by) % count) for i in range(count)])  28.5 us
    dot_general x9, matrix products, body(): lax.dot_general(queries, key_tile, (((1,), (1,)), ((), ())), preferred_el...  9.47 us
    ppermute x4, starting transfers between devices, swapped(): return lax.ppermute(x, axis, [(i, i ^ 1) for i in range(count)])  8.48 us
    ppermute x1, starting transfers between devices, body(): lax.ppermute(other, 'rep', [(0, 1), (1, 0)])  7.62 us
    dot_general x1, matrix products, body(): jnp.dot(coefficient, window, preferred_element_type=jnp.float32)  6.12 us
    ppermute x4, waiting for transfers between devices, swapped(): return lax.ppermute(x, axis, [(i, i ^ 1) for i in range(count)])  4.15 us
  transfers between devices with their start and end apart: 13, of which 7 were waited for; matrix products, arithmetic and copies ran while one was open for 15% of the time, Pallas kernels for 0%

profile of v6, /device:TPU:1, one launch (start us, length us, event | category | flops | bytes accessed | tf_op | source)
XLA Modules:
  0.0 140.7 jit_solution(149779616738158531)
XLA Ops:
  0.7 3.3 %collective-permute-start = (bf16[128,1024]{1,0:T(8,128)(2,1)}, bf16[128,1024]{1,0:T(8,128)(2,1)}, u32[]{:S(2)}, u32[]{:S(2)}) collective-permute-start(bf16[128,1024]{1,0:T(8,128)(2,1)} %param.6), channel_id=1, source_target_pairs={{0,2},{2,0},{4,6},{6,4},{8,10},{10,8},{12,14},{14,12},{16,18},{18,... | collective-permute-start | bytes 786440 | tf_op jit(solution)/shard_map/ppermute | solution.py:19
  3.9 1.3 collective-permute-start.1
  5.2 7.7 %collective-permute-start.2 = (bf16[128,1024]{1,0:T(8,128)(2,1)}, bf16[128,1024]{1,0:T(8,128)(2,1)S(1)}, u32[]{:S(2)}, u32[]{:S(2)}) collective-permute-start(bf16[128,1024]{1,0:T(8,128)(2,1)} %param.6), channel_id=1, source_target_pairs={{0,252},{2,254},{4,0},{6,2},{8,4},{10,6},{12,8},{14,10},{16,12},{1... | collective-permute-start | bytes 786440 | tf_op jit(solution)/shard_map/ppermute | solution.py:14
  12.9 1.3 fusion.23
  14.3 0.7 fusion.35
  15.0 0.1 broadcast_bitcast_fusion.16
  15.2 0.1 broadcast_bitcast_fusion.2
  15.3 0.1 broadcast_bitcast_fusion.12
  15.4 0.1 broadcast_bitcast_fusion.14
  15.4 0.1 broadcast_bitcast_fusion.6
  15.5 1.8 %select_reduce_fusion.26 = (f32[1024]{0:T(1024)S(1)}, f32[1024,128]{0,1:T(8,128)S(1)}) fusion(pred[1024]{0:T(1024)(128)(4,1)S(1)} %get-tuple-element.142, bf16[1024,1024]{1,0:T(8,128)(2,1)S(1)} %copy-done, bf16[128,1024]{1,0:T(8,128)(2,1)} %param.6), kind=kOutput, calls=%fused_computation.74 | convolution fusion | flops 268827648 | bytes 2888704 | tf_op jit(solution)/shard_map/dot_general | solution.py:70
  17.3 0.1 broadcast_bitcast_fusion
  17.4 0.1 broadcast_bitcast_fusion.5
  17.5 0.1 broadcast_bitcast_fusion.3
  17.7 4.0 %collective-permute-done.1 = bf16[128,1024]{1,0:T(8,128)(2,1)S(1)} collective-permute-done((bf16[128,1024]{1,0:T(8,128)(2,1)}, bf16[128,1024]{1,0:T(8,128)(2,1)S(1)}, u32[]{:S(2)}, u32[]{:S(2)}) %collective-permute-start.1) | collective-permute-done | bytes 262176 | tf_op jit(solution)/shard_map/ppermute | solution.py:14
  21.8 3.8 %collective-permute-start.3 = (bf16[256,1024]{1,0:T(8,128)(2,1)S(1)}, bf16[256,1024]{1,0:T(8,128)(2,1)S(1)}, u32[]{:S(2)}, u32[]{:S(2)}) collective-permute-start(bf16[256,1024]{1,0:T(8,128)(2,1)S(1)} %pad_maximum_fusion.1), channel_id=1, source_target_pairs={{0,2},{2,0},{4,6},{6,4},{8,10},{10,8},{12,14},{14,12},{16,18},{18,... | collective-permute-start | bytes 1572872 | tf_op jit(solution)/shard_map/ppermute | solution.py:19
  25.5 0.5 collective-permute-start.4
  26.0 8.0 %collective-permute-start.5 = (bf16[128,1024]{1,0:T(8,128)(2,1)S(1)}, bf16[128,1024]{1,0:T(8,128)(2,1)S(1)}, u32[]{:S(2)}, u32[]{:S(2)}) collective-permute-start(bf16[128,1024]{1,0:T(8,128)(2,1)S(1)} %collective-permute-done.2), channel_id=1, source_target_pairs={{0,252},{2,254},{4,0},{6,2},{8,4},{10,6},{12,8},{14,10},{16,12},{1... | collective-permute-start | bytes 786440 | tf_op jit(solution)/shard_map/ppermute | solution.py:14
  34.0 1.8 %select_reduce_fusion.25 = (f32[1024]{0:T(1024)S(1)}, f32[1024,128]{0,1:T(8,128)S(1)}) fusion(pred[1024]{0:T(1024)(128)(4,1)S(1)} %broadcast_bitcast_fusion.16, bf16[1024,1024]{1,0:T(8,128)(2,1)S(1)} %copy-done, bf16[128,1024]{1,0:T(8,128)(2,1)} %collective-permute-done), kind=kOutput, calls=%fused_computation.73 | convolution fusion | flops 268827648 | bytes 2888704 | tf_op jit(solution)/shard_map/dot_general | solution.py:70
  35.8 1.0 constant_dynamic-update-slice_fusion.15
  36.8 0.8 select_reduce_fusion.23
  37.7 0.8 select_reduce_fusion.24
  38.5 1.5 %collective-permute-done.5 = bf16[128,1024]{1,0:T(8,128)(2,1)S(1)} collective-permute-done((bf16[128,1024]{1,0:T(8,128)(2,1)S(1)}, bf16[128,1024]{1,0:T(8,128)(2,1)S(1)}, u32[]{:S(2)}, u32[]{:S(2)}) %collective-permute-start.5) | collective-permute-done | bytes 262176 | tf_op jit(solution)/shard_map/ppermute | solution.py:14
  40.1 0.8 select_reduce_fusion.19
  40.9 5.1 %collective-permute-done.4 = bf16[128,1024]{1,0:T(8,128)(2,1)S(1)} collective-permute-done((bf16[128,1024]{1,0:T(8,128)(2,1)S(1)}, bf16[128,1024]{1,0:T(8,128)(2,1)S(1)}, u32[]{:S(2)}, u32[]{:S(2)}) %collective-permute-start.4) | collective-permute-done | bytes 262176 | tf_op jit(solution)/shard_map/ppermute | solution.py:14
  46.0 0.8 select_reduce_fusion.20
  47.0 1.3 collective-permute-start.6
  48.3 0.8 select_reduce_fusion.21
  49.2 0.8 select_reduce_fusion.22
  50.0 0.8 select_reduce_fusion.18
  51.0 0.2 select_reduce_fusion.6
  51.2 0.8 select_reduce_fusion.7
  52.0 0.8 select_reduce_fusion.8
  52.8 0.6 add_subtract_fusion
  53.5 0.2 constant_dynamic-update-slice_fusion.8
  53.6 0.2 constant_dynamic-update-slice_fusion.22
  53.8 0.2 constant_dynamic-update-slice_fusion.6
  54.0 0.2 constant_dynamic-update-slice_fusion.5
  54.2 0.2 constant_dynamic-update-slice_fusion.21
  54.4 0.2 constant_dynamic-update-slice_fusion.20
  54.6 0.2 constant_dynamic-update-slice_fusion.19
  54.8 0.2 constant_dynamic-update-slice_fusion.18
  55.0 0.2 constant_dynamic-update-slice_fusion.17
  55.2 1.4 copy-done.7
  56.6 1.8 %fusion.37 = f32[768,1024]{1,0:T(8,128)S(1)} fusion(bf16[1024,768]{0,1:T(8,128)(2,1)S(1)} %get-tuple-element.80, bf16[1024,1024]{1,0:T(8,128)(2,1)S(1)} %copy-done), kind=kOutput, calls=%fused_computation.164 | convolution fusion | flops 1610612736 | bytes 6815744 | tf_op jit(solution)/shard_map/dot_general | solution.py:97
  58.4 0.2 slice.71
  58.6 0.2 pad_maximum_fusion
  58.9 0.1 collective-permute-start.7
  59.0 4.1 %collective-permute-done.7 = f32[512,1024]{1,0:T(8,128)S(1)} collective-permute-done((f32[512,1024]{1,0:T(8,128)S(1)}, f32[512,1024]{1,0:T(8,128)S(1)}, u32[]{:S(2)}, u32[]{:S(2)}) %collective-permute-start.7) | collective-permute-done | bytes 2097184 | tf_op jit(solution)/shard_map/ppermute | solution.py:19
  63.1 0.2 slice_add_fusion.2
  63.3 0.1 collective-permute-start.8
  63.4 8.6 %collective-permute-start.10 = (f32[128,1024]{1,0:T(8,128)S(1)}, f32[128,1024]{1,0:T(8,128)S(1)}, u32[]{:S(2)}, u32[]{:S(2)}) collective-permute-start(f32[128,1024]{1,0:T(8,128)S(1)} %get-tuple-element.77), channel_id=1, source_target_pairs={{0,252},{2,254},{4,0},{6,2},{8,4},{10,6},{12,8},{14,10},{16,12},{1... | collective-permute-start | bytes 1572872 | tf_op jit(solution)/shard_map/ppermute | solution.py:14
  71.9 1.0 fusion.3
  72.9 22.5 %collective-permute-done.8 = f32[128,1024]{1,0:T(8,128)S(1)} collective-permute-done((f32[128,1024]{1,0:T(8,128)S(1)}, f32[128,1024]{1,0:T(8,128)S(1)}, u32[]{:S(2)}, u32[]{:S(2)}) %collective-permute-start.8) | collective-permute-done | bytes 524320 | tf_op jit(solution)/shard_map/ppermute | solution.py:14
  95.5 1.3 fusion.10
  96.8 1.3 collective-permute-start.11
  98.0 1.1 collective-permute-start.9
  99.1 0.7 constant_dynamic-update-slice_fusion.9
  99.8 14.8 %collective-permute-done.11 = f32[128,1024]{1,0:T(8,128)S(1)} collective-permute-done((f32[128,1024]{1,0:T(8,128)}, f32[128,1024]{1,0:T(8,128)S(1)}, u32[]{:S(2)}, u32[]{:S(2)}) %collective-permute-start.11) | collective-permute-done | bytes 524320 | tf_op jit(solution)/shard_map/ppermute | solution.py:14
  114.7 10.2 %collective-permute-done.9 = f32[128,1024]{1,0:T(8,128)S(1)} collective-permute-done((f32[128,1024]{1,0:T(8,128)}, f32[128,1024]{1,0:T(8,128)S(1)}, u32[]{:S(2)}, u32[]{:S(2)}) %collective-permute-start.9) | collective-permute-done | bytes 524320 | tf_op jit(solution)/shard_map/ppermute | solution.py:14
  124.9 1.3 fusion.12
  126.2 7.6 %collective-permute-start.12 = (f32[64,1024]{1,0:T(8,128)S(1)}, f32[64,1024]{1,0:T(8,128)S(1)}, u32[]{:S(2)}, u32[]{:S(2)}) collective-permute-start(f32[64,1024]{1,0:T(8,128)S(1)} %slice_select_fusion), channel_id=1, source_target_pairs={{0,1},{1,0},{2,3},{3,2},{4,5},{5,4},{6,7},{7,6},{8,9},{9,8},{10,11... | collective-permute-start | bytes 786440 | tf_op jit(solution)/shard_map/ppermute | solution.py:127
  133.9 6.1 %convolution_multiply_fusion = f32[1024,1024]{1,0:T(8,128)} fusion(bf16[1024,1152]{0,1:T(8,128)(2,1)} %copy-done.7, bf16[1152,1024]{1,0:T(8,128)(2,1)S(1)} %copy-done.6), kind=kOutput, calls=%fused_computation | convolution fusion | flops 2416967680 | bytes 8912896 | tf_op jit(solution)/shard_map/dot_general | solution.py:91
  140.0 0.7 add_multiply_fusion
  (36 shorter events, 0.7 us)
Async XLA Ops:
  0.6 14.9 %copy-start = (bf16[1024,1024]{1,0:T(8,128)(2,1)S(1)}, bf16[1024,1024]{1,0:T(8,128)(2,1)}, u32[]{:S(2)}) copy-start(bf16[1024,1024]{1,0:T(8,128)(2,1)} %param.5) | copy-start | bytes 6291460
  0.6 17.0 %copy-start.4 = (bf16[128,1024]{1,0:T(8,128)(2,1)S(1)}, bf16[128,1024]{1,0:T(8,128)(2,1)}, u32[]{:S(2)}) copy-start(bf16[128,1024]{1,0:T(8,128)(2,1)} %param.6) | copy-start | bytes 786436
  0.7 33.4 %collective-permute-start = (bf16[128,1024]{1,0:T(8,128)(2,1)}, bf16[128,1024]{1,0:T(8,128)(2,1)}, u32[]{:S(2)}, u32[]{:S(2)}) collective-permute-start(bf16[128,1024]{1,0:T(8,128)(2,1)} %param.6), channel_id=1, source_target_pairs={{0,2},{2,0},{4,6},{6,4},{8,10},{10,8},{12,14},{14,12},{16,18},{18,... | collective-permute-start | bytes 786440 | tf_op jit(solution)/shard_map/ppermute | solution.py:19
  3.9 17.8 %collective-permute-start.1 = (bf16[128,1024]{1,0:T(8,128)(2,1)}, bf16[128,1024]{1,0:T(8,128)(2,1)S(1)}, u32[]{:S(2)}, u32[]{:S(2)}) collective-permute-start(bf16[128,1024]{1,0:T(8,128)(2,1)} %param.6), channel_id=1, source_target_pairs={{0,4},{2,6},{4,8},{6,10},{8,12},{10,14},{12,16},{14,18},{16,20},{1... | collective-permute-start | bytes 786440 | tf_op jit(solution)/shard_map/ppermute | solution.py:14
  5.2 16.5 %collective-permute-start.2 = (bf16[128,1024]{1,0:T(8,128)(2,1)}, bf16[128,1024]{1,0:T(8,128)(2,1)S(1)}, u32[]{:S(2)}, u32[]{:S(2)}) collective-permute-start(bf16[128,1024]{1,0:T(8,128)(2,1)} %param.6), channel_id=1, source_target_pairs={{0,252},{2,254},{4,0},{6,2},{8,4},{10,6},{12,8},{14,10},{16,12},{1... | collective-permute-start | bytes 786440 | tf_op jit(solution)/shard_map/ppermute | solution.py:14
  21.8 25.1 %collective-permute-start.3 = (bf16[256,1024]{1,0:T(8,128)(2,1)S(1)}, bf16[256,1024]{1,0:T(8,128)(2,1)S(1)}, u32[]{:S(2)}, u32[]{:S(2)}) collective-permute-start(bf16[256,1024]{1,0:T(8,128)(2,1)S(1)} %pad_maximum_fusion.1), channel_id=1, source_target_pairs={{0,2},{2,0},{4,6},{6,4},{8,10},{10,8},{12,14},{14,12},{16,18},{18,... | collective-permute-start | bytes 1572872 | tf_op jit(solution)/shard_map/ppermute | solution.py:19
  25.5 20.5 %collective-permute-start.4 = (bf16[128,1024]{1,0:T(8,128)(2,1)S(1)}, bf16[128,1024]{1,0:T(8,128)(2,1)S(1)}, u32[]{:S(2)}, u32[]{:S(2)}) collective-permute-start(bf16[128,1024]{1,0:T(8,128)(2,1)S(1)} %collective-permute-done.1), channel_id=1, source_target_pairs={{0,4},{2,6},{4,8},{6,10},{8,12},{10,14},{12,16},{14,18},{16,20},{1... | collective-permute-start | bytes 786440 | tf_op jit(solution)/shard_map/ppermute | solution.py:14
  26.0 14.1 %collective-permute-start.5 = (bf16[128,1024]{1,0:T(8,128)(2,1)S(1)}, bf16[128,1024]{1,0:T(8,128)(2,1)S(1)}, u32[]{:S(2)}, u32[]{:S(2)}) collective-permute-start(bf16[128,1024]{1,0:T(8,128)(2,1)S(1)} %collective-permute-done.2), channel_id=1, source_target_pairs={{0,252},{2,254},{4,0},{6,2},{8,4},{10,6},{12,8},{14,10},{16,12},{1... | collective-permute-start | bytes 786440 | tf_op jit(solution)/shard_map/ppermute | solution.py:14
  47.0 3.0 %copy-start.5 = (bf16[1152,1024]{1,0:T(8,128)(2,1)}, bf16[1152,1024]{1,0:T(8,128)(2,1)S(1)}, u32[]{:S(2)}) copy-start(bf16[1152,1024]{1,0:T(8,128)(2,1)S(1)} %get-tuple-element.92) | copy-start | bytes 7077892
  47.0 3.0 %collective-permute-start.6 = (bf16[128,1024]{1,0:T(8,128)(2,1)S(1)}, bf16[128,1024]{1,0:T(8,128)(2,1)S(1)}, u32[]{:S(2)}, u32[]{:S(2)}) collective-permute-start(bf16[128,1024]{1,0:T(8,128)(2,1)S(1)} %get-tuple-element.93), channel_id=1, source_target_pairs={{0,2},{2,0},{4,6},{6,4},{8,10},{10,8},{12,14},{14,12},{16,18},{18,... | collective-permute-start | bytes 786440 | tf_op jit(solution)/shard_map/ppermute | solution.py:19
  51.2 2.2 %copy-start.3 = (f32[1024]{0:T(1024)S(1)}, f32[1024]{0:T(1024)}, u32[]{:S(2)}) copy-start(f32[1024]{0:T(1024)} %param.9) | copy-start | bytes 12292
  55.2 1.4 %copy-start.7 = (bf16[1024,1152]{0,1:T(8,128)(2,1)}, bf16[1024,1152]{0,1:T(8,128)(2,1)S(1)}, u32[]{:S(2)}) copy-start(bf16[1024,1152]{0,1:T(8,128)(2,1)S(1)} %get-tuple-element.81) | copy-start | bytes 7077892
  58.9 4.2 %collective-permute-start.7 = (f32[512,1024]{1,0:T(8,128)S(1)}, f32[512,1024]{1,0:T(8,128)S(1)}, u32[]{:S(2)}, u32[]{:S(2)}) collective-permute-start(f32[512,1024]{1,0:T(8,128)S(1)} %pad_maximum_fusion), channel_id=1, source_target_pairs={{0,2},{2,0},{4,6},{6,4},{8,10},{10,8},{12,14},{14,12},{16,18},{18,... | collective-permute-start | bytes 6291464 | tf_op jit(solution)/shard_map/ppermute | solution.py:19
  63.1 32.4 %copy-start.1 = (f32[512,1024]{1,0:T(8,128)}, f32[512,1024]{1,0:T(8,128)S(1)}, u32[]{:S(2)}) copy-start(f32[512,1024]{1,0:T(8,128)S(1)} %collective-permute-done.7) | copy-start | bytes 6291460
  63.3 32.2 %collective-permute-start.8 = (f32[128,1024]{1,0:T(8,128)S(1)}, f32[128,1024]{1,0:T(8,128)S(1)}, u32[]{:S(2)}, u32[]{:S(2)}) collective-permute-start(f32[128,1024]{1,0:T(8,128)S(1)} %get-tuple-element.76), channel_id=1, source_target_pairs={{0,4},{2,6},{4,8},{6,10},{8,12},{10,14},{12,16},{14,18},{16,20},{1... | collective-permute-start | bytes 1572872 | tf_op jit(solution)/shard_map/ppermute | solution.py:14
  63.4 32.1 %collective-permute-start.10 = (f32[128,1024]{1,0:T(8,128)S(1)}, f32[128,1024]{1,0:T(8,128)S(1)}, u32[]{:S(2)}, u32[]{:S(2)}) collective-permute-start(f32[128,1024]{1,0:T(8,128)S(1)} %get-tuple-element.77), channel_id=1, source_target_pairs={{0,252},{2,254},{4,0},{6,2},{8,4},{10,6},{12,8},{14,10},{16,12},{1... | collective-permute-start | bytes 1572872 | tf_op jit(solution)/shard_map/ppermute | solution.py:14
  72.9 23.8 %copy-start.2 = (f32[384,1024]{1,0:T(8,128)}, f32[384,1024]{1,0:T(8,128)S(1)}, u32[]{:S(2)}) copy-start(f32[384,1024]{1,0:T(8,128)S(1)} %fusion.3) | copy-start | bytes 4718596
  96.8 17.9 %collective-permute-start.11 = (f32[128,1024]{1,0:T(8,128)}, f32[128,1024]{1,0:T(8,128)S(1)}, u32[]{:S(2)}, u32[]{:S(2)}) collective-permute-start(f32[128,1024]{1,0:T(8,128)} %get-tuple-element.79), channel_id=1, source_target_pairs={{0,252},{2,254},{4,0},{6,2},{8,4},{10,6},{12,8},{14,10},{16,12},{1... | collective-permute-start | bytes 1572872 | tf_op jit(solution)/shard_map/ppermute | solution.py:14
  98.0 26.8 %collective-permute-start.9 = (f32[128,1024]{1,0:T(8,128)}, f32[128,1024]{1,0:T(8,128)S(1)}, u32[]{:S(2)}, u32[]{:S(2)}) collective-permute-start(f32[128,1024]{1,0:T(8,128)} %get-tuple-element.78), channel_id=1, source_target_pairs={{0,4},{2,6},{4,8},{6,10},{8,12},{10,14},{12,16},{14,18},{16,20},{1... | collective-permute-start | bytes 1572872 | tf_op jit(solution)/shard_map/ppermute | solution.py:14
  99.8 34.0 %copy-start.6 = (bf16[1152,1024]{1,0:T(8,128)(2,1)S(1)}, bf16[1152,1024]{1,0:T(8,128)(2,1)}, u32[]{:S(2)}) copy-start(bf16[1152,1024]{1,0:T(8,128)(2,1)} %constant_dynamic-update-slice_fusion.9) | copy-start | bytes 7077892
  126.2 13.8 %collective-permute-start.12 = (f32[64,1024]{1,0:T(8,128)S(1)}, f32[64,1024]{1,0:T(8,128)S(1)}, u32[]{:S(2)}, u32[]{:S(2)}) collective-permute-start(f32[64,1024]{1,0:T(8,128)S(1)} %slice_select_fusion), channel_id=1, source_target_pairs={{0,1},{1,0},{2,3},{3,2},{4,5},{5,4},{6,7},{7,6},{8,9},{9,8},{10,11... | collective-permute-start | bytes 786440 | tf_op jit(solution)/shard_map/ppermute | solution.py:127

commit v7 on v2

--- a/solution.py
+++ b/solution.py
@@ -32,10 +32,10 @@
     inner_idx = jnp.arange(tile_rows, dtype=jnp.int32)
     same_row = inner_idx[:, None] == inner_idx[None, :]
 
+    up2 = passed_along(keys, "dp", -2)
     down2 = passed_along(keys, "dp", 2)
-    up2 = passed_along(keys, "dp", -2)
+    up4 = passed_along(up2, "dp", -2)
     down4 = passed_along(down2, "dp", 2)
-    up4 = passed_along(up2, "dp", -2)
     sw_own = swapped(keys, "dp")
     sw_down2 = swapped(down2, "dp")
     sw_up2 = swapped(up2, "dp")
@@ -101,13 +101,13 @@
     zero = jnp.zeros_like(back_far)
     far_up = key_parts["up4"] + jnp.where(core == 0, back_far, zero)
     far_down = key_parts["down4"] + jnp.where(core == 0, zero, back_far)
+    near_down = key_parts["down2"] + back_down2 + passed_along(far_down, "dp", -2)
     near_up = key_parts["up2"] + back_up2 + passed_along(far_up, "dp", 2)
-    near_down = key_parts["down2"] + back_down2 + passed_along(far_down, "dp", -2)
     total = (
         key_parts["own"]
         + back_own
+        + passed_along(near_down, "dp", -2)
         + passed_along(near_up, "dp", 2)
-        + passed_along(near_down, "dp", -2)
     )
     half = tile_rows // 2
     halves = total.reshape(2, half, total.shape[1])

time: 134 us -> 139 us (1.037)
  waiting for transfers between devices: 48.1 us -> 58.8 us
  starting transfers between devices: 46.1 us -> 40.6 us
    ppermute x8, waiting for transfers between devices: 45.5 us -> 56.3 us  [passed_along(): return lax.ppermute(x, axis, [(i, (i + by) % count) for i in range(count)])]
    ppermute x8, starting transfers between devices: 35.9 us -> 30.4 us  [passed_along(): return lax.ppermute(x, axis, [(i, (i + by) % count) for i in range(count)])]
  transfers between devices with their start and end apart: 17 -> 17, of which waited for: 6 -> 8; matrix products, arithmetic and copies ran while one was open for 19% -> 18% of each run, Pallas kernels for 0% -> 0%
where the time goes in v7:
time: 139 us
  waiting for transfers between devices  58.8 us (42%)
  starting transfers between devices  40.6 us (29%)
  matrix products  17.3 us (12%)
  other arithmetic  10.6 us (8%)
  local copies, waits for them, and re-layouts  10.5 us (8%)
    ppermute x8, waiting for transfers between devices, passed_along(): return lax.ppermute(x, axis, [(i, (i + by) % count) for i in range(count)])  56.3 us
    ppermute x8, starting transfers between devices, passed_along(): return lax.ppermute(x, axis, [(i, (i + by) % count) for i in range(count)])  30.4 us
    ppermute x8, starting transfers between devices, swapped(): return lax.ppermute(x, axis, [(i, i ^ 1) for i in range(count)])  10.1 us
    dot_general x9, matrix products, body(): lax.dot_general(queries, key_tile, (((1,), (1,)), ((), ())), preferred_el...  8.52 us
    unnamed x17, local copies, waits for them, and re-layouts  7.5 us
    dot_general x1, matrix products, body(): jnp.dot(coefficient, window, preferred_element_type=jnp.float32)  6.13 us
  transfers between devices with their start and end apart: 17, of which 8 were waited for; matrix products, arithmetic and copies ran while one was open for 18% of the time, Pallas kernels for 0%

profile of v7, /device:TPU:1, one launch (start us, length us, event | category | flops | bytes accessed | tf_op | source)
XLA Modules:
  0.0 138.6 jit_solution(13541067891145434106)
XLA Ops:
  0.6 3.9 %collective-permute-start.1 = (bf16[128,1024]{1,0:T(8,128)(2,1)}, bf16[128,1024]{1,0:T(8,128)(2,1)S(1)}, u32[]{:S(2)}, u32[]{:S(2)}) collective-permute-start(bf16[128,1024]{1,0:T(8,128)(2,1)} %param.6), channel_id=1, source_target_pairs={{0,4},{2,6},{4,8},{6,10},{8,12},{10,14},{12,16},{14,18},{16,20},{1... | collective-permute-start | bytes 786440 | tf_op jit(solution)/shard_map/ppermute | solution.py:14
  4.5 1.0 collective-permute-start
  5.5 7.5 %collective-permute-start.2 = (bf16[128,1024]{1,0:T(8,128)(2,1)}, bf16[128,1024]{1,0:T(8,128)(2,1)S(1)}, u32[]{:S(2)}, u32[]{:S(2)}) collective-permute-start(bf16[128,1024]{1,0:T(8,128)(2,1)} %param.6), channel_id=1, source_target_pairs={{0,252},{2,254},{4,0},{6,2},{8,4},{10,6},{12,8},{14,10},{16,12},{1... | collective-permute-start | bytes 786440 | tf_op jit(solution)/shard_map/ppermute | solution.py:14
  13.0 1.7 %constant_dynamic-update-slice_fusion.8 = bf16[1152,1024]{1,0:T(8,128)(2,1)} fusion(bf16[128,1024]{1,0:T(8,128)(2,1)} %param.6), kind=kLoop, calls=%fused_computation.86 | loop fusion | bytes 524288
  14.7 1.3 fusion.22
  16.0 0.7 fusion.33
  16.8 0.1 broadcast_bitcast_fusion.17
  17.9 1.8 %select_reduce_fusion.26 = (f32[1024]{0:T(1024)S(1)}, f32[1024,128]{0,1:T(8,128)S(1)}) fusion(pred[1024]{0:T(1024)(128)(4,1)S(1)} %broadcast_bitcast_fusion.17, bf16[1024,1024]{1,0:T(8,128)(2,1)S(1)} %copy-done, bf16[128,1024]{1,0:T(8,128)(2,1)} %param.6), kind=kOutput, calls=%fused_computation.64 | convolution fusion | flops 268827648 | bytes 2888704 | tf_op jit(solution)/shard_map/dot_general | solution.py:69
  19.7 0.3 collective-permute-done.1
  20.0 0.2 collective-permute-start.5
  20.1 1.5 %collective-permute-start.3 = (bf16[128,1024]{1,0:T(8,128)(2,1)S(1)}, bf16[128,1024]{1,0:T(8,128)(2,1)S(1)}, u32[]{:S(2)}, u32[]{:S(2)}) collective-permute-start(bf16[128,1024]{1,0:T(8,128)(2,1)S(1)} %collective-permute-done.1), channel_id=1, source_target_pairs={{0,2},{2,0},{4,6},{6,4},{8,10},{10,8},{12,14},{14,12},{16,18},{18,... | collective-permute-start | bytes 786440 | tf_op jit(solution)/shard_map/ppermute | solution.py:19
  21.7 0.5 collective-permute-done.2
  22.2 7.9 %collective-permute-start.6 = (bf16[128,1024]{1,0:T(8,128)(2,1)S(1)}, bf16[128,1024]{1,0:T(8,128)(2,1)S(1)}, u32[]{:S(2)}, u32[]{:S(2)}) collective-permute-start(bf16[128,1024]{1,0:T(8,128)(2,1)S(1)} %collective-permute-done.2), channel_id=1, source_target_pairs={{0,252},{2,254},{4,0},{6,2},{8,4},{10,6},{12,8},{14,10},{16,12},{1... | collective-permute-start | bytes 786440 | tf_op jit(solution)/shard_map/ppermute | solution.py:14
  30.1 4.2 %collective-permute-start.4 = (bf16[128,1024]{1,0:T(8,128)(2,1)S(1)}, bf16[128,1024]{1,0:T(8,128)(2,1)S(1)}, u32[]{:S(2)}, u32[]{:S(2)}) collective-permute-start(bf16[128,1024]{1,0:T(8,128)(2,1)S(1)} %collective-permute-done.2), channel_id=1, source_target_pairs={{0,2},{2,0},{4,6},{6,4},{8,10},{10,8},{12,14},{14,12},{16,18},{18,... | collective-permute-start | bytes 786440 | tf_op jit(solution)/shard_map/ppermute | solution.py:19
  34.2 0.8 select_reduce_fusion.23
  35.1 0.8 select_reduce_fusion.24
  36.0 0.8 select_reduce_fusion.25
  36.8 0.7 constant_dynamic-update-slice_fusion.7
  37.5 0.7 constant_dynamic-update-slice_fusion.6
  38.3 0.7 constant_dynamic-update-slice_fusion.5
  39.0 0.7 constant_dynamic-update-slice_fusion.4
  39.7 0.7 constant_dynamic-update-slice_fusion.3
  40.5 0.7 constant_dynamic-update-slice_fusion.2
  41.2 0.8 constant_dynamic-update-slice_fusion.1
  42.0 2.5 %collective-permute-start.7 = (bf16[128,1024]{1,0:T(8,128)(2,1)S(1)}, bf16[128,1024]{1,0:T(8,128)(2,1)S(1)}, u32[]{:S(2)}, u32[]{:S(2)}) collective-permute-start(bf16[128,1024]{1,0:T(8,128)(2,1)S(1)} %get-tuple-element.79), channel_id=1, source_target_pairs={{0,2},{2,0},{4,6},{6,4},{8,10},{10,8},{12,14},{14,12},{16,18},{18,... | collective-permute-start | bytes 786440 | tf_op jit(solution)/shard_map/ppermute | solution.py:19
  44.5 0.8 select_reduce_fusion.21
  45.3 0.8 select_reduce_fusion.19
  46.2 0.8 select_reduce_fusion.22
  47.0 0.8 select_reduce_fusion.20
  47.9 0.8 select_reduce_fusion.18
  48.9 0.2 select_reduce_fusion.6
  49.1 0.8 select_reduce_fusion.8
  49.9 0.8 select_reduce_fusion.7
  50.7 0.6 add_subtract_fusion
  51.3 0.2 fusion.5
  51.5 0.2 fusion.6
  51.7 0.2 fusion.7
  51.9 0.2 fusion.8
  52.1 0.2 fusion.9
  52.3 0.2 fusion.10
  52.5 0.2 fusion.11
  52.7 0.2 fusion.12
  52.8 0.2 fusion.13
  53.0 1.4 %copy-done.3 = bf16[1024,1152]{0,1:T(8,128)(2,1)} copy-done((bf16[1024,1152]{0,1:T(8,128)(2,1)}, bf16[1024,1152]{0,1:T(8,128)(2,1)S(1)}, u32[]{:S(2)}) %copy-start.3) | copy-done | bytes 2359320
  54.4 2.6 %fusion.36 = f32[1152,1024]{1,0:T(8,128)S(1)} fusion(bf16[1024,1152]{0,1:T(8,128)(2,1)S(1)} %fusion.13, bf16[1024,1024]{1,0:T(8,128)(2,1)S(1)} %copy-done), kind=kOutput, calls=%fused_computation.147 | convolution fusion | flops 2415919104 | bytes 9175040 | tf_op jit(solution)/shard_map/dot_general | solution.py:91
  57.1 1.1 fusion.35
  58.2 0.5 collective-permute-start.13
  58.7 1.4 %collective-permute-done.10 = f32[128,1024]{1,0:T(8,128)S(1)} collective-permute-done((f32[128,1024]{1,0:T(8,128)S(1)}, f32[128,1024]{1,0:T(8,128)S(1)}, u32[]{:S(2)}, u32[]{:S(2)}) %collective-permute-start.10) | collective-permute-done | bytes 524320 | tf_op jit(solution)/shard_map/ppermute | solution.py:19
  60.1 0.1 slice_add_fusion.2
  60.2 8.6 %collective-permute-start.11 = (f32[128,1024]{1,0:T(8,128)S(1)}, f32[128,1024]{1,0:T(8,128)S(1)}, u32[]{:S(2)}, u32[]{:S(2)}) collective-permute-start(f32[128,1024]{1,0:T(8,128)S(1)} %get-tuple-element.70), channel_id=1, source_target_pairs={{0,252},{2,254},{4,0},{6,2},{8,4},{10,6},{12,8},{14,10},{16,12},{1... | collective-permute-start | bytes 1572872 | tf_op jit(solution)/shard_map/ppermute | solution.py:14
  68.8 0.4 collective-permute-start.8
  69.2 21.4 %collective-permute-done.11 = f32[128,1024]{1,0:T(8,128)S(1)} collective-permute-done((f32[128,1024]{1,0:T(8,128)S(1)}, f32[128,1024]{1,0:T(8,128)S(1)}, u32[]{:S(2)}, u32[]{:S(2)}) %collective-permute-start.11) | collective-permute-done | bytes 524320 | tf_op jit(solution)/shard_map/ppermute | solution.py:14
  90.6 6.9 %collective-permute-done.14 = f32[128,1024]{1,0:T(8,128)S(1)} collective-permute-done((f32[128,1024]{1,0:T(8,128)S(1)}, f32[128,1024]{1,0:T(8,128)S(1)}, u32[]{:S(2)}, u32[]{:S(2)}) %collective-permute-start.14) | collective-permute-done | bytes 524320 | tf_op jit(solution)/shard_map/ppermute | solution.py:14
  97.6 1.3 fusion.2
  98.9 1.7 %collective-permute-start.12 = (f32[128,1024]{1,0:T(8,128)}, f32[128,1024]{1,0:T(8,128)S(1)}, u32[]{:S(2)}, u32[]{:S(2)}) collective-permute-start(f32[128,1024]{1,0:T(8,128)} %get-tuple-element.76), channel_id=1, source_target_pairs={{0,252},{2,254},{4,0},{6,2},{8,4},{10,6},{12,8},{14,10},{16,12},{1... | collective-permute-start | bytes 1572872 | tf_op jit(solution)/shard_map/ppermute | solution.py:14
  100.6 0.6 collective-permute-start.15
  101.3 0.7 constant_dynamic-update-slice_fusion
  102.0 10.6 %collective-permute-done.12 = f32[128,1024]{1,0:T(8,128)S(1)} collective-permute-done((f32[128,1024]{1,0:T(8,128)}, f32[128,1024]{1,0:T(8,128)S(1)}, u32[]{:S(2)}, u32[]{:S(2)}) %collective-permute-start.12) | collective-permute-done | bytes 524320 | tf_op jit(solution)/shard_map/ppermute | solution.py:14
  112.6 16.5 %collective-permute-done.15 = f32[128,1024]{1,0:T(8,128)} collective-permute-done((f32[128,1024]{1,0:T(8,128)}, f32[128,1024]{1,0:T(8,128)}, u32[]{:S(2)}, u32[]{:S(2)}) %collective-permute-start.15) | collective-permute-done | bytes 524320 | tf_op jit(solution)/shard_map/ppermute | solution.py:14
  129.1 1.3 fusion.4
  130.5 0.1 collective-permute-start.16
  130.6 6.1 %convolution_multiply_fusion = f32[1024,1024]{1,0:T(8,128)} fusion(bf16[1024,1152]{0,1:T(8,128)(2,1)S(1)} %copy-done.4, bf16[1152,1024]{1,0:T(8,128)(2,1)} %constant_dynamic-update-slice_fusion), kind=kOutput, calls=%fused_computation | convolution fusion | flops 2416967680 | bytes 8912896 | tf_op jit(solution)/shard_map/dot_general | solution.py:90
  136.7 1.2 collective-permute-done.16
  137.9 0.7 add_multiply_fusion
  (39 shorter events, 1.2 us)
Async XLA Ops:
  0.6 17.2 %copy-start = (bf16[1024,1024]{1,0:T(8,128)(2,1)S(1)}, bf16[1024,1024]{1,0:T(8,128)(2,1)}, u32[]{:S(2)}) copy-start(bf16[1024,1024]{1,0:T(8,128)(2,1)} %param.5) | copy-start | bytes 6291460
  0.6 19.3 %collective-permute-start.1 = (bf16[128,1024]{1,0:T(8,128)(2,1)}, bf16[128,1024]{1,0:T(8,128)(2,1)S(1)}, u32[]{:S(2)}, u32[]{:S(2)}) collective-permute-start(bf16[128,1024]{1,0:T(8,128)(2,1)} %param.6), channel_id=1, source_target_pairs={{0,4},{2,6},{4,8},{6,10},{8,12},{10,14},{12,16},{14,18},{16,20},{1... | collective-permute-start | bytes 786440 | tf_op jit(solution)/shard_map/ppermute | solution.py:14
  4.5 31.4 %collective-permute-start = (bf16[128,1024]{1,0:T(8,128)(2,1)}, bf16[128,1024]{1,0:T(8,128)(2,1)S(1)}, u32[]{:S(2)}, u32[]{:S(2)}) collective-permute-start(bf16[128,1024]{1,0:T(8,128)(2,1)} %param.6), channel_id=1, source_target_pairs={{0,2},{2,0},{4,6},{6,4},{8,10},{10,8},{12,14},{14,12},{16,18},{18,... | collective-permute-start | bytes 786440 | tf_op jit(solution)/shard_map/ppermute | solution.py:19
  5.5 16.7 %collective-permute-start.2 = (bf16[128,1024]{1,0:T(8,128)(2,1)}, bf16[128,1024]{1,0:T(8,128)(2,1)S(1)}, u32[]{:S(2)}, u32[]{:S(2)}) collective-permute-start(bf16[128,1024]{1,0:T(8,128)(2,1)} %param.6), channel_id=1, source_target_pairs={{0,252},{2,254},{4,0},{6,2},{8,4},{10,6},{12,8},{14,10},{16,12},{1... | collective-permute-start | bytes 786440 | tf_op jit(solution)/shard_map/ppermute | solution.py:14
  20.0 20.5 %collective-permute-start.5 = (bf16[128,1024]{1,0:T(8,128)(2,1)S(1)}, bf16[128,1024]{1,0:T(8,128)(2,1)S(1)}, u32[]{:S(2)}, u32[]{:S(2)}) collective-permute-start(bf16[128,1024]{1,0:T(8,128)(2,1)S(1)} %collective-permute-done.1), channel_id=1, source_target_pairs={{0,4},{2,6},{4,8},{6,10},{8,12},{10,14},{12,16},{14,18},{16,20},{1... | collective-permute-start | bytes 786440 | tf_op jit(solution)/shard_map/ppermute | solution.py:14
  20.1 18.9 %collective-permute-start.3 = (bf16[128,1024]{1,0:T(8,128)(2,1)S(1)}, bf16[128,1024]{1,0:T(8,128)(2,1)S(1)}, u32[]{:S(2)}, u32[]{:S(2)}) collective-permute-start(bf16[128,1024]{1,0:T(8,128)(2,1)S(1)} %collective-permute-done.1), channel_id=1, source_target_pairs={{0,2},{2,0},{4,6},{6,4},{8,10},{10,8},{12,14},{14,12},{16,18},{18,... | collective-permute-start | bytes 786440 | tf_op jit(solution)/shard_map/ppermute | solution.py:19
  22.2 19.0 %collective-permute-start.6 = (bf16[128,1024]{1,0:T(8,128)(2,1)S(1)}, bf16[128,1024]{1,0:T(8,128)(2,1)S(1)}, u32[]{:S(2)}, u32[]{:S(2)}) collective-permute-start(bf16[128,1024]{1,0:T(8,128)(2,1)S(1)} %collective-permute-done.2), channel_id=1, source_target_pairs={{0,252},{2,254},{4,0},{6,2},{8,4},{10,6},{12,8},{14,10},{16,12},{1... | collective-permute-start | bytes 786440 | tf_op jit(solution)/shard_map/ppermute | solution.py:14
  30.1 9.7 %collective-permute-start.4 = (bf16[128,1024]{1,0:T(8,128)(2,1)S(1)}, bf16[128,1024]{1,0:T(8,128)(2,1)S(1)}, u32[]{:S(2)}, u32[]{:S(2)}) collective-permute-start(bf16[128,1024]{1,0:T(8,128)(2,1)S(1)} %collective-permute-done.2), channel_id=1, source_target_pairs={{0,2},{2,0},{4,6},{6,4},{8,10},{10,8},{12,14},{14,12},{16,18},{18,... | collective-permute-start | bytes 786440 | tf_op jit(solution)/shard_map/ppermute | solution.py:19
  42.0 5.9 %collective-permute-start.7 = (bf16[128,1024]{1,0:T(8,128)(2,1)S(1)}, bf16[128,1024]{1,0:T(8,128)(2,1)S(1)}, u32[]{:S(2)}, u32[]{:S(2)}) collective-permute-start(bf16[128,1024]{1,0:T(8,128)(2,1)S(1)} %get-tuple-element.79), channel_id=1, source_target_pairs={{0,2},{2,0},{4,6},{6,4},{8,10},{10,8},{12,14},{14,12},{16,18},{18,... | collective-permute-start | bytes 786440 | tf_op jit(solution)/shard_map/ppermute | solution.py:19
  49.1 2.2 %copy-start.2 = (f32[1024]{0:T(1024)S(1)}, f32[1024]{0:T(1024)}, u32[]{:S(2)}) copy-start(f32[1024]{0:T(1024)} %param.9) | copy-start | bytes 12292
  53.0 1.4 %copy-start.3 = (bf16[1024,1152]{0,1:T(8,128)(2,1)}, bf16[1024,1152]{0,1:T(8,128)(2,1)S(1)}, u32[]{:S(2)}) copy-start(bf16[1024,1152]{0,1:T(8,128)(2,1)S(1)} %fusion.13) | copy-start | bytes 7077892
  57.1 40.5 %copy-start.1 = (f32[1152,1024]{1,0:T(8,128)}, f32[1152,1024]{1,0:T(8,128)S(1)}, u32[]{:S(2)}) copy-start(f32[1152,1024]{1,0:T(8,128)S(1)} %fusion.36) | copy-start | bytes 14155780
  58.2 1.9 %collective-permute-start.10 = (f32[128,1024]{1,0:T(8,128)S(1)}, f32[128,1024]{1,0:T(8,128)S(1)}, u32[]{:S(2)}, u32[]{:S(2)}) collective-permute-start(f32[128,1024]{1,0:T(8,128)S(1)} %get-tuple-element.74), channel_id=1, source_target_pairs={{0,2},{2,0},{4,6},{6,4},{8,10},{10,8},{12,14},{14,12},{16,18},{18,... | collective-permute-start | bytes 1572872 | tf_op jit(solution)/shard_map/ppermute | solution.py:19
  58.2 11.0 %collective-permute-start.13 = (f32[128,1024]{1,0:T(8,128)S(1)}, f32[128,1024]{1,0:T(8,128)S(1)}, u32[]{:S(2)}, u32[]{:S(2)}) collective-permute-start(f32[128,1024]{1,0:T(8,128)S(1)} %get-tuple-element.73), channel_id=1, source_target_pairs={{0,2},{2,0},{4,6},{6,4},{8,10},{10,8},{12,14},{14,12},{16,18},{18,... | collective-permute-start | bytes 1572872 | tf_op jit(solution)/shard_map/ppermute | solution.py:19
  58.7 10.5 %collective-permute-start.9 = (f32[128,1024]{1,0:T(8,128)S(1)}, f32[128,1024]{1,0:T(8,128)S(1)}, u32[]{:S(2)}, u32[]{:S(2)}) collective-permute-start(f32[128,1024]{1,0:T(8,128)S(1)} %get-tuple-element.75), channel_id=1, source_target_pairs={{0,2},{2,0},{4,6},{6,4},{8,10},{10,8},{12,14},{14,12},{16,18},{18,... | collective-permute-start | bytes 1572872 | tf_op jit(solution)/shard_map/ppermute | solution.py:19
  60.2 30.4 %collective-permute-start.11 = (f32[128,1024]{1,0:T(8,128)S(1)}, f32[128,1024]{1,0:T(8,128)S(1)}, u32[]{:S(2)}, u32[]{:S(2)}) collective-permute-start(f32[128,1024]{1,0:T(8,128)S(1)} %get-tuple-element.70), channel_id=1, source_target_pairs={{0,252},{2,254},{4,0},{6,2},{8,4},{10,6},{12,8},{14,10},{16,12},{1... | collective-permute-start | bytes 1572872 | tf_op jit(solution)/shard_map/ppermute | solution.py:14
  68.8 28.8 %collective-permute-start.14 = (f32[128,1024]{1,0:T(8,128)S(1)}, f32[128,1024]{1,0:T(8,128)S(1)}, u32[]{:S(2)}, u32[]{:S(2)}) collective-permute-start(f32[128,1024]{1,0:T(8,128)S(1)} %get-tuple-element.71), channel_id=1, source_target_pairs={{0,4},{2,6},{4,8},{6,10},{8,12},{10,14},{12,16},{14,18},{16,20},{1... | collective-permute-start | bytes 1572872 | tf_op jit(solution)/shard_map/ppermute | solution.py:14
  68.8 33.2 %collective-permute-start.8 = (f32[128,1024]{1,0:T(8,128)}, f32[128,1024]{1,0:T(8,128)S(1)}, u32[]{:S(2)}, u32[]{:S(2)}) collective-permute-start(f32[128,1024]{1,0:T(8,128)} %get-tuple-element.72), channel_id=1, source_target_pairs={{0,2},{2,0},{4,6},{6,4},{8,10},{10,8},{12,14},{14,12},{16,18},{18,... | collective-permute-start | bytes 1572872 | tf_op jit(solution)/shard_map/ppermute | solution.py:19
  98.9 13.7 %collective-permute-start.12 = (f32[128,1024]{1,0:T(8,128)}, f32[128,1024]{1,0:T(8,128)S(1)}, u32[]{:S(2)}, u32[]{:S(2)}) collective-permute-start(f32[128,1024]{1,0:T(8,128)} %get-tuple-element.76), channel_id=1, source_target_pairs={{0,252},{2,254},{4,0},{6,2},{8,4},{10,6},{12,8},{14,10},{16,12},{1... | collective-permute-start | bytes 1572872 | tf_op jit(solution)/shard_map/ppermute | solution.py:14
  100.6 28.4 %collective-permute-start.15 = (f32[128,1024]{1,0:T(8,128)}, f32[128,1024]{1,0:T(8,128)}, u32[]{:S(2)}, u32[]{:S(2)}) collective-permute-start(f32[128,1024]{1,0:T(8,128)} %get-tuple-element.77), channel_id=1, source_target_pairs={{0,4},{2,6},{4,8},{6,10},{8,12},{10,14},{12,16},{14,18},{16,20},{1... | collective-permute-start | bytes 1572872 | tf_op jit(solution)/shard_map/ppermute | solution.py:14
  101.3 29.3 %copy-start.4 = (bf16[1024,1152]{0,1:T(8,128)(2,1)S(1)}, bf16[1024,1152]{0,1:T(8,128)(2,1)}, u32[]{:S(2)}) copy-start(bf16[1024,1152]{0,1:T(8,128)(2,1)} %copy-done.3) | copy-start | bytes 7077892
  130.5 7.4 %collective-permute-start.16 = (f32[64,1024]{1,0:T(8,128)S(1)}, f32[64,1024]{1,0:T(8,128)S(1)}, u32[]{:S(2)}, u32[]{:S(2)}) collective-permute-start(f32[64,1024]{1,0:T(8,128)S(1)} %slice_select_fusion), channel_id=1, source_target_pairs={{0,1},{1,0},{2,3},{3,2},{4,5},{5,4},{6,7},{7,6},{8,9},{9,8},{10,11... | collective-permute-start | bytes 786440 | tf_op jit(solution)/shard_map/ppermute | solution.py:116

commit v8 on v2

--- a/solution.py
+++ b/solution.py
@@ -5,8 +5,8 @@
 from jax import lax
 from jax.sharding import PartitionSpec as P
 
+
 D = 1024
-REACH = 4
 
 
 def passed_along(x, axis, by):
@@ -19,7 +19,7 @@
     return lax.ppermute(x, axis, [(i, i ^ 1) for i in range(count)])
 
 
-def body(queries, keys, neg_mask, positive, row_weight):
+def step(queries, keys, neg_mask, positive, row_weight):
     logit_scale = 2.0 / math.sqrt(D)
     cycle_size = lax.axis_size("dp")
     cycle_index = lax.axis_index("dp")
@@ -88,12 +88,17 @@
     coefficient = jnp.concatenate(coefficients, axis=1)
     window = jnp.concatenate([key_tile for _, key_tile, _, _ in stored], axis=0)
     grad_query = logit_scale * jnp.dot(coefficient, window, preferred_element_type=jnp.float32)
-    all_parts = lax.dot_general(
-        coefficient, queries, (((0,), (0,)), ((), ())), preferred_element_type=jnp.float32
-    )
-    key_parts = {
-        name: all_parts[i * tile_rows : (i + 1) * tile_rows] for i, (name, _, _, _) in enumerate(stored)
-    }
+    order = {name: i for i, (name, _, _, _) in enumerate(stored)}
+
+    def parts_of(names):
+        cols = jnp.concatenate([coefficients[order[n]] for n in names], axis=1)
+        out = lax.dot_general(
+            cols, queries, (((0,), (0,)), ((), ())), preferred_element_type=jnp.float32
+        )
+        return {n: out[i * tile_rows : (i + 1) * tile_rows] for i, n in enumerate(names)}
+
+    key_parts = parts_of(("sw_far", "up4", "down4"))
+    key_parts.update(parts_of(("own", "sw_own", "down2", "up2", "sw_down2", "sw_up2")))
     back_own = swapped(key_parts["sw_own"], "dp")
     back_down2 = swapped(key_parts["sw_down2"], "dp")
     back_up2 = swapped(key_parts["sw_up2"], "dp")
@@ -101,8 +106,10 @@
     zero = jnp.zeros_like(back_far)
     far_up = key_parts["up4"] + jnp.where(core == 0, back_far, zero)
     far_down = key_parts["down4"] + jnp.where(core == 0, zero, back_far)
-    near_up = key_parts["up2"] + back_up2 + passed_along(far_up, "dp", 2)
-    near_down = key_parts["down2"] + back_down2 + passed_along(far_down, "dp", -2)
+    far_up_in = passed_along(far_up, "dp", 2)
+    far_down_in = passed_along(far_down, "dp", -2)
+    near_up = key_parts["up2"] + back_up2 + far_up_in
+    near_down = key_parts["down2"] + back_down2 + far_down_in
     total = (
         key_parts["own"]
         + back_own
@@ -126,7 +133,7 @@
         P(("dp", "rep")),
     )
     return jax.shard_map(
-        body,
+        step,
         mesh=mesh,
         in_specs=placed,
         out_specs=(P(("dp", "rep")), P(("dp", "rep"), None), P(("dp", "rep"), None)),

time: 134 us -> 132 us (0.985)
  waiting for transfers between devices: 48.1 us -> 46.1 us
    ppermute x8, waiting for transfers between devices: 1.41 us -> 0.02 us  [swapped(): return lax.ppermute(x, axis, [(i, i ^ 1) for i in range(count)])]
    dot_general x11 -> x12, matrix products: 17.3 us -> 17.5 us  [the longest x9 8.52 us: step(): lax.dot_general(queries, key_tile, (((1,), (1,)), ((), ())), preferred_el...]
  transfers between devices with their start and end apart: 17 -> 17, of which waited for: 6 -> 5; matrix products, arithmetic and copies ran while one was open for 19% -> 21% of each run, Pallas kernels for 0% -> 0%
where the time goes in v8:
time: 132 us
  starting transfers between devices  46.5 us (35%)
  waiting for transfers between devices  46.1 us (35%)
  matrix products  17.5 us (13%)
  other arithmetic  10.5 us (8%)
  local copies, waits for them, and re-layouts  10.3 us (8%)
    ppermute x8, waiting for transfers between devices, passed_along(): return lax.ppermute(x, axis, [(i, (i + by) % count) for i in range(count)])  44.9 us
    ppermute x8, starting transfers between devices, passed_along(): return lax.ppermute(x, axis, [(i, (i + by) % count) for i in range(count)])  35.9 us
    ppermute x8, starting transfers between devices, swapped(): return lax.ppermute(x, axis, [(i, i ^ 1) for i in range(count)])  10.6 us
    dot_general x9, matrix products, step(): lax.dot_general(queries, key_tile, (((1,), (1,)), ((), ())), preferred_el...  8.52 us
    unnamed x17, local copies, waits for them, and re-layouts  7.48 us
    dot_general x1, matrix products, step(): jnp.dot(coefficient, window, preferred_element_type=jnp.float32)  6.14 us
    dot_general x2, matrix products, parts_of(): lax.dot_general(cols, queries, (((0,), (0,)), ((), ())), preferred_elemen...  2.8 us
  transfers between devices with their start and end apart: 17, of which 5 were waited for; matrix products, arithmetic and copies ran while one was open for 21% of the time, Pallas kernels for 0%

profile of v8, /device:TPU:1, one launch (start us, length us, event | category | flops | bytes accessed | tf_op | source)
XLA Modules:
  0.0 131.8 jit_solution(1315124175833828745)
XLA Ops:
  0.6 3.9 %collective-permute-start.1 = (bf16[128,1024]{1,0:T(8,128)(2,1)}, bf16[128,1024]{1,0:T(8,128)(2,1)S(1)}, u32[]{:S(2)}, u32[]{:S(2)}) collective-permute-start(bf16[128,1024]{1,0:T(8,128)(2,1)} %param.6), channel_id=1, source_target_pairs={{0,4},{2,6},{4,8},{6,10},{8,12},{10,14},{12,16},{14,18},{16,20},{1... | collective-permute-start | bytes 786440 | tf_op jit(solution)/shard_map/ppermute | solution.py:14
  4.5 1.0 collective-permute-start
  5.5 7.5 %collective-permute-start.2 = (bf16[128,1024]{1,0:T(8,128)(2,1)}, bf16[128,1024]{1,0:T(8,128)(2,1)S(1)}, u32[]{:S(2)}, u32[]{:S(2)}) collective-permute-start(bf16[128,1024]{1,0:T(8,128)(2,1)} %param.6), channel_id=1, source_target_pairs={{0,252},{2,254},{4,0},{6,2},{8,4},{10,6},{12,8},{14,10},{16,12},{1... | collective-permute-start | bytes 786440 | tf_op jit(solution)/shard_map/ppermute | solution.py:14
  13.0 1.7 %constant_dynamic-update-slice_fusion.17 = bf16[1152,1024]{1,0:T(8,128)(2,1)} fusion(bf16[128,1024]{1,0:T(8,128)(2,1)} %param.6), kind=kLoop, calls=%fused_computation.92 | loop fusion | bytes 524288
  14.7 1.3 %fusion.19 = (pred[8]{0:T(512)(128)(4,1)S(1)}, pred[8]{0:T(512)(128)(4,1)S(1)}, pred[8]{0:T(512)(128)(4,1)S(1)}, pred[8]{0:T(512)(128)(4,1)S(1)}, pred[8]{0:T(51...) fusion(s32[8,128]{1,0:T(8,128)} %param.7, ...), kind=kLoop, calls=%fused_computation.118 | loop fusion | flops 72 | bytes 396 | tf_op jit(solution)/shard_map/eq | solution.py:62
  16.0 0.7 fusion.31
  16.8 0.1 broadcast_bitcast_fusion.11
  17.3 0.1 broadcast_bitcast_fusion.5
  17.6 1.8 %select_reduce_fusion.26 = (f32[1024]{0:T(1024)S(1)}, f32[1024,128]{0,1:T(8,128)S(1)}) fusion(pred[1024]{0:T(1024)(128)(4,1)S(1)} %get-tuple-element.143, bf16[1024,1024]{1,0:T(8,128)(2,1)S(1)} %copy-done, bf16[128,1024]{1,0:T(8,128)(2,1)} %param.6), kind=kOutput, calls=%fused_computation.70 | convolution fusion | flops 268827648 | bytes 2888704 | tf_op jit(solution)/shard_map/dot_general | solution.py:69
  19.5 0.5 collective-permute-done.1
  20.0 0.2 collective-permute-start.5
  20.1 1.5 %collective-permute-start.3 = (bf16[128,1024]{1,0:T(8,128)(2,1)S(1)}, bf16[128,1024]{1,0:T(8,128)(2,1)S(1)}, u32[]{:S(2)}, u32[]{:S(2)}) collective-permute-start(bf16[128,1024]{1,0:T(8,128)(2,1)S(1)} %collective-permute-done.1), channel_id=1, source_target_pairs={{0,2},{2,0},{4,6},{6,4},{8,10},{10,8},{12,14},{14,12},{16,18},{18,... | collective-permute-start | bytes 786440 | tf_op jit(solution)/shard_map/ppermute | solution.py:19
  21.7 0.5 collective-permute-done.2
  22.2 7.9 %collective-permute-start.6 = (bf16[128,1024]{1,0:T(8,128)(2,1)S(1)}, bf16[128,1024]{1,0:T(8,128)(2,1)S(1)}, u32[]{:S(2)}, u32[]{:S(2)}) collective-permute-start(bf16[128,1024]{1,0:T(8,128)(2,1)S(1)} %collective-permute-done.2), channel_id=1, source_target_pairs={{0,252},{2,254},{4,0},{6,2},{8,4},{10,6},{12,8},{14,10},{16,12},{1... | collective-permute-start | bytes 786440 | tf_op jit(solution)/shard_map/ppermute | solution.py:14
  30.1 4.2 %collective-permute-start.4 = (bf16[128,1024]{1,0:T(8,128)(2,1)S(1)}, bf16[128,1024]{1,0:T(8,128)(2,1)S(1)}, u32[]{:S(2)}, u32[]{:S(2)}) collective-permute-start(bf16[128,1024]{1,0:T(8,128)(2,1)S(1)} %collective-permute-done.2), channel_id=1, source_target_pairs={{0,2},{2,0},{4,6},{6,4},{8,10},{10,8},{12,14},{14,12},{16,18},{18,... | collective-permute-start | bytes 786440 | tf_op jit(solution)/shard_map/ppermute | solution.py:19
  34.2 0.8 select_reduce_fusion.23
  35.1 0.8 select_reduce_fusion.24
  36.0 0.8 select_reduce_fusion.25
  36.8 0.7 constant_dynamic-update-slice_fusion.16
  37.5 0.7 constant_dynamic-update-slice_fusion.15
  38.3 0.7 constant_dynamic-update-slice_fusion.14
  39.0 0.7 constant_dynamic-update-slice_fusion.13
  39.7 0.7 constant_dynamic-update-slice_fusion.12
  40.4 0.7 constant_dynamic-update-slice_fusion.11
  41.2 0.8 constant_dynamic-update-slice_fusion.10
  41.9 2.6 %collective-permute-start.7 = (bf16[128,1024]{1,0:T(8,128)(2,1)S(1)}, bf16[128,1024]{1,0:T(8,128)(2,1)S(1)}, u32[]{:S(2)}, u32[]{:S(2)}) collective-permute-start(bf16[128,1024]{1,0:T(8,128)(2,1)S(1)} %get-tuple-element.96), channel_id=1, source_target_pairs={{0,2},{2,0},{4,6},{6,4},{8,10},{10,8},{12,14},{14,12},{16,18},{18,... | collective-permute-start | bytes 786440 | tf_op jit(solution)/shard_map/ppermute | solution.py:19
  44.5 0.8 select_reduce_fusion.21
  45.3 0.8 select_reduce_fusion.19
  46.2 0.8 select_reduce_fusion.22
  47.0 0.8 select_reduce_fusion.20
  47.9 0.8 select_reduce_fusion.18
  48.8 0.2 select_reduce_fusion.6
  49.1 0.8 select_reduce_fusion.8
  49.9 0.8 select_reduce_fusion.7
  50.7 0.6 add_subtract_fusion
  51.3 0.2 constant_dynamic-update-slice_fusion.23
  51.5 0.2 constant_dynamic-update-slice_fusion.22
  51.7 0.2 constant_dynamic-update-slice_fusion.21
  51.9 0.2 constant_dynamic-update-slice_fusion.20
  52.1 0.2 constant_dynamic-update-slice_fusion.19
  52.3 0.2 constant_dynamic-update-slice_fusion.18
  52.5 0.2 constant_dynamic-update-slice_fusion.2
  52.6 0.2 constant_dynamic-update-slice_fusion.1
  52.8 0.2 constant_dynamic-update-slice_fusion
  53.0 1.4 %copy-done.4 = bf16[1024,1152]{0,1:T(8,128)(2,1)} copy-done((bf16[1024,1152]{0,1:T(8,128)(2,1)}, bf16[1024,1152]{0,1:T(8,128)(2,1)S(1)}, u32[]{:S(2)}) %copy-start.4) | copy-done | bytes 2359320
  54.4 1.0 fusion.1
  55.5 0.1 collective-permute-start.10
  55.6 1.8 %fusion.34 = f32[768,1024]{1,0:T(8,128)S(1)} fusion(bf16[1024,768]{0,1:T(8,128)(2,1)S(1)} %get-tuple-element.83, bf16[1024,1024]{1,0:T(8,128)(2,1)S(1)} %copy-done), kind=kOutput, calls=%fused_computation.160 | convolution fusion | flops 1610612736 | bytes 6815744 | tf_op jit(solution)/shard_map/dot_general | solution.py:95
  57.4 1.1 fusion.33
  58.5 0.5 collective-permute-start.13
  59.0 0.1 slice_add_fusion.2
  59.1 0.1 collective-permute-start.11
  59.2 8.6 %collective-permute-start.14 = (f32[128,1024]{1,0:T(8,128)S(1)}, f32[128,1024]{1,0:T(8,128)S(1)}, u32[]{:S(2)}, u32[]{:S(2)}) collective-permute-start(f32[128,1024]{1,0:T(8,128)S(1)} %get-tuple-element.82), channel_id=1, source_target_pairs={{0,252},{2,254},{4,0},{6,2},{8,4},{10,6},{12,8},{14,10},{16,12},{1... | collective-permute-start | bytes 1572872 | tf_op jit(solution)/shard_map/ppermute | solution.py:14
  67.8 0.8 collective-permute-start.8
  68.6 22.6 %collective-permute-done.11 = f32[128,1024]{1,0:T(8,128)S(1)} collective-permute-done((f32[128,1024]{1,0:T(8,128)S(1)}, f32[128,1024]{1,0:T(8,128)S(1)}, u32[]{:S(2)}, u32[]{:S(2)}) %collective-permute-start.11) | collective-permute-done | bytes 524320 | tf_op jit(solution)/shard_map/ppermute | solution.py:14
  91.2 1.3 fusion.8
  92.5 7.8 %collective-permute-start.15 = (f32[128,1024]{1,0:T(8,128)}, f32[128,1024]{1,0:T(8,128)}, u32[]{:S(2)}, u32[]{:S(2)}) collective-permute-start(f32[128,1024]{1,0:T(8,128)} %get-tuple-element.80), channel_id=1, source_target_pairs={{0,252},{2,254},{4,0},{6,2},{8,4},{10,6},{12,8},{14,10},{16,12},{1... | collective-permute-start | bytes 1572872 | tf_op jit(solution)/shard_map/ppermute | solution.py:14
  100.3 0.7 constant_dynamic-update-slice_fusion.9
  101.0 21.2 %collective-permute-done.12 = f32[128,1024]{1,0:T(8,128)S(1)} collective-permute-done((f32[128,1024]{1,0:T(8,128)}, f32[128,1024]{1,0:T(8,128)S(1)}, u32[]{:S(2)}, u32[]{:S(2)}) %collective-permute-start.12) | collective-permute-done | bytes 524320 | tf_op jit(solution)/shard_map/ppermute | solution.py:14
  122.2 1.3 %fusion.10 = f32[128,1024]{1,0:T(8,128)S(1)} fusion(f32[128,1024]{1,0:T(8,128)} %collective-permute-done.15, f32[128,1024]{1,0:T(8,128)S(1)} %collective-permute-done.12, f32[128,1024]{1,0:T(8,128)S(1)} %collective-permute-done.8, f32[768,1024]{1,0:T(8,128)} %copy-done.1), kind=kLoop, calls=%fused_computation.25 | loop fusion | flops 393216 | bytes 2621440 | tf_op jit(solution)/shard_map/add | solution.py:114
  123.6 0.1 collective-permute-start.16
  123.7 6.1 %convolution_multiply_fusion = f32[1024,1024]{1,0:T(8,128)} fusion(bf16[1024,1152]{0,1:T(8,128)(2,1)} %copy-done.4, bf16[1152,1024]{1,0:T(8,128)(2,1)S(1)} %copy-done.3), kind=kOutput, calls=%fused_computation | convolution fusion | flops 2416967680 | bytes 8912896 | tf_op jit(solution)/shard_map/dot_general | solution.py:90
  129.8 1.2 collective-permute-done.16
  131.0 0.7 add_multiply_fusion
  (38 shorter events, 1.0 us)
Async XLA Ops:
  0.6 17.0 %copy-start = (bf16[1024,1024]{1,0:T(8,128)(2,1)S(1)}, bf16[1024,1024]{1,0:T(8,128)(2,1)}, u32[]{:S(2)}) copy-start(bf16[1024,1024]{1,0:T(8,128)(2,1)} %param.5) | copy-start | bytes 6291460
  0.6 19.3 %collective-permute-start.1 = (bf16[128,1024]{1,0:T(8,128)(2,1)}, bf16[128,1024]{1,0:T(8,128)(2,1)S(1)}, u32[]{:S(2)}, u32[]{:S(2)}) collective-permute-start(bf16[128,1024]{1,0:T(8,128)(2,1)} %param.6), channel_id=1, source_target_pairs={{0,4},{2,6},{4,8},{6,10},{8,12},{10,14},{12,16},{14,18},{16,20},{1... | collective-permute-start | bytes 786440 | tf_op jit(solution)/shard_map/ppermute | solution.py:14
  4.5 31.4 %collective-permute-start = (bf16[128,1024]{1,0:T(8,128)(2,1)}, bf16[128,1024]{1,0:T(8,128)(2,1)S(1)}, u32[]{:S(2)}, u32[]{:S(2)}) collective-permute-start(bf16[128,1024]{1,0:T(8,128)(2,1)} %param.6), channel_id=1, source_target_pairs={{0,2},{2,0},{4,6},{6,4},{8,10},{10,8},{12,14},{14,12},{16,18},{18,... | collective-permute-start | bytes 786440 | tf_op jit(solution)/shard_map/ppermute | solution.py:19
  5.5 16.7 %collective-permute-start.2 = (bf16[128,1024]{1,0:T(8,128)(2,1)}, bf16[128,1024]{1,0:T(8,128)(2,1)S(1)}, u32[]{:S(2)}, u32[]{:S(2)}) collective-permute-start(bf16[128,1024]{1,0:T(8,128)(2,1)} %param.6), channel_id=1, source_target_pairs={{0,252},{2,254},{4,0},{6,2},{8,4},{10,6},{12,8},{14,10},{16,12},{1... | collective-permute-start | bytes 786440 | tf_op jit(solution)/shard_map/ppermute | solution.py:14
  20.0 20.5 %collective-permute-start.5 = (bf16[128,1024]{1,0:T(8,128)(2,1)S(1)}, bf16[128,1024]{1,0:T(8,128)(2,1)S(1)}, u32[]{:S(2)}, u32[]{:S(2)}) collective-permute-start(bf16[128,1024]{1,0:T(8,128)(2,1)S(1)} %collective-permute-done.1), channel_id=1, source_target_pairs={{0,4},{2,6},{4,8},{6,10},{8,12},{10,14},{12,16},{14,18},{16,20},{1... | collective-permute-start | bytes 786440 | tf_op jit(solution)/shard_map/ppermute | solution.py:14
  20.1 18.8 %collective-permute-start.3 = (bf16[128,1024]{1,0:T(8,128)(2,1)S(1)}, bf16[128,1024]{1,0:T(8,128)(2,1)S(1)}, u32[]{:S(2)}, u32[]{:S(2)}) collective-permute-start(bf16[128,1024]{1,0:T(8,128)(2,1)S(1)} %collective-permute-done.1), channel_id=1, source_target_pairs={{0,2},{2,0},{4,6},{6,4},{8,10},{10,8},{12,14},{14,12},{16,18},{18,... | collective-permute-start | bytes 786440 | tf_op jit(solution)/shard_map/ppermute | solution.py:19
  22.2 19.0 %collective-permute-start.6 = (bf16[128,1024]{1,0:T(8,128)(2,1)S(1)}, bf16[128,1024]{1,0:T(8,128)(2,1)S(1)}, u32[]{:S(2)}, u32[]{:S(2)}) collective-permute-start(bf16[128,1024]{1,0:T(8,128)(2,1)S(1)} %collective-permute-done.2), channel_id=1, source_target_pairs={{0,252},{2,254},{4,0},{6,2},{8,4},{10,6},{12,8},{14,10},{16,12},{1... | collective-permute-start | bytes 786440 | tf_op jit(solution)/shard_map/ppermute | solution.py:14
  30.1 9.6 %collective-permute-start.4 = (bf16[128,1024]{1,0:T(8,128)(2,1)S(1)}, bf16[128,1024]{1,0:T(8,128)(2,1)S(1)}, u32[]{:S(2)}, u32[]{:S(2)}) collective-permute-start(bf16[128,1024]{1,0:T(8,128)(2,1)S(1)} %collective-permute-done.2), channel_id=1, source_target_pairs={{0,2},{2,0},{4,6},{6,4},{8,10},{10,8},{12,14},{14,12},{16,18},{18,... | collective-permute-start | bytes 786440 | tf_op jit(solution)/shard_map/ppermute | solution.py:19
  41.9 6.0 %collective-permute-start.7 = (bf16[128,1024]{1,0:T(8,128)(2,1)S(1)}, bf16[128,1024]{1,0:T(8,128)(2,1)S(1)}, u32[]{:S(2)}, u32[]{:S(2)}) collective-permute-start(bf16[128,1024]{1,0:T(8,128)(2,1)S(1)} %get-tuple-element.96), channel_id=1, source_target_pairs={{0,2},{2,0},{4,6},{6,4},{8,10},{10,8},{12,14},{14,12},{16,18},{18,... | collective-permute-start | bytes 786440 | tf_op jit(solution)/shard_map/ppermute | solution.py:19
  49.1 2.2 %copy-start.2 = (f32[1024]{0:T(1024)S(1)}, f32[1024]{0:T(1024)}, u32[]{:S(2)}) copy-start(f32[1024]{0:T(1024)} %param.9) | copy-start | bytes 12292
  53.0 1.4 %copy-start.4 = (bf16[1024,1152]{0,1:T(8,128)(2,1)}, bf16[1024,1152]{0,1:T(8,128)(2,1)S(1)}, u32[]{:S(2)}) copy-start(bf16[1024,1152]{0,1:T(8,128)(2,1)S(1)} %get-tuple-element.42) | copy-start | bytes 7077892
  55.5 3.5 %collective-permute-start.10 = (f32[128,1024]{1,0:T(8,128)S(1)}, f32[128,1024]{1,0:T(8,128)S(1)}, u32[]{:S(2)}, u32[]{:S(2)}) collective-permute-start(f32[128,1024]{1,0:T(8,128)S(1)} %slice.53), channel_id=1, source_target_pairs={{0,2},{2,0},{4,6},{6,4},{8,10},{10,8},{12,14},{14,12},{16,18},{18,... | collective-permute-start | bytes 1572872 | tf_op jit(solution)/shard_map/ppermute | solution.py:19
  57.4 33.8 %copy-start.1 = (f32[768,1024]{1,0:T(8,128)}, f32[768,1024]{1,0:T(8,128)S(1)}, u32[]{:S(2)}) copy-start(f32[768,1024]{1,0:T(8,128)S(1)} %fusion.34) | copy-start | bytes 9437188
  58.5 10.1 %collective-permute-start.13 = (f32[128,1024]{1,0:T(8,128)S(1)}, f32[128,1024]{1,0:T(8,128)S(1)}, u32[]{:S(2)}, u32[]{:S(2)}) collective-permute-start(f32[128,1024]{1,0:T(8,128)S(1)} %get-tuple-element.77), channel_id=1, source_target_pairs={{0,2},{2,0},{4,6},{6,4},{8,10},{10,8},{12,14},{14,12},{16,18},{18,... | collective-permute-start | bytes 1572872 | tf_op jit(solution)/shard_map/ppermute | solution.py:19
  59.0 9.6 %collective-permute-start.9 = (f32[128,1024]{1,0:T(8,128)S(1)}, f32[128,1024]{1,0:T(8,128)S(1)}, u32[]{:S(2)}, u32[]{:S(2)}) collective-permute-start(f32[128,1024]{1,0:T(8,128)S(1)} %get-tuple-element.78), channel_id=1, source_target_pairs={{0,2},{2,0},{4,6},{6,4},{8,10},{10,8},{12,14},{14,12},{16,18},{18,... | collective-permute-start | bytes 1572872 | tf_op jit(solution)/shard_map/ppermute | solution.py:19
  59.1 32.1 %collective-permute-start.11 = (f32[128,1024]{1,0:T(8,128)S(1)}, f32[128,1024]{1,0:T(8,128)S(1)}, u32[]{:S(2)}, u32[]{:S(2)}) collective-permute-start(f32[128,1024]{1,0:T(8,128)S(1)} %get-tuple-element.81), channel_id=1, source_target_pairs={{0,4},{2,6},{4,8},{6,10},{8,12},{10,14},{12,16},{14,18},{16,20},{1... | collective-permute-start | bytes 1572872 | tf_op jit(solution)/shard_map/ppermute | solution.py:14
  59.2 32.0 %collective-permute-start.14 = (f32[128,1024]{1,0:T(8,128)S(1)}, f32[128,1024]{1,0:T(8,128)S(1)}, u32[]{:S(2)}, u32[]{:S(2)}) collective-permute-start(f32[128,1024]{1,0:T(8,128)S(1)} %get-tuple-element.82), channel_id=1, source_target_pairs={{0,252},{2,254},{4,0},{6,2},{8,4},{10,6},{12,8},{14,10},{16,12},{1... | collective-permute-start | bytes 1572872 | tf_op jit(solution)/shard_map/ppermute | solution.py:14
  67.8 33.2 %collective-permute-start.8 = (f32[128,1024]{1,0:T(8,128)}, f32[128,1024]{1,0:T(8,128)S(1)}, u32[]{:S(2)}, u32[]{:S(2)}) collective-permute-start(f32[128,1024]{1,0:T(8,128)} %get-tuple-element.76), channel_id=1, source_target_pairs={{0,2},{2,0},{4,6},{6,4},{8,10},{10,8},{12,14},{14,12},{16,18},{18,... | collective-permute-start | bytes 1572872 | tf_op jit(solution)/shard_map/ppermute | solution.py:19
  92.5 29.7 %collective-permute-start.12 = (f32[128,1024]{1,0:T(8,128)}, f32[128,1024]{1,0:T(8,128)S(1)}, u32[]{:S(2)}, u32[]{:S(2)}) collective-permute-start(f32[128,1024]{1,0:T(8,128)} %get-tuple-element.79), channel_id=1, source_target_pairs={{0,4},{2,6},{4,8},{6,10},{8,12},{10,14},{12,16},{14,18},{16,20},{1... | collective-permute-start | bytes 1572872 | tf_op jit(solution)/shard_map/ppermute | solution.py:14
  92.5 29.7 %collective-permute-start.15 = (f32[128,1024]{1,0:T(8,128)}, f32[128,1024]{1,0:T(8,128)}, u32[]{:S(2)}, u32[]{:S(2)}) collective-permute-start(f32[128,1024]{1,0:T(8,128)} %get-tuple-element.80), channel_id=1, source_target_pairs={{0,252},{2,254},{4,0},{6,2},{8,4},{10,6},{12,8},{14,10},{16,12},{1... | collective-permute-start | bytes 1572872 | tf_op jit(solution)/shard_map/ppermute | solution.py:14
  101.0 22.7 %copy-start.3 = (bf16[1152,1024]{1,0:T(8,128)(2,1)S(1)}, bf16[1152,1024]{1,0:T(8,128)(2,1)}, u32[]{:S(2)}) copy-start(bf16[1152,1024]{1,0:T(8,128)(2,1)} %constant_dynamic-update-slice_fusion.9) | copy-start | bytes 7077892
  123.6 7.5 %collective-permute-start.16 = (f32[64,1024]{1,0:T(8,128)S(1)}, f32[64,1024]{1,0:T(8,128)S(1)}, u32[]{:S(2)}, u32[]{:S(2)}) collective-permute-start(f32[64,1024]{1,0:T(8,128)S(1)} %slice_select_fusion), channel_id=1, source_target_pairs={{0,1},{1,0},{2,3},{3,2},{4,5},{5,4},{6,7},{7,6},{8,9},{9,8},{10,11... | collective-permute-start | bytes 786440 | tf_op jit(solution)/shard_map/ppermute | solution.py:123

commit v9 on v8

--- a/solution.py
+++ b/solution.py
@@ -110,17 +110,23 @@
     far_down_in = passed_along(far_down, "dp", -2)
     near_up = key_parts["up2"] + back_up2 + far_up_in
     near_down = key_parts["down2"] + back_down2 + far_down_in
-    total = (
-        key_parts["own"]
-        + back_own
-        + passed_along(near_up, "dp", 2)
-        + passed_along(near_down, "dp", -2)
+    parts = (
+        key_parts["own"],
+        back_own,
+        passed_along(near_up, "dp", 2),
+        passed_along(near_down, "dp", -2),
     )
     half = tile_rows // 2
-    halves = total.reshape(2, half, total.shape[1])
-    mine = jnp.where(rep_index == 0, halves[0], halves[1])
-    other = jnp.where(rep_index == 0, halves[1], halves[0])
-    grad_keys = logit_scale * (mine + lax.ppermute(other, "rep", [(0, 1), (1, 0)]))
+    mine_at = rep_index * half
+    other_at = (1 - rep_index) * half
+    other = sum(lax.dynamic_slice_in_dim(p, other_at, half, 0) for p in parts[1:]) + lax.dynamic_slice_in_dim(
+        parts[0], other_at, half, 0
+    )
+    received = lax.ppermute(other, "rep", [(0, 1), (1, 0)])
+    mine = sum(lax.dynamic_slice_in_dim(p, mine_at, half, 0) for p in parts[1:]) + lax.dynamic_slice_in_dim(
+        parts[0], mine_at, half, 0
+    )
+    grad_keys = logit_scale * (mine + received)
     return (row_loss, grad_query, grad_keys)
 
 

time: 132 us -> 133 us (level)
    unnamed x17 -> x13, local copies, waits for them, and re-layouts: 7.48 us -> 7.47 us
  transfers between devices with their start and end apart: 17 -> 17, of which waited for: 5 -> 4; matrix products, arithmetic and copies ran while one was open for 21% -> 22% of each run, Pallas kernels for 0% -> 0%
where the time goes in v9:
time: 133 us
  starting transfers between devices  46.9 us (35%)
  waiting for transfers between devices  44.9 us (34%)
  matrix products  18.6 us (14%)
  other arithmetic  11.3 us (8%)
  local copies, waits for them, and re-layouts  10.2 us (8%)
    ppermute x8, waiting for transfers between devices, passed_along(): return lax.ppermute(x, axis, [(i, (i + by) % count) for i in range(count)])  44.8 us
    ppermute x8, starting transfers between devices, passed_along(): return lax.ppermute(x, axis, [(i, (i + by) % count) for i in range(count)])  36.2 us
    ppermute x8, starting transfers between devices, swapped(): return lax.ppermute(x, axis, [(i, i ^ 1) for i in range(count)])  10.6 us
    dot_general x9, matrix products, step(): lax.dot_general(queries, key_tile, (((1,), (1,)), ((), ())), preferred_el...  8.52 us
    unnamed x13, local copies, waits for them, and re-layouts  7.47 us
    dot_general x1, matrix products, step(): jnp.dot(coefficient, window, preferred_element_type=jnp.float32)  7.32 us
    dot_general x2, matrix products, parts_of(): lax.dot_general(cols, queries, (((0,), (0,)), ((), ())), preferred_elemen...  2.79 us
  transfers between devices with their start and end apart: 17, of which 4 were waited for; matrix products, arithmetic and copies ran while one was open for 22% of the time, Pallas kernels for 0%

profile of v9, /device:TPU:1, one launch (start us, length us, event | category | flops | bytes accessed | tf_op | source)
XLA Modules:
  0.0 132.8 jit_solution(1549836562341659512)
XLA Ops:
  0.6 3.9 %collective-permute-start.1 = (bf16[128,1024]{1,0:T(8,128)(2,1)}, bf16[128,1024]{1,0:T(8,128)(2,1)S(1)}, u32[]{:S(2)}, u32[]{:S(2)}) collective-permute-start(bf16[128,1024]{1,0:T(8,128)(2,1)} %param.6), channel_id=1, source_target_pairs={{0,4},{2,6},{4,8},{6,10},{8,12},{10,14},{12,16},{14,18},{16,20},{1... | collective-permute-start | bytes 786440 | tf_op jit(solution)/shard_map/ppermute | solution.py:14
  4.5 1.0 collective-permute-start
  5.5 7.5 %collective-permute-start.2 = (bf16[128,1024]{1,0:T(8,128)(2,1)}, bf16[128,1024]{1,0:T(8,128)(2,1)S(1)}, u32[]{:S(2)}, u32[]{:S(2)}) collective-permute-start(bf16[128,1024]{1,0:T(8,128)(2,1)} %param.6), channel_id=1, source_target_pairs={{0,252},{2,254},{4,0},{6,2},{8,4},{10,6},{12,8},{14,10},{16,12},{1... | collective-permute-start | bytes 786440 | tf_op jit(solution)/shard_map/ppermute | solution.py:14
  13.0 1.7 %constant_dynamic-update-slice_fusion.17 = bf16[1152,1024]{1,0:T(8,128)(2,1)} fusion(bf16[128,1024]{1,0:T(8,128)(2,1)} %param.6), kind=kLoop, calls=%fused_computation.89 | loop fusion | bytes 524288
  14.7 1.3 %fusion.18 = (pred[8]{0:T(512)(128)(4,1)S(1)}, pred[8]{0:T(512)(128)(4,1)S(1)}, pred[8]{0:T(512)(128)(4,1)S(1)}, pred[8]{0:T(512)(128)(4,1)S(1)}, pred[8]{0:T(51...) fusion(s32[8,128]{1,0:T(8,128)} %param.7, ...), kind=kLoop, calls=%fused_computation.116 | loop fusion | flops 72 | bytes 396 | tf_op jit(solution)/shard_map/eq | solution.py:62
  16.0 0.7 fusion.38
  16.8 0.1 broadcast_bitcast_fusion.11
  17.3 0.1 broadcast_bitcast_fusion.5
  17.4 0.1 broadcast_bitcast_fusion.2
  17.6 1.8 %select_reduce_fusion.26 = (f32[1024]{0:T(1024)S(1)}, f32[1024,128]{0,1:T(8,128)S(1)}) fusion(pred[1024]{0:T(1024)(128)(4,1)S(1)} %get-tuple-element.144, bf16[1024,1024]{1,0:T(8,128)(2,1)S(1)} %copy-done, bf16[128,1024]{1,0:T(8,128)(2,1)} %param.6), kind=kOutput, calls=%fused_computation.67 | convolution fusion | flops 268827648 | bytes 2888704 | tf_op jit(solution)/shard_map/dot_general | solution.py:69
  19.5 0.5 collective-permute-done.1
  20.0 0.2 collective-permute-start.5
  20.1 1.5 %collective-permute-start.3 = (bf16[128,1024]{1,0:T(8,128)(2,1)S(1)}, bf16[128,1024]{1,0:T(8,128)(2,1)S(1)}, u32[]{:S(2)}, u32[]{:S(2)}) collective-permute-start(bf16[128,1024]{1,0:T(8,128)(2,1)S(1)} %collective-permute-done.1), channel_id=1, source_target_pairs={{0,2},{2,0},{4,6},{6,4},{8,10},{10,8},{12,14},{14,12},{16,18},{18,... | collective-permute-start | bytes 786440 | tf_op jit(solution)/shard_map/ppermute | solution.py:19
  21.7 0.5 collective-permute-done.2
  22.2 7.9 %collective-permute-start.6 = (bf16[128,1024]{1,0:T(8,128)(2,1)S(1)}, bf16[128,1024]{1,0:T(8,128)(2,1)S(1)}, u32[]{:S(2)}, u32[]{:S(2)}) collective-permute-start(bf16[128,1024]{1,0:T(8,128)(2,1)S(1)} %collective-permute-done.2), channel_id=1, source_target_pairs={{0,252},{2,254},{4,0},{6,2},{8,4},{10,6},{12,8},{14,10},{16,12},{1... | collective-permute-start | bytes 786440 | tf_op jit(solution)/shard_map/ppermute | solution.py:14
  30.1 4.2 %collective-permute-start.4 = (bf16[128,1024]{1,0:T(8,128)(2,1)S(1)}, bf16[128,1024]{1,0:T(8,128)(2,1)S(1)}, u32[]{:S(2)}, u32[]{:S(2)}) collective-permute-start(bf16[128,1024]{1,0:T(8,128)(2,1)S(1)} %collective-permute-done.2), channel_id=1, source_target_pairs={{0,2},{2,0},{4,6},{6,4},{8,10},{10,8},{12,14},{14,12},{16,18},{18,... | collective-permute-start | bytes 786440 | tf_op jit(solution)/shard_map/ppermute | solution.py:19
  34.2 0.8 select_reduce_fusion.23
  35.1 0.8 select_reduce_fusion.24
  36.0 0.8 select_reduce_fusion.25
  36.8 0.7 constant_dynamic-update-slice_fusion.16
  37.5 0.7 constant_dynamic-update-slice_fusion.15
  38.3 0.7 constant_dynamic-update-slice_fusion.14
  39.0 0.7 constant_dynamic-update-slice_fusion.13
  39.7 0.7 constant_dynamic-update-slice_fusion.12
  40.4 0.7 constant_dynamic-update-slice_fusion.11
  41.2 0.8 constant_dynamic-update-slice_fusion.10
  41.9 2.6 %collective-permute-start.7 = (bf16[128,1024]{1,0:T(8,128)(2,1)S(1)}, bf16[128,1024]{1,0:T(8,128)(2,1)S(1)}, u32[]{:S(2)}, u32[]{:S(2)}) collective-permute-start(bf16[128,1024]{1,0:T(8,128)(2,1)S(1)} %get-tuple-element.97), channel_id=1, source_target_pairs={{0,2},{2,0},{4,6},{6,4},{8,10},{10,8},{12,14},{14,12},{16,18},{18,... | collective-permute-start | bytes 786440 | tf_op jit(solution)/shard_map/ppermute | solution.py:19
  44.5 0.8 select_reduce_fusion.21
  45.3 0.8 select_reduce_fusion.19
  46.2 0.8 select_reduce_fusion.22
  47.0 0.8 select_reduce_fusion.20
  47.9 0.8 select_reduce_fusion.18
  48.8 0.2 select_reduce_fusion.6
  49.1 0.8 select_reduce_fusion.8
  49.9 0.8 select_reduce_fusion.7
  50.7 0.6 add_subtract_fusion
  51.3 0.2 constant_dynamic-update-slice_fusion.23
  51.5 0.2 constant_dynamic-update-slice_fusion.22
  51.7 0.2 constant_dynamic-update-slice_fusion.21
  51.9 0.2 constant_dynamic-update-slice_fusion.20
  52.1 0.2 constant_dynamic-update-slice_fusion.19
  52.3 0.2 constant_dynamic-update-slice_fusion.18
  52.5 0.2 constant_dynamic-update-slice_fusion.2
  52.6 0.2 constant_dynamic-update-slice_fusion.1
  52.8 0.2 constant_dynamic-update-slice_fusion
  53.0 1.4 %copy-done.2 = bf16[1024,1152]{0,1:T(8,128)(2,1)} copy-done((bf16[1024,1152]{0,1:T(8,128)(2,1)}, bf16[1024,1152]{0,1:T(8,128)(2,1)S(1)}, u32[]{:S(2)}) %copy-start.2) | copy-done | bytes 2359320
  54.4 1.0 fusion.1
  55.5 0.1 collective-permute-start.10
  55.6 1.8 %fusion.41 = f32[768,1024]{1,0:T(8,128)S(1)} fusion(bf16[1024,768]{0,1:T(8,128)(2,1)S(1)} %get-tuple-element.84, bf16[1024,1024]{1,0:T(8,128)(2,1)S(1)} %copy-done), kind=kOutput, calls=%fused_computation.166 | convolution fusion | flops 1610612736 | bytes 6815744 | tf_op jit(solution)/shard_map/dot_general | solution.py:95
  57.4 1.0 fusion.40
  58.4 0.5 collective-permute-start.13
  58.9 0.1 slice_add_fusion.2
  59.0 0.1 collective-permute-start.11
  59.1 8.8 %collective-permute-start.14 = (f32[128,1024]{1,0:T(8,128)S(1)}, f32[128,1024]{1,0:T(8,128)S(1)}, u32[]{:S(2)}, u32[]{:S(2)}) collective-permute-start(f32[128,1024]{1,0:T(8,128)S(1)} %get-tuple-element.83), channel_id=1, source_target_pairs={{0,252},{2,254},{4,0},{6,2},{8,4},{10,6},{12,8},{14,10},{16,12},{1... | collective-permute-start | bytes 1572872 | tf_op jit(solution)/shard_map/ppermute | solution.py:14
  67.9 0.8 collective-permute-start.8
  68.7 22.4 %collective-permute-done.11 = f32[128,1024]{1,0:T(8,128)S(1)} collective-permute-done((f32[128,1024]{1,0:T(8,128)S(1)}, f32[128,1024]{1,0:T(8,128)S(1)}, u32[]{:S(2)}, u32[]{:S(2)}) %collective-permute-start.11) | collective-permute-done | bytes 524320 | tf_op jit(solution)/shard_map/ppermute | solution.py:14
  91.1 1.3 fusion.8
  92.4 7.9 %collective-permute-start.15 = (f32[128,1024]{1,0:T(8,128)}, f32[128,1024]{1,0:T(8,128)}, u32[]{:S(2)}, u32[]{:S(2)}) collective-permute-start(f32[128,1024]{1,0:T(8,128)} %get-tuple-element.81), channel_id=1, source_target_pairs={{0,252},{2,254},{4,0},{6,2},{8,4},{10,6},{12,8},{14,10},{16,12},{1... | collective-permute-start | bytes 1572872 | tf_op jit(solution)/shard_map/ppermute | solution.py:14
  100.3 0.7 constant_dynamic-update-slice_fusion.9
  101.0 21.4 %collective-permute-done.12 = f32[128,1024]{1,0:T(8,128)} collective-permute-done((f32[128,1024]{1,0:T(8,128)}, f32[128,1024]{1,0:T(8,128)}, u32[]{:S(2)}, u32[]{:S(2)}) %collective-permute-start.12) | collective-permute-done | bytes 524320 | tf_op jit(solution)/shard_map/ppermute | solution.py:14
  122.4 1.1 dynamic-slice_add_fusion
  123.5 0.1 collective-permute-start.16
  123.6 7.3 %convolution_multiply_fusion = f32[1024,1024]{1,0:T(8,128)} fusion(bf16[1024,1152]{0,1:T(8,128)(2,1)} %copy-done.2, bf16[1152,1024]{1,0:T(8,128)(2,1)} %constant_dynamic-update-slice_fusion.9), kind=kOutput, calls=%fused_computation | convolution fusion | flops 2416967680 | bytes 8912896 | tf_op jit(solution)/shard_map/dot_general | solution.py:90
  130.9 1.8 %add_multiply_fusion = f32[64,1024]{1,0:T(8,128)} fusion(f32[64,1024]{1,0:T(8,128)S(1)} %collective-permute-done.16, f32[128,1024]{1,0:T(8,128)S(1)} %get-tuple-element.77, s32[]{:T(128)S(6)} %select_n.231, f32[128,1024]{1,0:T(8,128)} %collective-permute-done.15, f32[128,1024]{1,0:T(8,128)} %collective-permute-done.12, f32[128,1024]{1,0:T(8,128)S(1)} %collective-permute-done.8), kind=kLoop, calls=%fused_computation.68 | loop fusion | flops 327680 | bytes 1572868 | tf_op jit(solution)/shard_map/mul | solution.py:129
  (33 shorter events, 0.9 us)
Async XLA Ops:
  0.6 17.0 %copy-start = (bf16[1024,1024]{1,0:T(8,128)(2,1)S(1)}, bf16[1024,1024]{1,0:T(8,128)(2,1)}, u32[]{:S(2)}) copy-start(bf16[1024,1024]{1,0:T(8,128)(2,1)} %param.5) | copy-start | bytes 6291460
  0.6 19.3 %collective-permute-start.1 = (bf16[128,1024]{1,0:T(8,128)(2,1)}, bf16[128,1024]{1,0:T(8,128)(2,1)S(1)}, u32[]{:S(2)}, u32[]{:S(2)}) collective-permute-start(bf16[128,1024]{1,0:T(8,128)(2,1)} %param.6), channel_id=1, source_target_pairs={{0,4},{2,6},{4,8},{6,10},{8,12},{10,14},{12,16},{14,18},{16,20},{1... | collective-permute-start | bytes 786440 | tf_op jit(solution)/shard_map/ppermute | solution.py:14
  4.5 31.4 %collective-permute-start = (bf16[128,1024]{1,0:T(8,128)(2,1)}, bf16[128,1024]{1,0:T(8,128)(2,1)S(1)}, u32[]{:S(2)}, u32[]{:S(2)}) collective-permute-start(bf16[128,1024]{1,0:T(8,128)(2,1)} %param.6), channel_id=1, source_target_pairs={{0,2},{2,0},{4,6},{6,4},{8,10},{10,8},{12,14},{14,12},{16,18},{18,... | collective-permute-start | bytes 786440 | tf_op jit(solution)/shard_map/ppermute | solution.py:19
  5.5 16.7 %collective-permute-start.2 = (bf16[128,1024]{1,0:T(8,128)(2,1)}, bf16[128,1024]{1,0:T(8,128)(2,1)S(1)}, u32[]{:S(2)}, u32[]{:S(2)}) collective-permute-start(bf16[128,1024]{1,0:T(8,128)(2,1)} %param.6), channel_id=1, source_target_pairs={{0,252},{2,254},{4,0},{6,2},{8,4},{10,6},{12,8},{14,10},{16,12},{1... | collective-permute-start | bytes 786440 | tf_op jit(solution)/shard_map/ppermute | solution.py:14
  20.0 20.5 %collective-permute-start.5 = (bf16[128,1024]{1,0:T(8,128)(2,1)S(1)}, bf16[128,1024]{1,0:T(8,128)(2,1)S(1)}, u32[]{:S(2)}, u32[]{:S(2)}) collective-permute-start(bf16[128,1024]{1,0:T(8,128)(2,1)S(1)} %collective-permute-done.1), channel_id=1, source_target_pairs={{0,4},{2,6},{4,8},{6,10},{8,12},{10,14},{12,16},{14,18},{16,20},{1... | collective-permute-start | bytes 786440 | tf_op jit(solution)/shard_map/ppermute | solution.py:14
  20.1 18.8 %collective-permute-start.3 = (bf16[128,1024]{1,0:T(8,128)(2,1)S(1)}, bf16[128,1024]{1,0:T(8,128)(2,1)S(1)}, u32[]{:S(2)}, u32[]{:S(2)}) collective-permute-start(bf16[128,1024]{1,0:T(8,128)(2,1)S(1)} %collective-permute-done.1), channel_id=1, source_target_pairs={{0,2},{2,0},{4,6},{6,4},{8,10},{10,8},{12,14},{14,12},{16,18},{18,... | collective-permute-start | bytes 786440 | tf_op jit(solution)/shard_map/ppermute | solution.py:19
  22.2 19.0 %collective-permute-start.6 = (bf16[128,1024]{1,0:T(8,128)(2,1)S(1)}, bf16[128,1024]{1,0:T(8,128)(2,1)S(1)}, u32[]{:S(2)}, u32[]{:S(2)}) collective-permute-start(bf16[128,1024]{1,0:T(8,128)(2,1)S(1)} %collective-permute-done.2), channel_id=1, source_target_pairs={{0,252},{2,254},{4,0},{6,2},{8,4},{10,6},{12,8},{14,10},{16,12},{1... | collective-permute-start | bytes 786440 | tf_op jit(solution)/shard_map/ppermute | solution.py:14
  30.1 9.6 %collective-permute-start.4 = (bf16[128,1024]{1,0:T(8,128)(2,1)S(1)}, bf16[128,1024]{1,0:T(8,128)(2,1)S(1)}, u32[]{:S(2)}, u32[]{:S(2)}) collective-permute-start(bf16[128,1024]{1,0:T(8,128)(2,1)S(1)} %collective-permute-done.2), channel_id=1, source_target_pairs={{0,2},{2,0},{4,6},{6,4},{8,10},{10,8},{12,14},{14,12},{16,18},{18,... | collective-permute-start | bytes 786440 | tf_op jit(solution)/shard_map/ppermute | solution.py:19
  41.9 6.0 %collective-permute-start.7 = (bf16[128,1024]{1,0:T(8,128)(2,1)S(1)}, bf16[128,1024]{1,0:T(8,128)(2,1)S(1)}, u32[]{:S(2)}, u32[]{:S(2)}) collective-permute-start(bf16[128,1024]{1,0:T(8,128)(2,1)S(1)} %get-tuple-element.97), channel_id=1, source_target_pairs={{0,2},{2,0},{4,6},{6,4},{8,10},{10,8},{12,14},{14,12},{16,18},{18,... | collective-permute-start | bytes 786440 | tf_op jit(solution)/shard_map/ppermute | solution.py:19
  49.1 2.2 %copy-start.1 = (f32[1024]{0:T(1024)S(1)}, f32[1024]{0:T(1024)}, u32[]{:S(2)}) copy-start(f32[1024]{0:T(1024)} %param.9) | copy-start | bytes 12292
  53.0 1.4 %copy-start.2 = (bf16[1024,1152]{0,1:T(8,128)(2,1)}, bf16[1024,1152]{0,1:T(8,128)(2,1)S(1)}, u32[]{:S(2)}) copy-start(bf16[1024,1152]{0,1:T(8,128)(2,1)S(1)} %get-tuple-element.42) | copy-start | bytes 7077892
  55.5 3.4 %collective-permute-start.10 = (f32[128,1024]{1,0:T(8,128)S(1)}, f32[128,1024]{1,0:T(8,128)S(1)}, u32[]{:S(2)}, u32[]{:S(2)}) collective-permute-start(f32[128,1024]{1,0:T(8,128)S(1)} %slice.40), channel_id=1, source_target_pairs={{0,2},{2,0},{4,6},{6,4},{8,10},{10,8},{12,14},{14,12},{16,18},{18,... | collective-permute-start | bytes 1572872 | tf_op jit(solution)/shard_map/ppermute | solution.py:19
  58.4 10.3 %collective-permute-start.13 = (f32[128,1024]{1,0:T(8,128)S(1)}, f32[128,1024]{1,0:T(8,128)S(1)}, u32[]{:S(2)}, u32[]{:S(2)}) collective-permute-start(f32[128,1024]{1,0:T(8,128)S(1)} %get-tuple-element.78), channel_id=1, source_target_pairs={{0,2},{2,0},{4,6},{6,4},{8,10},{10,8},{12,14},{14,12},{16,18},{18,... | collective-permute-start | bytes 1572872 | tf_op jit(solution)/shard_map/ppermute | solution.py:19
  58.9 9.8 %collective-permute-start.9 = (f32[128,1024]{1,0:T(8,128)S(1)}, f32[128,1024]{1,0:T(8,128)S(1)}, u32[]{:S(2)}, u32[]{:S(2)}) collective-permute-start(f32[128,1024]{1,0:T(8,128)S(1)} %get-tuple-element.79), channel_id=1, source_target_pairs={{0,2},{2,0},{4,6},{6,4},{8,10},{10,8},{12,14},{14,12},{16,18},{18,... | collective-permute-start | bytes 1572872 | tf_op jit(solution)/shard_map/ppermute | solution.py:19
  59.0 32.1 %collective-permute-start.11 = (f32[128,1024]{1,0:T(8,128)S(1)}, f32[128,1024]{1,0:T(8,128)S(1)}, u32[]{:S(2)}, u32[]{:S(2)}) collective-permute-start(f32[128,1024]{1,0:T(8,128)S(1)} %get-tuple-element.82), channel_id=1, source_target_pairs={{0,4},{2,6},{4,8},{6,10},{8,12},{10,14},{12,16},{14,18},{16,20},{1... | collective-permute-start | bytes 1572872 | tf_op jit(solution)/shard_map/ppermute | solution.py:14
  59.1 32.0 %collective-permute-start.14 = (f32[128,1024]{1,0:T(8,128)S(1)}, f32[128,1024]{1,0:T(8,128)S(1)}, u32[]{:S(2)}, u32[]{:S(2)}) collective-permute-start(f32[128,1024]{1,0:T(8,128)S(1)} %get-tuple-element.83), channel_id=1, source_target_pairs={{0,252},{2,254},{4,0},{6,2},{8,4},{10,6},{12,8},{14,10},{16,12},{1... | collective-permute-start | bytes 1572872 | tf_op jit(solution)/shard_map/ppermute | solution.py:14
  67.9 33.1 %collective-permute-start.8 = (f32[128,1024]{1,0:T(8,128)}, f32[128,1024]{1,0:T(8,128)S(1)}, u32[]{:S(2)}, u32[]{:S(2)}) collective-permute-start(f32[128,1024]{1,0:T(8,128)} %get-tuple-element.76), channel_id=1, source_target_pairs={{0,2},{2,0},{4,6},{6,4},{8,10},{10,8},{12,14},{14,12},{16,18},{18,... | collective-permute-start | bytes 1572872 | tf_op jit(solution)/shard_map/ppermute | solution.py:19
  92.4 30.0 %collective-permute-start.12 = (f32[128,1024]{1,0:T(8,128)}, f32[128,1024]{1,0:T(8,128)}, u32[]{:S(2)}, u32[]{:S(2)}) collective-permute-start(f32[128,1024]{1,0:T(8,128)} %get-tuple-element.80), channel_id=1, source_target_pairs={{0,4},{2,6},{4,8},{6,10},{8,12},{10,14},{12,16},{14,18},{16,20},{1... | collective-permute-start | bytes 1572872 | tf_op jit(solution)/shard_map/ppermute | solution.py:14
  92.4 30.0 %collective-permute-start.15 = (f32[128,1024]{1,0:T(8,128)}, f32[128,1024]{1,0:T(8,128)}, u32[]{:S(2)}, u32[]{:S(2)}) collective-permute-start(f32[128,1024]{1,0:T(8,128)} %get-tuple-element.81), channel_id=1, source_target_pairs={{0,252},{2,254},{4,0},{6,2},{8,4},{10,6},{12,8},{14,10},{16,12},{1... | collective-permute-start | bytes 1572872 | tf_op jit(solution)/shard_map/ppermute | solution.py:14
  123.5 7.5 %collective-permute-start.16 = (f32[64,1024]{1,0:T(8,128)S(1)}, f32[64,1024]{1,0:T(8,128)S(1)}, u32[]{:S(2)}, u32[]{:S(2)}) collective-permute-start(f32[64,1024]{1,0:T(8,128)S(1)} %dynamic-slice_add_fusion), channel_id=1, source_target_pairs={{0,1},{1,0},{2,3},{3,2},{4,5},{5,4},{6,7},{7,6},{8,9},{9,8},{10,11... | collective-permute-start | bytes 786440 | tf_op jit(solution)/shard_map/ppermute | solution.py:125

commit v10 on v8

--- a/solution.py
+++ b/solution.py
@@ -85,9 +85,6 @@
         coefficients.append(
             (row_weight[:, None] * (softmax_p - at_positive.astype(jnp.float32))).astype(jnp.bfloat16)
         )
-    coefficient = jnp.concatenate(coefficients, axis=1)
-    window = jnp.concatenate([key_tile for _, key_tile, _, _ in stored], axis=0)
-    grad_query = logit_scale * jnp.dot(coefficient, window, preferred_element_type=jnp.float32)
     order = {name: i for i, (name, _, _, _) in enumerate(stored)}
 
     def parts_of(names):
@@ -95,10 +92,17 @@
         out = lax.dot_general(
             cols, queries, (((0,), (0,)), ((), ())), preferred_element_type=jnp.float32
         )
-        return {n: out[i * tile_rows : (i + 1) * tile_rows] for i, n in enumerate(names)}
+        rows = jnp.concatenate([stored[order[n]][1] for n in names], axis=0)
+        return {n: out[i * tile_rows : (i + 1) * tile_rows] for i, n in enumerate(names)}, cols, rows
 
-    key_parts = parts_of(("sw_far", "up4", "down4"))
-    key_parts.update(parts_of(("own", "sw_own", "down2", "up2", "sw_down2", "sw_up2")))
+    key_parts, far_cols, far_rows = parts_of(("sw_far", "up4", "down4"))
+    near_parts, near_cols, near_rows = parts_of(("own", "sw_own", "down2", "up2", "sw_down2", "sw_up2"))
+    key_parts.update(near_parts)
+    grad_query = logit_scale * jnp.dot(
+        jnp.concatenate([far_cols, near_cols], axis=1),
+        jnp.concatenate([far_rows, near_rows], axis=0),
+        preferred_element_type=jnp.float32,
+    )
     back_own = swapped(key_parts["sw_own"], "dp")
     back_down2 = swapped(key_parts["sw_down2"], "dp")
     back_up2 = swapped(key_parts["sw_up2"], "dp")

time: 132 us -> 133 us (level)
  local copies, waits for them, and re-layouts: 10.3 us -> 4.85 us
  starting transfers between devices: 46.5 us -> 51.2 us
  waiting for transfers between devices: 46.1 us -> 48.7 us
  matrix products: 17.5 us -> 15.8 us
    unnamed x17 -> x38, local copies, waits for them, and re-layouts: 7.48 us -> 2.62 us
    ppermute x8, starting transfers between devices: 10.6 us -> 15.2 us  [swapped(): return lax.ppermute(x, axis, [(i, i ^ 1) for i in range(count)])]
    ppermute x1, waiting for transfers between devices: 1.21 us -> 2.88 us  [step(): lax.ppermute(other, 'rep', [(0, 1), (1, 0)])]
    dot_general x1, matrix products: 6.14 us -> 4.46 us  [step(): jnp.dot(jnp.concatenate([far_cols, near_cols], axis=1), jnp.concatenate([...]
  transfers between devices with their start and end apart: 17 -> 17, of which waited for: 5 -> 5; matrix products, arithmetic and copies ran while one was open for 21% -> 18% of each run, Pallas kernels for 0% -> 0%
where the time goes in v10:
time: 133 us
  starting transfers between devices  51.2 us (38%)
  waiting for transfers between devices  48.7 us (37%)
  matrix products  15.8 us (12%)
  other arithmetic  11.5 us (9%)
  local copies, waits for them, and re-layouts  4.85 us (4%)
    ppermute x8, waiting for transfers between devices, passed_along(): return lax.ppermute(x, axis, [(i, (i + by) % count) for i in range(count)])  45.8 us
    ppermute x8, starting transfers between devices, passed_along(): return lax.ppermute(x, axis, [(i, (i + by) % count) for i in range(count)])  35.9 us
    ppermute x8, starting transfers between devices, swapped(): return lax.ppermute(x, axis, [(i, i ^ 1) for i in range(count)])  15.2 us
    dot_general x9, matrix products, step(): lax.dot_general(queries, key_tile, (((1,), (1,)), ((), ())), preferred_el...  8.52 us
    dot_general x1, matrix products, step(): jnp.dot(jnp.concatenate([far_cols, near_cols], axis=1), jnp.concatenate([...  4.46 us
    ppermute x1, waiting for transfers between devices, step(): lax.ppermute(other, 'rep', [(0, 1), (1, 0)])  2.88 us
    dot_general x2, matrix products, parts_of(): lax.dot_general(cols, queries, (((0,), (0,)), ((), ())), preferred_elemen...  2.79 us
  transfers between devices with their start and end apart: 17, of which 5 were waited for; matrix products, arithmetic and copies ran while one was open for 18% of the time, Pallas kernels for 0%

profile of v10, /device:TPU:1, one launch (start us, length us, event | category | flops | bytes accessed | tf_op | source)
XLA Modules:
  0.0 133.2 jit_solution(7566646095370935954)
XLA Ops:
  0.6 3.9 %collective-permute-start.1 = (bf16[128,1024]{1,0:T(8,128)(2,1)}, bf16[128,1024]{1,0:T(8,128)(2,1)S(1)}, u32[]{:S(2)}, u32[]{:S(2)}) collective-permute-start(bf16[128,1024]{1,0:T(8,128)(2,1)} %param.6), channel_id=1, source_target_pairs={{0,4},{2,6},{4,8},{6,10},{8,12},{10,14},{12,16},{14,18},{16,20},{1... | collective-permute-start | bytes 786440 | tf_op jit(solution)/shard_map/ppermute | solution.py:14
  4.5 1.0 collective-permute-start
  5.5 7.5 %collective-permute-start.2 = (bf16[128,1024]{1,0:T(8,128)(2,1)}, bf16[128,1024]{1,0:T(8,128)(2,1)S(1)}, u32[]{:S(2)}, u32[]{:S(2)}) collective-permute-start(bf16[128,1024]{1,0:T(8,128)(2,1)} %param.6), channel_id=1, source_target_pairs={{0,252},{2,254},{4,0},{6,2},{8,4},{10,6},{12,8},{14,10},{16,12},{1... | collective-permute-start | bytes 786440 | tf_op jit(solution)/shard_map/ppermute | solution.py:14
  13.1 1.4 %fusion.19 = (pred[8]{0:T(512)(128)(4,1)S(1)}, pred[8]{0:T(512)(128)(4,1)S(1)}, pred[8]{0:T(512)(128)(4,1)S(1)}, pred[8]{0:T(512)(128)(4,1)S(1)}, pred[8]{0:T(51...) fusion(s32[8,128]{1,0:T(8,128)} %param.7, ...), kind=kLoop, calls=%fused_computation.118 | loop fusion | flops 72 | bytes 396 | tf_op jit(solution)/shard_map/eq | solution.py:62
  14.4 0.7 fusion.31
  15.1 0.1 broadcast_bitcast_fusion.11
  15.2 0.1 broadcast_bitcast_fusion.12
  15.3 0.1 broadcast_bitcast_fusion.13
  15.4 0.1 broadcast_bitcast_fusion.14
  15.5 0.1 broadcast_bitcast_fusion.5
  15.6 0.1 broadcast_bitcast_fusion.2
  15.7 0.1 broadcast_bitcast_fusion.3
  15.7 0.1 broadcast_bitcast_fusion.6
  15.8 0.1 broadcast_bitcast_fusion.9
  15.9 0.1 broadcast_bitcast_fusion
  16.0 1.8 %select_reduce_fusion.26 = (f32[1024]{0:T(1024)S(1)}, f32[1024,128]{0,1:T(8,128)S(1)}) fusion(pred[1024]{0:T(1024)(128)(4,1)S(1)} %get-tuple-element.143, bf16[1024,1024]{1,0:T(8,128)(2,1)S(1)} %copy-done, bf16[128,1024]{1,0:T(8,128)(2,1)} %param.6), kind=kOutput, calls=%fused_computation.70 | convolution fusion | flops 268827648 | bytes 2888704 | tf_op jit(solution)/shard_map/dot_general | solution.py:69
  17.8 2.2 %collective-permute-done.1 = bf16[128,1024]{1,0:T(8,128)(2,1)S(1)} collective-permute-done((bf16[128,1024]{1,0:T(8,128)(2,1)}, bf16[128,1024]{1,0:T(8,128)(2,1)S(1)}, u32[]{:S(2)}, u32[]{:S(2)}) %collective-permute-start.1) | collective-permute-done | bytes 262176 | tf_op jit(solution)/shard_map/ppermute | solution.py:14
  20.0 0.2 collective-permute-start.5
  20.1 1.5 %collective-permute-start.3 = (bf16[128,1024]{1,0:T(8,128)(2,1)S(1)}, bf16[128,1024]{1,0:T(8,128)(2,1)S(1)}, u32[]{:S(2)}, u32[]{:S(2)}) collective-permute-start(bf16[128,1024]{1,0:T(8,128)(2,1)S(1)} %collective-permute-done.1), channel_id=1, source_target_pairs={{0,2},{2,0},{4,6},{6,4},{8,10},{10,8},{12,14},{14,12},{16,18},{18,... | collective-permute-start | bytes 786440 | tf_op jit(solution)/shard_map/ppermute | solution.py:19
  21.7 0.5 collective-permute-done.2
  22.2 7.9 %collective-permute-start.6 = (bf16[128,1024]{1,0:T(8,128)(2,1)S(1)}, bf16[128,1024]{1,0:T(8,128)(2,1)S(1)}, u32[]{:S(2)}, u32[]{:S(2)}) collective-permute-start(bf16[128,1024]{1,0:T(8,128)(2,1)S(1)} %collective-permute-done.2), channel_id=1, source_target_pairs={{0,252},{2,254},{4,0},{6,2},{8,4},{10,6},{12,8},{14,10},{16,12},{1... | collective-permute-start | bytes 786440 | tf_op jit(solution)/shard_map/ppermute | solution.py:14
  30.1 4.2 %collective-permute-start.4 = (bf16[128,1024]{1,0:T(8,128)(2,1)S(1)}, bf16[128,1024]{1,0:T(8,128)(2,1)S(1)}, u32[]{:S(2)}, u32[]{:S(2)}) collective-permute-start(bf16[128,1024]{1,0:T(8,128)(2,1)S(1)} %collective-permute-done.2), channel_id=1, source_target_pairs={{0,2},{2,0},{4,6},{6,4},{8,10},{10,8},{12,14},{14,12},{16,18},{18,... | collective-permute-start | bytes 786440 | tf_op jit(solution)/shard_map/ppermute | solution.py:19
  34.2 0.8 select_reduce_fusion.23
  35.1 0.8 select_reduce_fusion.24
  36.0 0.8 select_reduce_fusion.25
  36.9 7.1 %collective-permute-start.7 = (bf16[128,1024]{1,0:T(8,128)(2,1)S(1)}, bf16[128,1024]{1,0:T(8,128)(2,1)S(1)}, u32[]{:S(2)}, u32[]{:S(2)}) collective-permute-start(bf16[128,1024]{1,0:T(8,128)(2,1)S(1)} %broadcast_select_fusion), channel_id=1, source_target_pairs={{0,2},{2,0},{4,6},{6,4},{8,10},{10,8},{12,14},{14,12},{16,18},{18,... | collective-permute-start | bytes 786440 | tf_op jit(solution)/shard_map/ppermute | solution.py:19
  44.0 0.8 select_reduce_fusion.19
  44.9 0.8 select_reduce_fusion.20
  45.8 0.8 select_reduce_fusion.21
  46.6 0.8 select_reduce_fusion.22
  47.5 0.8 select_reduce_fusion.18
  48.4 0.2 select_reduce_fusion.6
  48.7 0.8 select_reduce_fusion.8
  49.5 0.8 select_reduce_fusion.7
  50.3 0.6 add_subtract_fusion
  50.9 0.2 constant_dynamic-update-slice_fusion.8
  51.1 0.2 constant_dynamic-update-slice_fusion.7
  51.3 0.2 constant_dynamic-update-slice_fusion.6
  51.5 0.2 constant_dynamic-update-slice_fusion.23
  51.7 1.0 fusion.1
  52.7 0.1 collective-permute-start.10
  52.8 0.2 constant_dynamic-update-slice_fusion.22
  53.0 0.2 constant_dynamic-update-slice_fusion.21
  53.2 0.2 constant_dynamic-update-slice_fusion.20
  53.4 0.2 constant_dynamic-update-slice_fusion.19
  53.6 0.2 constant_dynamic-update-slice_fusion.18
  53.8 1.4 %copy-done.13 = bf16[1024,1152]{0,1:T(8,128)(2,1)} copy-done((bf16[1024,1152]{0,1:T(8,128)(2,1)}, bf16[1024,1152]{0,1:T(8,128)(2,1)S(1)}, u32[]{:S(2)}) %copy-start.13) | copy-done | bytes 2359320
  55.2 1.8 %fusion.34 = f32[768,1024]{1,0:T(8,128)S(1)} fusion(bf16[1024,768]{0,1:T(8,128)(2,1)S(1)} %get-tuple-element.83, bf16[1024,1024]{1,0:T(8,128)(2,1)S(1)} %copy-done), kind=kOutput, calls=%fused_computation.160 | convolution fusion | flops 1610612736 | bytes 6815744 | tf_op jit(solution)/shard_map/dot_general | solution.py:92
  57.0 1.3 fusion.33
  58.3 0.5 collective-permute-start.13
  58.8 1.1 slice_add_fusion.2
  59.9 8.5 %collective-permute-start.14 = (f32[128,1024]{1,0:T(8,128)}, f32[128,1024]{1,0:T(8,128)}, u32[]{:S(2)}, u32[]{:S(2)}) collective-permute-start(f32[128,1024]{1,0:T(8,128)} %get-tuple-element.82), channel_id=1, source_target_pairs={{0,252},{2,254},{4,0},{6,2},{8,4},{10,6},{12,8},{14,10},{16,12},{1... | collective-permute-start | bytes 1572872 | tf_op jit(solution)/shard_map/ppermute | solution.py:14
  68.4 0.8 collective-permute-start.8
  69.3 1.0 constant_dynamic-update-slice_fusion.14
  70.4 21.8 %collective-permute-done.11 = f32[128,1024]{1,0:T(8,128)} collective-permute-done((f32[128,1024]{1,0:T(8,128)}, f32[128,1024]{1,0:T(8,128)}, u32[]{:S(2)}, u32[]{:S(2)}) %collective-permute-start.11) | collective-permute-done | bytes 524320 | tf_op jit(solution)/shard_map/ppermute | solution.py:14
  92.2 2.1 %fusion.8 = (f32[128,1024]{1,0:T(8,128)S(1)}, f32[128,1024]{1,0:T(8,128)S(1)}) fusion(f32[128,1024]{1,0:T(8,128)} %collective-permute-done.11, f32[128,1024]{1,0:T(8,128)} %collective-permute-done.9, f32[768,1024]{1,0:T(8,128)} %copy-done.1, f32[128,1024]{1,0:T(8,128)} %collective-permute-done.14, f32[128,1024]{1,0:T(8,128)} %collective-permute-done.13), kind=kLoop, calls=%fused_computation.22 | loop fusion | flops 524288 | bytes 4194304 | tf_op jit(solution)/shard_map/add | solution.py:115
  94.3 0.1 collective-permute-start.12
  94.4 7.9 %collective-permute-start.15 = (f32[128,1024]{1,0:T(8,128)S(1)}, f32[128,1024]{1,0:T(8,128)S(1)}, u32[]{:S(2)}, u32[]{:S(2)}) collective-permute-start(f32[128,1024]{1,0:T(8,128)S(1)} %get-tuple-element.80), channel_id=1, source_target_pairs={{0,252},{2,254},{4,0},{6,2},{8,4},{10,6},{12,8},{14,10},{16,12},{1... | collective-permute-start | bytes 1572872 | tf_op jit(solution)/shard_map/ppermute | solution.py:14
  102.5 21.2 %collective-permute-done.12 = f32[128,1024]{1,0:T(8,128)S(1)} collective-permute-done((f32[128,1024]{1,0:T(8,128)S(1)}, f32[128,1024]{1,0:T(8,128)S(1)}, u32[]{:S(2)}, u32[]{:S(2)}) %collective-permute-start.12) | collective-permute-done | bytes 524320 | tf_op jit(solution)/shard_map/ppermute | solution.py:14
  123.7 1.2 fusion.10
  125.0 0.1 collective-permute-start.16
  125.1 4.5 %convolution_multiply_fusion = f32[1024,1024]{1,0:T(8,128)} fusion(bf16[1024,1152]{0,1:T(8,128)(2,1)S(1)} %copy-done.14, bf16[1152,1024]{1,0:T(8,128)(2,1)S(1)} %constant_dynamic-update-slice_fusion.9), kind=kOutput, calls=%fused_computation | convolution fusion | flops 2416967680 | bytes 8912896 | tf_op jit(solution)/shard_map/dot_general | solution.py:101
  129.6 2.9 %collective-permute-done.16 = f32[64,1024]{1,0:T(8,128)S(1)} collective-permute-done((f32[64,1024]{1,0:T(8,128)S(1)}, f32[64,1024]{1,0:T(8,128)S(1)}, u32[]{:S(2)}, u32[]{:S(2)}) %collective-permute-start.16) | collective-permute-done | bytes 262176 | tf_op jit(solution)/shard_map/ppermute | solution.py:127
  132.5 0.7 add_multiply_fusion
  (58 shorter events, 0.5 us)
Async XLA Ops:
  0.6 15.3 %copy-start = (bf16[1024,1024]{1,0:T(8,128)(2,1)S(1)}, bf16[1024,1024]{1,0:T(8,128)(2,1)}, u32[]{:S(2)}) copy-start(bf16[1024,1024]{1,0:T(8,128)(2,1)} %param.5) | copy-start | bytes 6291460
  0.6 19.3 %collective-permute-start.1 = (bf16[128,1024]{1,0:T(8,128)(2,1)}, bf16[128,1024]{1,0:T(8,128)(2,1)S(1)}, u32[]{:S(2)}, u32[]{:S(2)}) collective-permute-start(bf16[128,1024]{1,0:T(8,128)(2,1)} %param.6), channel_id=1, source_target_pairs={{0,4},{2,6},{4,8},{6,10},{8,12},{10,14},{12,16},{14,18},{16,20},{1... | collective-permute-start | bytes 786440 | tf_op jit(solution)/shard_map/ppermute | solution.py:14
  4.5 31.4 %collective-permute-start = (bf16[128,1024]{1,0:T(8,128)(2,1)}, bf16[128,1024]{1,0:T(8,128)(2,1)S(1)}, u32[]{:S(2)}, u32[]{:S(2)}) collective-permute-start(bf16[128,1024]{1,0:T(8,128)(2,1)} %param.6), channel_id=1, source_target_pairs={{0,2},{2,0},{4,6},{6,4},{8,10},{10,8},{12,14},{14,12},{16,18},{18,... | collective-permute-start | bytes 786440 | tf_op jit(solution)/shard_map/ppermute | solution.py:19
  5.5 16.7 %collective-permute-start.2 = (bf16[128,1024]{1,0:T(8,128)(2,1)}, bf16[128,1024]{1,0:T(8,128)(2,1)S(1)}, u32[]{:S(2)}, u32[]{:S(2)}) collective-permute-start(bf16[128,1024]{1,0:T(8,128)(2,1)} %param.6), channel_id=1, source_target_pairs={{0,252},{2,254},{4,0},{6,2},{8,4},{10,6},{12,8},{14,10},{16,12},{1... | collective-permute-start | bytes 786440 | tf_op jit(solution)/shard_map/ppermute | solution.py:14
  20.0 16.0 %copy-start.3 = (bf16[128,1024]{1,0:T(8,128)(2,1)}, bf16[128,1024]{1,0:T(8,128)(2,1)S(1)}, u32[]{:S(2)}) copy-start(bf16[128,1024]{1,0:T(8,128)(2,1)S(1)} %collective-permute-done.1) | copy-start | bytes 786436
  20.0 16.8 %collective-permute-start.5 = (bf16[128,1024]{1,0:T(8,128)(2,1)S(1)}, bf16[128,1024]{1,0:T(8,128)(2,1)S(1)}, u32[]{:S(2)}, u32[]{:S(2)}) collective-permute-start(bf16[128,1024]{1,0:T(8,128)(2,1)S(1)} %collective-permute-done.1), channel_id=1, source_target_pairs={{0,4},{2,6},{4,8},{6,10},{8,12},{10,14},{12,16},{14,18},{16,20},{1... | collective-permute-start | bytes 786440 | tf_op jit(solution)/shard_map/ppermute | solution.py:14
  20.1 26.5 %collective-permute-start.3 = (bf16[128,1024]{1,0:T(8,128)(2,1)S(1)}, bf16[128,1024]{1,0:T(8,128)(2,1)S(1)}, u32[]{:S(2)}, u32[]{:S(2)}) collective-permute-start(bf16[128,1024]{1,0:T(8,128)(2,1)S(1)} %collective-permute-done.1), channel_id=1, source_target_pairs={{0,2},{2,0},{4,6},{6,4},{8,10},{10,8},{12,14},{14,12},{16,18},{18,... | collective-permute-start | bytes 786440 | tf_op jit(solution)/shard_map/ppermute | solution.py:19
  22.2 13.7 %copy-start.5 = (bf16[128,1024]{1,0:T(8,128)(2,1)}, bf16[128,1024]{1,0:T(8,128)(2,1)S(1)}, u32[]{:S(2)}) copy-start(bf16[128,1024]{1,0:T(8,128)(2,1)S(1)} %collective-permute-done.2) | copy-start | bytes 786436
  22.2 14.6 %collective-permute-start.6 = (bf16[128,1024]{1,0:T(8,128)(2,1)S(1)}, bf16[128,1024]{1,0:T(8,128)(2,1)S(1)}, u32[]{:S(2)}, u32[]{:S(2)}) collective-permute-start(bf16[128,1024]{1,0:T(8,128)(2,1)S(1)} %collective-permute-done.2), channel_id=1, source_target_pairs={{0,252},{2,254},{4,0},{6,2},{8,4},{10,6},{12,8},{14,10},{16,12},{1... | collective-permute-start | bytes 786440 | tf_op jit(solution)/shard_map/ppermute | solution.py:14
  30.1 15.6 %collective-permute-start.4 = (bf16[128,1024]{1,0:T(8,128)(2,1)S(1)}, bf16[128,1024]{1,0:T(8,128)(2,1)S(1)}, u32[]{:S(2)}, u32[]{:S(2)}) collective-permute-start(bf16[128,1024]{1,0:T(8,128)(2,1)S(1)} %collective-permute-done.2), channel_id=1, source_target_pairs={{0,2},{2,0},{4,6},{6,4},{8,10},{10,8},{12,14},{14,12},{16,18},{18,... | collective-permute-start | bytes 786440 | tf_op jit(solution)/shard_map/ppermute | solution.py:19
  36.0 0.9 copy-start.7
  36.9 10.6 %collective-permute-start.7 = (bf16[128,1024]{1,0:T(8,128)(2,1)S(1)}, bf16[128,1024]{1,0:T(8,128)(2,1)S(1)}, u32[]{:S(2)}, u32[]{:S(2)}) collective-permute-start(bf16[128,1024]{1,0:T(8,128)(2,1)S(1)} %broadcast_select_fusion), channel_id=1, source_target_pairs={{0,2},{2,0},{4,6},{6,4},{8,10},{10,8},{12,14},{14,12},{16,18},{18,... | collective-permute-start | bytes 786440 | tf_op jit(solution)/shard_map/ppermute | solution.py:19
  45.7 0.9 copy-start.11
  46.6 0.9 copy-start.9
  48.7 2.2 %copy-start.2 = (f32[1024]{0:T(1024)S(1)}, f32[1024]{0:T(1024)}, u32[]{:S(2)}) copy-start(f32[1024]{0:T(1024)} %param.9) | copy-start | bytes 12292
  52.7 6.1 %collective-permute-start.10 = (f32[128,1024]{1,0:T(8,128)S(1)}, f32[128,1024]{1,0:T(8,128)S(1)}, u32[]{:S(2)}, u32[]{:S(2)}) collective-permute-start(f32[128,1024]{1,0:T(8,128)S(1)} %slice.53), channel_id=1, source_target_pairs={{0,2},{2,0},{4,6},{6,4},{8,10},{10,8},{12,14},{14,12},{16,18},{18,... | collective-permute-start | bytes 1572872 | tf_op jit(solution)/shard_map/ppermute | solution.py:19
  53.8 1.4 %copy-start.13 = (bf16[1024,1152]{0,1:T(8,128)(2,1)}, bf16[1024,1152]{0,1:T(8,128)(2,1)S(1)}, u32[]{:S(2)}) copy-start(bf16[1024,1152]{0,1:T(8,128)(2,1)S(1)} %get-tuple-element.84) | copy-start | bytes 7077892
  57.0 3.0 %copy-start.1 = (f32[768,1024]{1,0:T(8,128)}, f32[768,1024]{1,0:T(8,128)S(1)}, u32[]{:S(2)}) copy-start(f32[768,1024]{1,0:T(8,128)S(1)} %fusion.34) | copy-start | bytes 9437188
  58.3 12.1 %collective-permute-start.13 = (f32[128,1024]{1,0:T(8,128)}, f32[128,1024]{1,0:T(8,128)}, u32[]{:S(2)}, u32[]{:S(2)}) collective-permute-start(f32[128,1024]{1,0:T(8,128)} %get-tuple-element.77), channel_id=1, source_target_pairs={{0,2},{2,0},{4,6},{6,4},{8,10},{10,8},{12,14},{14,12},{16,18},{18,... | collective-permute-start | bytes 1572872 | tf_op jit(solution)/shard_map/ppermute | solution.py:19
  58.8 11.6 %collective-permute-start.9 = (f32[128,1024]{1,0:T(8,128)}, f32[128,1024]{1,0:T(8,128)}, u32[]{:S(2)}, u32[]{:S(2)}) collective-permute-start(f32[128,1024]{1,0:T(8,128)} %get-tuple-element.78), channel_id=1, source_target_pairs={{0,2},{2,0},{4,6},{6,4},{8,10},{10,8},{12,14},{14,12},{16,18},{18,... | collective-permute-start | bytes 1572872 | tf_op jit(solution)/shard_map/ppermute | solution.py:19
  59.9 32.3 %collective-permute-start.11 = (f32[128,1024]{1,0:T(8,128)}, f32[128,1024]{1,0:T(8,128)}, u32[]{:S(2)}, u32[]{:S(2)}) collective-permute-start(f32[128,1024]{1,0:T(8,128)} %get-tuple-element.81), channel_id=1, source_target_pairs={{0,4},{2,6},{4,8},{6,10},{8,12},{10,14},{12,16},{14,18},{16,20},{1... | collective-permute-start | bytes 1572872 | tf_op jit(solution)/shard_map/ppermute | solution.py:14
  59.9 32.3 %collective-permute-start.14 = (f32[128,1024]{1,0:T(8,128)}, f32[128,1024]{1,0:T(8,128)}, u32[]{:S(2)}, u32[]{:S(2)}) collective-permute-start(f32[128,1024]{1,0:T(8,128)} %get-tuple-element.82), channel_id=1, source_target_pairs={{0,252},{2,254},{4,0},{6,2},{8,4},{10,6},{12,8},{14,10},{16,12},{1... | collective-permute-start | bytes 1572872 | tf_op jit(solution)/shard_map/ppermute | solution.py:14
  68.4 34.0 %collective-permute-start.8 = (f32[128,1024]{1,0:T(8,128)S(1)}, f32[128,1024]{1,0:T(8,128)S(1)}, u32[]{:S(2)}, u32[]{:S(2)}) collective-permute-start(f32[128,1024]{1,0:T(8,128)S(1)} %get-tuple-element.76), channel_id=1, source_target_pairs={{0,2},{2,0},{4,6},{6,4},{8,10},{10,8},{12,14},{14,12},{16,18},{18,... | collective-permute-start | bytes 1572872 | tf_op jit(solution)/shard_map/ppermute | solution.py:19
  69.3 33.0 %copy-start.8 = (bf16[128,1024]{1,0:T(8,128)(2,1)S(1)}, bf16[128,1024]{1,0:T(8,128)(2,1)}, u32[]{:S(2)}) copy-start(bf16[128,1024]{1,0:T(8,128)(2,1)} %copy-done.7) | copy-start | bytes 786436
  70.3 32.0 %copy-start.4 = (bf16[128,1024]{1,0:T(8,128)(2,1)S(1)}, bf16[128,1024]{1,0:T(8,128)(2,1)}, u32[]{:S(2)}) copy-start(bf16[128,1024]{1,0:T(8,128)(2,1)} %copy-done.3) | copy-start | bytes 786436
  70.3 32.0 %copy-start.6 = (bf16[128,1024]{1,0:T(8,128)(2,1)S(1)}, bf16[128,1024]{1,0:T(8,128)(2,1)}, u32[]{:S(2)}) copy-start(bf16[128,1024]{1,0:T(8,128)(2,1)} %copy-done.5) | copy-start | bytes 786436
  70.4 32.0 %copy-start.10 = (bf16[128,1024]{1,0:T(8,128)(2,1)S(1)}, bf16[128,1024]{1,0:T(8,128)(2,1)}, u32[]{:S(2)}) copy-start(bf16[128,1024]{1,0:T(8,128)(2,1)} %copy-done.9) | copy-start | bytes 786436
  70.4 32.1 %copy-start.12 = (bf16[128,1024]{1,0:T(8,128)(2,1)S(1)}, bf16[128,1024]{1,0:T(8,128)(2,1)}, u32[]{:S(2)}) copy-start(bf16[128,1024]{1,0:T(8,128)(2,1)} %copy-done.11) | copy-start | bytes 786436
  94.3 29.4 %collective-permute-start.12 = (f32[128,1024]{1,0:T(8,128)S(1)}, f32[128,1024]{1,0:T(8,128)S(1)}, u32[]{:S(2)}, u32[]{:S(2)}) collective-permute-start(f32[128,1024]{1,0:T(8,128)S(1)} %get-tuple-element.79), channel_id=1, source_target_pairs={{0,4},{2,6},{4,8},{6,10},{8,12},{10,14},{12,16},{14,18},{16,20},{1... | collective-permute-start | bytes 1572872 | tf_op jit(solution)/shard_map/ppermute | solution.py:14
  94.4 29.3 %collective-permute-start.15 = (f32[128,1024]{1,0:T(8,128)S(1)}, f32[128,1024]{1,0:T(8,128)S(1)}, u32[]{:S(2)}, u32[]{:S(2)}) collective-permute-start(f32[128,1024]{1,0:T(8,128)S(1)} %get-tuple-element.80), channel_id=1, source_target_pairs={{0,252},{2,254},{4,0},{6,2},{8,4},{10,6},{12,8},{14,10},{16,12},{1... | collective-permute-start | bytes 1572872 | tf_op jit(solution)/shard_map/ppermute | solution.py:14
  102.4 22.7 %copy-start.14 = (bf16[1024,1152]{0,1:T(8,128)(2,1)S(1)}, bf16[1024,1152]{0,1:T(8,128)(2,1)}, u32[]{:S(2)}) copy-start(bf16[1024,1152]{0,1:T(8,128)(2,1)} %copy-done.13) | copy-start | bytes 7077892
  125.0 7.5 %collective-permute-start.16 = (f32[64,1024]{1,0:T(8,128)S(1)}, f32[64,1024]{1,0:T(8,128)S(1)}, u32[]{:S(2)}, u32[]{:S(2)}) collective-permute-start(f32[64,1024]{1,0:T(8,128)S(1)} %slice_select_fusion), channel_id=1, source_target_pairs={{0,1},{1,0},{2,3},{3,2},{4,5},{5,4},{6,7},{7,6},{8,9},{9,8},{10,11... | collective-permute-start | bytes 786440 | tf_op jit(solution)/shard_map/ppermute | solution.py:127
